TPU v7x, 512 devices: a whole 4x8x8 slice. The times are simulated.
512 devices in a mesh: seq: 128 (over z, y, core), tp: 4 (over x).
Axes of the slice: x: 4, y: 8, z: 8, core: 2. Of those that a mesh axis runs over, the one named last changes fastest.
Arguments:
- hidden_in: bfloat16 [16384, 1536], P('seq'), may hold values from -6 to 6
- w_query: bfloat16 [1536, 1536], P(None, 'tp'), may hold values from -0.625 to 0.625
- key_weight: bfloat16 [1536, 512], P(None, 'tp'), may hold values from -0.625 to 0.625
- value_weight: bfloat16 [1536, 512], P(None, 'tp'), may hold values from -0.15625 to 0.15625
- w_out: bfloat16 [1536, 1536], P('tp'), may hold values from -0.4375 to 0.4375
- cached_prefix_keys: bfloat16 [4096, 512], P('seq', 'tp'), may hold values from -60000 to 60000
- cached_prefix_values: bfloat16 [4096, 512], P('seq', 'tp'), may hold values from -6 to 6
- doc_ids: int32 [128, 128], P('seq'), may hold values from 0 to 3, never falling along the last dimension, each value on 1 to 64 neighbouring positions
- routes: int32 [16384, 8], P(('seq', 'tp')), may hold values from 0 to 31, all different within a row; in each aligned block of 32 rows (0 to 31, 32 to 63, ...) at most 16 rows name the same one
- gate_scores: float32 [16384, 8], P(('seq', 'tp')), may hold values from 0.2 to 1
- expert_in: bfloat16 [128, 1536, 256], P('seq'), may hold values from -0.15625 to 0.15625
- expert_out: bfloat16 [128, 128, 1536], P('seq'), may hold values from -0.25 to 0.25
Outputs:
- attn_proj: bfloat16 [16384, 1536], P(('seq', 'tp'))
- expert_mix: bfloat16 [16384, 1536], P(('seq', 'tp'))
- layer_out: bfloat16 [16384, 1536], P(('seq', 'tp'))
Inputs may be any that keep to these rules, and one draw needn't show every extreme that they name: `routes`: within the rows of one device (aligned blocks of 32 tokens) no expert is picked by more than 16 tokens, a bound that some block reaches; every expert is picked somewhere.
All inputs are finite; a program needn't handle non-finite values.
Results may differ from a plain program's by a relative error of at most 0.028.
Values may be sent and summed in bfloat16 or wider, within the bound.
No kernel may reach another device: no remote copies, remote signals or barrier semaphores. Data moves between devices by JAX's collectives and lax.ppermute only.
A program may use at most 64 MiB of HBM per device.

v0:
```python
import jax
import jax.numpy as jnp
from jax import lax
from jax.sharding import PartitionSpec as P

HEAD_WIDTH = 64
EXPERTS = 32


EPSILON = 1e-06
RESIDUAL = 0.22


def normalize(values):
    values = values.astype(jnp.float32)
    return values * lax.rsqrt(jnp.mean(values * values, axis=-1, keepdims=True) + EPSILON)


def rotary_apply(values, token_positions):
    half_size = values.shape[-1] // 2
    frequency = jnp.exp(
        -jnp.log(10000.0) * jnp.arange(half_size, dtype=jnp.float32) * 2.0 / values.shape[-1]
    )
    angles = token_positions[:, None] * frequency[None, :]
    cosine = jnp.cos(angles)[:, None, :]
    sine_part = jnp.sin(angles)[:, None, :]
    first_half = values[..., :half_size]
    second = values[..., half_size:]
    return jnp.concatenate(
        [first_half * cosine - second * sine_part, second * cosine + first_half * sine_part],
        axis=-1,
    )


def body(
    hidden_in,
    w_query,
    key_weight,
    value_weight,
    w_out,
    cached_prefix_keys,
    cached_prefix_values,
    doc_ids,
    routes,
    gate_scores,
    expert_in,
    expert_out,
):
    rows_dev = hidden_in.shape[0]
    column_list = hidden_in.shape[1]
    head_size = HEAD_WIDTH
    kv_local = key_weight.shape[1] // head_size
    group_width = w_query.shape[1] // head_size // kv_local
    seq_count = lax.axis_size("seq")
    prefix_len = cached_prefix_keys.shape[0] * seq_count
    doc_row = doc_ids[0]
    row_index = jnp.arange(rows_dev, dtype=jnp.int32)
    same_doc = doc_row[:, None] == doc_row[None, :]
    doc_start = jnp.min(jnp.where(same_doc, row_index[None, :], rows_dev), axis=1)
    token_positions = (prefix_len + row_index - doc_start).astype(jnp.float32)
    normed_input = normalize(hidden_in).astype(jnp.bfloat16)
    query_rows_all = jnp.dot(normed_input, w_query, preferred_element_type=jnp.float32).reshape(
        rows_dev, kv_local * group_width, head_size
    )
    query_rows_all = (
        rotary_apply(query_rows_all, token_positions)
        .astype(jnp.bfloat16)
        .reshape(rows_dev, kv_local, group_width, head_size)
    )
    fresh_key = jnp.dot(normed_input, key_weight, preferred_element_type=jnp.float32).reshape(
        rows_dev, kv_local, head_size
    )
    fresh_key = rotary_apply(fresh_key, token_positions).astype(jnp.bfloat16)
    fresh_value = (
        jnp.dot(normed_input, value_weight, preferred_element_type=jnp.float32)
        .astype(jnp.bfloat16)
        .reshape(rows_dev, kv_local, head_size)
    )
    own_scores = (
        jnp.einsum("tkgd,skd->tkgs", query_rows_all, fresh_key, preferred_element_type=jnp.float32)
        / head_size
    )
    visible = same_doc & (row_index[None, :] <= row_index[:, None])
    own_scores = jnp.where(visible[:, None, None, :], own_scores, -jnp.inf)
    row_top = jnp.max(own_scores, axis=-1)
    weights = jnp.exp(own_scores - row_top[..., None])
    denominator = jnp.sum(weights, axis=-1)
    numerator = jnp.einsum(
        "tkgs,skd->tkgd",
        weights.astype(jnp.bfloat16),
        fresh_value,
        preferred_element_type=jnp.float32,
    )
    running = (row_top, denominator, numerator)
    whole_keys, whole_values = (
        lax.all_gather(cached_prefix_keys, "seq", axis=0, tiled=True),
        lax.all_gather(cached_prefix_values, "seq", axis=0, tiled=True),
    )
    top_old, denom_old, numer_old = running
    key_rows = whole_keys.reshape(-1, kv_local, head_size)
    value_rows = whole_values.reshape(-1, kv_local, head_size)
    scores = (
        jnp.einsum("tkgd,pkd->tkgp", query_rows_all, key_rows, preferred_element_type=jnp.float32)
        / head_size
    )
    top_new = jnp.maximum(top_old, jnp.max(scores, axis=-1))
    shrink = jnp.exp(top_old - top_new)
    part_weights = jnp.exp(scores - top_new[..., None])
    denom_new = denom_old * shrink + jnp.sum(part_weights, axis=-1)
    numer_new = numer_old * shrink[..., None] + jnp.einsum(
        "tkgp,pkd->tkgd",
        part_weights.astype(jnp.bfloat16),
        value_rows,
        preferred_element_type=jnp.float32,
    )
    running = (top_new, denom_new, numer_new)
    attended = (
        (running[2] / running[1][..., None])
        .astype(jnp.bfloat16)
        .reshape(rows_dev, kv_local * group_width * head_size)
    )
    moe_rows = routes.shape[0]
    row_start = lax.axis_index("tp") * moe_rows
    summed_all = lax.psum(jnp.dot(attended, w_out, preferred_element_type=jnp.float32), "tp")
    attn_sum = lax.dynamic_slice_in_dim(summed_all, row_start, moe_rows, 0)
    residual = (
        lax.dynamic_slice_in_dim(hidden_in, row_start, moe_rows, 0).astype(jnp.float32)
        + RESIDUAL * attn_sum
    )
    routed = normalize(residual).astype(jnp.bfloat16)
    experts = EXPERTS
    units_dev = expert_in.shape[0]
    hparts = units_dev * seq_count // experts
    capacity = moe_rows // 2
    ff_part = expert_out.shape[1]
    onehot = (routes[:, :, None] == jnp.arange(experts, dtype=jnp.int32)[None, None, :]).astype(
        jnp.int32
    )
    per_row = jnp.sum(onehot, axis=1)
    before = jnp.cumsum(per_row, axis=0) - per_row
    rank_in = jnp.sum(onehot * before[:, None, :], axis=2)
    slot_of = routes * capacity + rank_in
    slot_ids = jnp.arange(experts * capacity, dtype=jnp.int32)
    pick_hit = slot_of[:, :, None] == slot_ids[None, None, :]
    selector = jnp.any(pick_hit, axis=1).T.astype(jnp.bfloat16)
    combiner = jnp.sum(jnp.where(pick_hit, gate_scores[:, :, None], 0.0), axis=1)
    gathered = jnp.dot(selector, routed, preferred_element_type=jnp.float32).astype(jnp.bfloat16)
    outgoing = jnp.broadcast_to(
        gathered.reshape(experts, 1, capacity, column_list),
        (experts, hparts, capacity, column_list),
    )
    outgoing = outgoing.reshape(seq_count, units_dev, capacity, column_list)
    gate_up = jnp.einsum(
        "sucd,udf->sucf",
        lax.all_to_all(outgoing, "seq", split_axis=0, concat_axis=0, tiled=True),
        expert_in,
        preferred_element_type=jnp.float32,
    )
    activated = (jax.nn.silu(gate_up[..., :ff_part]) * gate_up[..., ff_part:]).astype(jnp.bfloat16)
    partial_value = jnp.einsum(
        "sucf,ufd->sucd", activated, expert_out, preferred_element_type=jnp.float32
    ).astype(jnp.bfloat16)
    returned = lax.all_to_all(partial_value, "seq", split_axis=0, concat_axis=0, tiled=True)
    part_sum = jnp.sum(
        returned.reshape(experts, hparts, capacity, column_list).astype(jnp.float32), axis=1
    )
    part_sum = part_sum.reshape(experts * capacity, column_list)
    expert_sum = jnp.dot(
        combiner, part_sum, precision=lax.Precision.HIGHEST, preferred_element_type=jnp.float32
    )
    layer_out = (residual + RESIDUAL * expert_sum).astype(jnp.bfloat16)
    return (attn_sum.astype(jnp.bfloat16), expert_sum.astype(jnp.bfloat16), layer_out)


def solution(mesh):
    in_specs = (
        P("seq", None),
        P(None, "tp"),
        P(None, "tp"),
        P(None, "tp"),
        P("tp", None),
        P("seq", "tp"),
        P("seq", "tp"),
        P("seq", None),
        P(("seq", "tp"), None),
        P(("seq", "tp"), None),
        P("seq", None, None),
        P("seq", None, None),
    )
    out_specs = (P(("seq", "tp"), None), P(("seq", "tp"), None), P(("seq", "tp"), None))
    return jax.shard_map(body, mesh=mesh, in_specs=in_specs, out_specs=out_specs, check_vma=False)
```

profile of v0, /device:TPU:24, one launch (start us, length us, event | category | flops | bytes accessed | tf_op | source)
XLA Modules:
  0.0 620.0 jit_solution(3944682123108635875)
XLA Ops:
  7.2 0.7 all-gather.3.cloned.1.call-update
  8.0 0.7 all-gather.5.cloned.1.call-update
  8.7 1.2 fusion.21
  9.9 0.8 fusion.33
  10.7 2.0 fusion.43
  12.7 1.5 fusion.45
  14.4 0.8 compare_and_fusion
  15.2 0.3 fusion.48
  15.6 1.5 convolution_convert_fusion.1
  17.1 76.4 %all-gather.3.cloned.1.call-done = bf16[4096,128]{1,0:T(8,128)(2,1)} async-done(((bf16[32,128]{1,0:T(8,128)(2,1)}), bf16[4096,128]{1,0:T(8,128)(2,1)}) %all-gather.3.cloned.1.call-update) | async-done | bytes 1048592 | tf_op jit(solution)/shard_map/all_gather | solution.py:96
  93.5 1.5 copy.68
  95.0 1.9 bitcast_reduce_fusion
  96.9 4.6 copy-done.1
  101.5 2.2 fusion.1
  103.7 67.8 %all-gather.5.cloned.1.call-done = bf16[4096,128]{1,0:T(8,128)(2,1)} async-done(((bf16[32,128]{1,0:T(8,128)(2,1)}), bf16[4096,128]{1,0:T(8,128)(2,1)}) %all-gather.5.cloned.1.call-update) | async-done | bytes 1048592 | tf_op jit(solution)/shard_map/all_gather | solution.py:97
  171.5 1.5 copy.69
  173.0 5.9 fusion.16
  179.1 1.3 fusion.49
  180.7 0.7 select_reduce_fusion.1
  181.8 50.7 %all-reduce.2.cloned.1.call-done = f32[128,1536]{1,0:T(8,128)} async-done(((f32[128,1536]{1,0:T(8,128)}), f32[128,1536]{1,0:T(8,128)}) %all-reduce.2.cloned.1.call-update) | async-done | bytes 786448 | tf_op jit(solution)/shard_map/psum | solution.py:124
  232.5 1.1 multiply_reduce_fusion
  233.6 1.6 convolution_convert_fusion
  235.2 0.8 broadcast_in_dim.40
  236.0 158.2 %all_to_all.10 = bf16[128,1,16,1536]{3,2,1,0:T(8,128)(2,1)S(1)} all-to-all(bf16[128,1,16,1536]{3,2,1,0:T(8,128)(2,1)S(1)} %bitcast.102), channel_id=1, replica_groups=mesh['seq'=128,'tp'=4] {'seq'}, dimensions={0} | all-to-all | bytes 12582912 | tf_op jit(solution)/shard_map/all_to_all | solution.py:155
  394.2 7.3 %fusion.8 = f32[128,1,16,256]{3,0,2,1:T(8,128)S(1)} fusion(bf16[128,1,16,1536]{3,2,1,0:T(8,128)(2,1)S(1)} %all_to_all.10, bf16[1,1536,256]{2,1,0:T(8,128)(2,1)S(1)} %copy-done.6), kind=kOutput, calls=%fused_computation.12 | convolution fusion | flops 1610612736 | bytes 9175040 | tf_op jit(solution)/shard_map/sucd,udf->sucf/dot_general | solution.py:153
  401.5 1.8 convert_bitcast_fusion
  403.3 6.4 %copy.75 = bf16[128,1,16,1536]{3,2,1,0:T(8,128)(2,1)} copy(bf16[128,1,16,1536]{3,0,2,1:T(8,128)(2,1)S(1)} %convert_bitcast_fusion) | data formatting | bytes 12582912 | tf_op jit(solution)/shard_map/convert_element_type | solution.py:162
  409.7 19.3 %all-to-all-start.1 = ((bf16[128,1,16,1536]{3,2,1,0:T(8,128)(2,1)}), bf16[128,1,16,1536]{3,2,1,0:T(8,128)(2,1)}, u32[]{:S(2)}, u32[]{:S(2)}) async-start(bf16[128,1,16,1536]{3,2,1,0:T(8,128)(2,1)} %copy.75), calls=%async_computation.1 | async-start | bytes 12582912 | tf_op jit(solution)/shard_map/all_to_all | solution.py:163
  429.3 1.6 dynamic-slice_convert_fusion
  430.9 174.8 %all-to-all-done.1 = bf16[128,1,16,1536]{3,2,1,0:T(8,128)(2,1)} async-done(((bf16[128,1,16,1536]{3,2,1,0:T(8,128)(2,1)}), bf16[128,1,16,1536]{3,2,1,0:T(8,128)(2,1)}, u32[]{:S(2)}, u32[]{:S(2)}) %all-to-all-start.1) | async-done | bytes 6291488 | tf_op jit(solution)/shard_map/all_to_all | solution.py:163
  605.7 4.3 convert_reduce_fusion
  610.0 3.5 add_convert_fusion
  (38 shorter events, 1.6 us)
Async XLA Ops:
  7.2 172.0 %copy-start = (bf16[384,1536]{1,0:T(8,128)(2,1)S(1)}, bf16[384,1536]{1,0:T(8,128)(2,1)}, u32[]{:S(2)}) copy-start(bf16[384,1536]{1,0:T(8,128)(2,1)} %param.16) | copy-start | bytes 3538948
  7.2 86.3 %all-gather.3.cloned.1.call-start = ((), (), s32[]{:S(2)}) async-start(), calls=%async_computation.2 | async-start | bytes 1056768 | tf_op jit(solution)/shard_map/all_gather | solution.py:96
  7.9 163.6 %all-gather.5.cloned.1.call-start = ((), (), s32[]{:S(2)}) async-start(), calls=%async_computation.3 | async-start | bytes 1056768 | tf_op jit(solution)/shard_map/all_gather | solution.py:97
  8.7 223.9 %all-reduce.2.cloned.1.call-start = ((), (), s32[]{:S(2)}) async-start(), calls=%async_computation.4 | async-start | bytes 1572864 | tf_op jit(solution)/shard_map/psum | solution.py:124
  96.9 4.6 copy-start.1
  173.0 7.5 %copy-start.4 = (s32[32,8]{0,1:T(8,128)S(1)}, s32[32,8]{0,1:T(8,128)}, u32[]{:S(2)}) copy-start(s32[32,8]{0,1:T(8,128)} %param.20) | copy-start | bytes 3076
  173.0 59.6 %copy-start.2 = (bf16[128,1536]{1,0:T(8,128)(2,1)S(1)}, bf16[128,1536]{1,0:T(8,128)(2,1)}, u32[]{:S(2)}) copy-start(bf16[128,1536]{1,0:T(8,128)(2,1)} %param.12) | copy-start | bytes 1179652
  236.0 158.2 %copy-start.6 = (bf16[1,1536,256]{2,1,0:T(8,128)(2,1)S(1)}, bf16[1,1536,256]{2,1,0:T(8,128)(2,1)}, u32[]{:S(2)}) copy-start(bf16[1,1536,256]{2,1,0:T(8,128)(2,1)} %param.22) | copy-start | bytes 2359300
  394.2 7.3 %copy-start.3 = (bf16[1,128,1536]{2,1,0:T(8,128)(2,1)S(1)}, bf16[1,128,1536]{2,1,0:T(8,128)(2,1)}, u32[]{:S(2)}) copy-start(bf16[1,128,1536]{2,1,0:T(8,128)(2,1)} %param.23) | copy-start | bytes 1179652
  409.7 19.3 %copy-start.5 = (f32[32,8]{0,1:T(8,128)S(1)}, f32[32,8]{0,1:T(8,128)}, u32[]{:S(2)}) copy-start(f32[32,8]{0,1:T(8,128)} %param.21) | copy-start | bytes 3076
  409.7 196.0 %all-to-all-start.1 = ((bf16[128,1,16,1536]{3,2,1,0:T(8,128)(2,1)}), bf16[128,1,16,1536]{3,2,1,0:T(8,128)(2,1)}, u32[]{:S(2)}, u32[]{:S(2)}) async-start(bf16[128,1,16,1536]{3,2,1,0:T(8,128)(2,1)} %copy.75), calls=%async_computation.1 | async-start | bytes 12582912 | tf_op jit(solution)/shard_map/all_to_all | solution.py:163
Sparse Core Ops, SparseCore 0:
  11.0 82.4 all-gather.2
  96.5 74.8 all-gather.4
  180.6 51.9 all-reduce.1
where the time goes:
time: 621 us; the launch traced here: 620 us
  waiting for transfers between devices  371 us (60%)
  blocking collectives  158 us (25%)
  matrix products  28.7 us (5%)
  starting transfers between devices  19.4 us (3%)
  local copies, waits for them, and re-layouts  16.6 us (3%)
  between operations  14 us (2%)
  other arithmetic  11.9 us (2%)
    all_to_all x1, waiting for transfers between devices, body(): lax.all_to_all(partial_value, 'seq', split_axis=0, concat_axis=0, tiled=T...  175 us
    all_to_all x1, blocking collectives, body(): lax.all_to_all(outgoing, 'seq', split_axis=0, concat_axis=0, tiled=True)  158 us
    all_gather x1, waiting for transfers between devices, body(): lax.all_gather(cached_prefix_keys, 'seq', axis=0, tiled=True)  76.4 us
    all_gather x1, waiting for transfers between devices, body(): lax.all_gather(cached_prefix_values, 'seq', axis=0, tiled=True)  67.8 us
    psum x1, waiting for transfers between devices, body(): lax.psum(jnp.dot(attended, w_out, preferred_element_type=jnp.float32), 'tp')  50.7 us
    all_to_all x1, starting transfers between devices, body(): lax.all_to_all(partial_value, 'seq', split_axis=0, concat_axis=0, tiled=T...  19.3 us
  transfers between devices with their start and end apart: 4, of which 4 were waited for; matrix products, arithmetic and copies ran while one was open for 3% of the time, Pallas kernels for 0%

commit v1 on v0

--- a/solution.py
+++ b/solution.py
@@ -1,11 +1,15 @@
 import jax
 import jax.numpy as jnp
 from jax import lax
-from jax.sharding import PartitionSpec as P
+from jax.sharding import Mesh, PartitionSpec as P
 
 HEAD_WIDTH = 64
 EXPERTS = 32
 
+
+SEQ = ("z", "yh", "yl", "c")
+EXPERT_AXES = ("z", "yh")
+PART_AXES = ("yl", "c")
 
 EPSILON = 1e-06
 RESIDUAL = 0.22
@@ -51,7 +55,7 @@
     head_size = HEAD_WIDTH
     kv_local = key_weight.shape[1] // head_size
     group_width = w_query.shape[1] // head_size // kv_local
-    seq_count = lax.axis_size("seq")
+    seq_count = lax.axis_size(SEQ)
     prefix_len = cached_prefix_keys.shape[0] * seq_count
     doc_row = doc_ids[0]
     row_index = jnp.arange(rows_dev, dtype=jnp.int32)
@@ -92,10 +96,11 @@
         preferred_element_type=jnp.float32,
     )
     running = (row_top, denominator, numerator)
-    whole_keys, whole_values = (
-        lax.all_gather(cached_prefix_keys, "seq", axis=0, tiled=True),
-        lax.all_gather(cached_prefix_values, "seq", axis=0, tiled=True),
-    )
+    prefix_both = jnp.concatenate([cached_prefix_keys, cached_prefix_values], axis=1)
+    whole_both = lax.all_gather(prefix_both, SEQ, axis=0, tiled=True)
+    kv_cols = cached_prefix_keys.shape[1]
+    whole_keys = whole_both[:, :kv_cols]
+    whole_values = whole_both[:, kv_cols:]
     top_old, denom_old, numer_old = running
     key_rows = whole_keys.reshape(-1, kv_local, head_size)
     value_rows = whole_values.reshape(-1, kv_local, head_size)
@@ -121,16 +126,15 @@
     )
     moe_rows = routes.shape[0]
     row_start = lax.axis_index("tp") * moe_rows
-    summed_all = lax.psum(jnp.dot(attended, w_out, preferred_element_type=jnp.float32), "tp")
-    attn_sum = lax.dynamic_slice_in_dim(summed_all, row_start, moe_rows, 0)
+    attn_sum = lax.psum_scatter(
+        jnp.dot(attended, w_out, preferred_element_type=jnp.float32), "tp", scatter_dimension=0, tiled=True
+    )
     residual = (
         lax.dynamic_slice_in_dim(hidden_in, row_start, moe_rows, 0).astype(jnp.float32)
         + RESIDUAL * attn_sum
     )
     routed = normalize(residual).astype(jnp.bfloat16)
     experts = EXPERTS
-    units_dev = expert_in.shape[0]
-    hparts = units_dev * seq_count // experts
     capacity = moe_rows // 2
     ff_part = expert_out.shape[1]
     onehot = (routes[:, :, None] == jnp.arange(experts, dtype=jnp.int32)[None, None, :]).astype(
@@ -145,26 +149,21 @@
     selector = jnp.any(pick_hit, axis=1).T.astype(jnp.bfloat16)
     combiner = jnp.sum(jnp.where(pick_hit, gate_scores[:, :, None], 0.0), axis=1)
     gathered = jnp.dot(selector, routed, preferred_element_type=jnp.float32).astype(jnp.bfloat16)
-    outgoing = jnp.broadcast_to(
-        gathered.reshape(experts, 1, capacity, column_list),
-        (experts, hparts, capacity, column_list),
-    )
-    outgoing = outgoing.reshape(seq_count, units_dev, capacity, column_list)
-    gate_up = jnp.einsum(
-        "sucd,udf->sucf",
-        lax.all_to_all(outgoing, "seq", split_axis=0, concat_axis=0, tiled=True),
-        expert_in,
-        preferred_element_type=jnp.float32,
-    )
+    outgoing = gathered.reshape(experts, capacity, column_list)
+    incoming = lax.all_to_all(outgoing, EXPERT_AXES, split_axis=0, concat_axis=0, tiled=True)
+    incoming = incoming.reshape(experts * capacity, column_list)
+    full_in = lax.all_gather(expert_in, PART_AXES, axis=0, tiled=True)
+    full_out = lax.all_gather(expert_out, PART_AXES, axis=0, tiled=True)
+    gate_up = jnp.einsum("rd,pdf->prf", incoming, full_in, preferred_element_type=jnp.float32)
     activated = (jax.nn.silu(gate_up[..., :ff_part]) * gate_up[..., ff_part:]).astype(jnp.bfloat16)
     partial_value = jnp.einsum(
-        "sucf,ufd->sucd", activated, expert_out, preferred_element_type=jnp.float32
+        "prf,pfd->prd", activated, full_out, preferred_element_type=jnp.float32
     ).astype(jnp.bfloat16)
-    returned = lax.all_to_all(partial_value, "seq", split_axis=0, concat_axis=0, tiled=True)
-    part_sum = jnp.sum(
-        returned.reshape(experts, hparts, capacity, column_list).astype(jnp.float32), axis=1
+    part_total = jnp.sum(partial_value.astype(jnp.float32), axis=0).astype(jnp.bfloat16)
+    returned = lax.all_to_all(
+        part_total.reshape(experts, capacity, column_list), EXPERT_AXES, split_axis=0, concat_axis=0, tiled=True
     )
-    part_sum = part_sum.reshape(experts * capacity, column_list)
+    part_sum = returned.reshape(experts * capacity, column_list).astype(jnp.float32)
     expert_sum = jnp.dot(
         combiner, part_sum, precision=lax.Precision.HIGHEST, preferred_element_type=jnp.float32
     )
@@ -173,19 +172,24 @@
 
 
 def solution(mesh):
+    seq_size = mesh.shape["seq"]
+    tp_size = mesh.shape["tp"]
+    split = (seq_size // 16, 4, 2, 2, tp_size)
+    fine_mesh = Mesh(mesh.devices.reshape(split), ("z", "yh", "yl", "c", "tp"))
+    seq_spec = SEQ
     in_specs = (
-        P("seq", None),
+        P(seq_spec, None),
         P(None, "tp"),
         P(None, "tp"),
         P(None, "tp"),
         P("tp", None),
-        P("seq", "tp"),
-        P("seq", "tp"),
-        P("seq", None),
-        P(("seq", "tp"), None),
-        P(("seq", "tp"), None),
-        P("seq", None, None),
-        P("seq", None, None),
+        P(seq_spec, "tp"),
+        P(seq_spec, "tp"),
+        P(seq_spec, None),
+        P(SEQ + ("tp",), None),
+        P(SEQ + ("tp",), None),
+        P(seq_spec, None, None),
+        P(seq_spec, None, None),
     )
-    out_specs = (P(("seq", "tp"), None), P(("seq", "tp"), None), P(("seq", "tp"), None))
-    return jax.shard_map(body, mesh=mesh, in_specs=in_specs, out_specs=out_specs, check_vma=False)
+    out_specs = (P(SEQ + ("tp",), None),) * 3
+    return jax.shard_map(body, mesh=fine_mesh, in_specs=in_specs, out_specs=out_specs, check_vma=False)

time: 621 us -> 281 us (0.45)
  the two profiles are of different devices: /device:TPU:24 before, /device:TPU:6 now
where the time goes in v1:
time: 281 us; the launch traced here: 277 us
  waiting for transfers between devices  196 us (70%)
  matrix products  25.6 us (9%)
  starting transfers between devices  23.7 us (8%)
  between operations  15.7 us (6%)
  other arithmetic  8.96 us (3%)
  local copies, waits for them, and re-layouts  7.04 us (3%)
    all_gather x1, waiting for transfers between devices, body(): whole_both = lax.all_gather(prefix_both, SEQ, axis=0, tiled=True)  83.4 us
    all_to_all x1, waiting for transfers between devices, body(): lax.all_to_all(part_total.reshape(experts, capacity, column_list), EXPERT...  44.3 us
    all_to_all x1, waiting for transfers between devices, body(): lax.all_to_all(outgoing, EXPERT_AXES, split_axis=0, concat_axis=0, tiled=...  33.1 us
    reduce_scatter x1, waiting for transfers between devices, body(): lax.psum_scatter(jnp.dot(attended, w_out, preferred_element_type=jnp.floa...  20.9 us
    all_gather x1, waiting for transfers between devices, body(): full_in = lax.all_gather(expert_in, PART_AXES, axis=0, tiled=True)  13.6 us
    all_to_all x1, starting transfers between devices, body(): lax.all_to_all(outgoing, EXPERT_AXES, split_axis=0, concat_axis=0, tiled=...  12.5 us
    all_to_all x1, starting transfers between devices, body(): lax.all_to_all(part_total.reshape(experts, capacity, column_list), EXPERT...  10.8 us
  transfers between devices with their start and end apart: 6, of which 5 were waited for; matrix products, arithmetic and copies ran while one was open for 6% of the time, Pallas kernels for 0%

profile of v1, /device:TPU:6, one launch (start us, length us, event | category | flops | bytes accessed | tf_op | source)
XLA Modules:
  0.0 277.2 jit_solution(2323323206248349324)
XLA Ops:
  8.1 1.4 pad_maximum_fusion.3
  9.6 0.8 fusion.25
  10.4 1.2 fusion.15
  11.6 0.8 compare_and_fusion
  12.6 1.5 fusion.37
  14.1 2.0 fusion.35
  16.1 0.3 fusion.41
  16.5 0.3 convolution_convert_fusion.1
  16.8 83.4 %all-gather.4.cloned.1.call-done = bf16[4096,256]{1,0:T(8,128)(2,1)} async-done(((bf16[32,256]{1,0:T(8,128)(2,1)}), bf16[4096,256]{1,0:T(8,128)(2,1)}) %all-gather.4.cloned.1.call-update) | async-done | bytes 2097168 | tf_op jit(solution)/shard_map/all_gather | solution.py:100
  100.3 3.0 %fusion.40 = (bf16[4096,128]{1,0:T(8,128)(2,1)}, bf16[4096,128]{1,0:T(8,128)(2,1)}) fusion(bf16[4096,256]{1,0:T(8,128)(2,1)} %all-gather.4.cloned.1.call-done), kind=kLoop, calls=%fused_computation.72 | loop fusion | bytes 4194304 | tf_op jit(solution)/shard_map/slice | solution.py:102
  103.2 1.5 copy.53
  104.7 2.3 copy.52
  107.0 3.1 %bitcast_reduce_fusion = (f32[128,2,3]{0,2,1:T(4,128)S(1)}, f32[2,4096,128,3]{2,1,3,0:T(8,128)S(1)}) fusion(bf16[4096,2,64,1]{0,2,3,1:T(8,128)(2,1)} %bitcast.80, bf16[128,2,3,32]{0,3,2,1:T(8,128)(2,1)S(1)} %bitcast.88, bf16[128,2,3,32]{0,3,2,1:T(8,128)(2,1)S(1)} %bitcast.86), kind=kOutput, calls=%fused_computation.1 | convolution fusion | flops 409140480 | bytes 13732864 | tf_op jit(solution)/shard_map/tkgd,pkd->tkgp/dot_general | solution.py:108
  110.1 2.0 fusion.1
  112.1 2.3 fusion.10
  114.6 1.3 fusion.42
  116.0 0.5 all-gather.6.cloned.1.call-update
  116.8 0.7 select_reduce_fusion.1
  117.6 0.2 fusion.19
  117.9 20.9 %reduce-scatter.2.cloned.1.call-done = f32[32,1536]{1,0:T(8,128)} async-done(((f32[128,1536]{1,0:T(8,128)}), f32[32,1536]{1,0:T(8,128)}) %reduce-scatter.2.cloned.1.call-update) | async-done | bytes 196624 | tf_op jit(solution)/shard_map/reduce_scatter | solution.py:129
  138.8 1.1 multiply_reduce_fusion
  139.9 2.7 convolution_convert_fusion
  142.6 12.5 %all-to-all-start = ((bf16[32,16,1536]{2,1,0:T(8,128)(2,1)}), bf16[32,16,1536]{2,1,0:T(8,128)(2,1)S(1)}, u32[]{:S(2)}, u32[]{:S(2)}) async-start(bf16[32,16,1536]{2,1,0:T(8,128)(2,1)} %bitcast.21), calls=%async_computation.1 | async-start | bytes 3145728 | tf_op jit(solution)/shard_map/all_to_all | solution.py:153
  155.1 0.2 all-gather.8.cloned.1.call-start
  155.4 0.4 all-gather.8.cloned.1.call-update
  155.7 13.6 %all-gather.6.cloned.1.call-done = bf16[4,1536,256]{2,1,0:T(8,128)(2,1)} async-done(((bf16[1,1536,256]{2,1,0:T(8,128)(2,1)}), bf16[4,1536,256]{2,1,0:T(8,128)(2,1)}) %all-gather.6.cloned.1.call-update) | async-done | bytes 3145744 | tf_op jit(solution)/shard_map/all_gather | solution.py:155
  169.3 33.1 %all-to-all-done = bf16[32,16,1536]{2,1,0:T(8,128)(2,1)S(1)} async-done(((bf16[32,16,1536]{2,1,0:T(8,128)(2,1)}), bf16[32,16,1536]{2,1,0:T(8,128)(2,1)S(1)}, u32[]{:S(2)}, u32[]{:S(2)}) %all-to-all-start) | async-done | bytes 1572896 | tf_op jit(solution)/shard_map/all_to_all | solution.py:153
  202.4 5.1 %convolution_bitcast_fusion = f32[4,512,256]{2,1,0:T(8,128)} fusion(bf16[512,1536,1]{1,0,2:T(8,128)(2,1)S(1)} %bitcast.81, bf16[4,1536,256]{2,1,0:T(8,128)(2,1)} %all-gather.6.cloned.1.call-done), kind=kOutput, calls=%fused_computation.8 | convolution fusion | flops 1610612736 | bytes 6815744 | tf_op jit(solution)/shard_map/rd,pdf->prf/dot_general | solution.py:157
  207.5 5.4 %convert_reduce_fusion = bf16[512,1536]{1,0:T(8,128)(2,1)} fusion(bf16[4,128,1536]{2,1,0:T(8,128)(2,1)} %all-gather.8.cloned.1.call-done, f32[4,512,256]{2,1,0:T(8,128)} %convolution_bitcast_fusion), kind=kOutput, calls=%fused_computation.5 | convolution fusion | flops 812384256 | bytes 5242880 | tf_op jit(solution)/shard_map/prf,pfd->prd/dot_general | solution.py:159
  212.8 10.8 %all-to-all-start.1 = ((bf16[32,16,1536]{2,1,0:T(8,128)(2,1)}), bf16[32,16,1536]{2,1,0:T(8,128)(2,1)S(1)}, u32[]{:S(2)}, u32[]{:S(2)}) async-start(bf16[32,16,1536]{2,1,0:T(8,128)(2,1)} %bitcast.82), calls=%async_computation.2 | async-start | bytes 3145728 | tf_op jit(solution)/shard_map/all_to_all | solution.py:163
  224.0 44.3 %all-to-all-done.1 = bf16[32,16,1536]{2,1,0:T(8,128)(2,1)S(1)} async-done(((bf16[32,16,1536]{2,1,0:T(8,128)(2,1)}), bf16[32,16,1536]{2,1,0:T(8,128)(2,1)S(1)}, u32[]{:S(2)}, u32[]{:S(2)}) %all-to-all-start.1) | async-done | bytes 1572896 | tf_op jit(solution)/shard_map/all_to_all | solution.py:163
  268.3 1.5 add_convert_fusion
  (38 shorter events, 1.4 us)
Async XLA Ops:
  8.0 106.6 %copy-start = (bf16[384,1536]{1,0:T(8,128)(2,1)S(1)}, bf16[384,1536]{1,0:T(8,128)(2,1)}, u32[]{:S(2)}) copy-start(bf16[384,1536]{1,0:T(8,128)(2,1)} %param.16) | copy-start | bytes 3538948
  8.0 92.2 %all-gather.4.cloned.1.call-start = ((), (), s32[]{:S(2)}) async-start(), calls=%async_computation.3 | async-start | bytes 2113536 | tf_op jit(solution)/shard_map/all_gather | solution.py:100
  9.5 129.3 %reduce-scatter.2.cloned.1.call-start = ((), (), s32[]{:S(2)}) async-start(), calls=%async_computation.4 | async-start | bytes 983040 | tf_op jit(solution)/shard_map/reduce_scatter | solution.py:129
  11.5 4.9 %copy-start.1 = (bf16[128,1536]{1,0:T(8,128)(2,1)S(1)}, bf16[128,1536]{1,0:T(8,128)(2,1)}, u32[]{:S(2)}) copy-start(bf16[128,1536]{1,0:T(8,128)(2,1)} %param.12) | copy-start | bytes 1179652
  11.5 4.9 %copy-start.3 = (bf16[1536,128]{1,0:T(8,128)(2,1)S(1)}, bf16[1536,128]{1,0:T(8,128)(2,1)}, u32[]{:S(2)}) copy-start(bf16[1536,128]{1,0:T(8,128)(2,1)} %param.15) | copy-start | bytes 1179652
  114.4 2.1 copy-start.4
  115.9 53.3 %all-gather.6.cloned.1.call-start = ((), (), s32[]{:S(2)}) async-start(), calls=%async_computation.5 | async-start | bytes 3932160 | tf_op jit(solution)/shard_map/all_gather | solution.py:155
  142.6 59.8 %all-to-all-start = ((bf16[32,16,1536]{2,1,0:T(8,128)(2,1)}), bf16[32,16,1536]{2,1,0:T(8,128)(2,1)S(1)}, u32[]{:S(2)}, u32[]{:S(2)}) async-start(bf16[32,16,1536]{2,1,0:T(8,128)(2,1)} %bitcast.21), calls=%async_computation.1 | async-start | bytes 3145728 | tf_op jit(solution)/shard_map/all_to_all | solution.py:153
  155.1 52.3 %all-gather.8.cloned.1.call-start = ((), (), s32[]{:S(2)}) async-start(), calls=%async_computation.6 | async-start | bytes 1966080 | tf_op jit(solution)/shard_map/all_gather | solution.py:156
  212.8 10.8 %copy-start.5 = (f32[32,8]{0,1:T(8,128)S(1)}, f32[32,8]{0,1:T(8,128)}, u32[]{:S(2)}) copy-start(f32[32,8]{0,1:T(8,128)} %param.21) | copy-start | bytes 3076
  212.8 55.4 %copy-start.2 = (f32[32,1536]{1,0:T(8,128)S(1)}, f32[32,1536]{1,0:T(8,128)}, u32[]{:S(2)}) copy-start(f32[32,1536]{1,0:T(8,128)} %reduce-scatter.2.cloned.1.call-done) | copy-start | bytes 589828
  212.8 55.4 %all-to-all-start.1 = ((bf16[32,16,1536]{2,1,0:T(8,128)(2,1)}), bf16[32,16,1536]{2,1,0:T(8,128)(2,1)S(1)}, u32[]{:S(2)}, u32[]{:S(2)}) async-start(bf16[32,16,1536]{2,1,0:T(8,128)(2,1)} %bitcast.82), calls=%async_computation.2 | async-start | bytes 3145728 | tf_op jit(solution)/shard_map/all_to_all | solution.py:163
Sparse Core Ops, SparseCore 0:
  12.5 87.6 all-gather.3
  116.1 22.6 reduce-scatter.1
Sparse Core Ops, SparseCore 1:
  118.5 50.7 all-gather.5
  171.2 35.1 all-gather.7

commit v2 on v1

--- a/solution.py
+++ b/solution.py
@@ -34,6 +34,15 @@
         [first_half * cosine - second * sine_part, second * cosine + first_half * sine_part],
         axis=-1,
     )
+
+
+def group_gather(local):
+    count = lax.axis_size(PART_AXES)
+    pieces = [local]
+    for shift in range(1, count):
+        ring = [(i, (i + shift) % count) for i in range(count)]
+        pieces.append(lax.ppermute(local, PART_AXES, ring))
+    return jnp.concatenate(pieces, axis=0)
 
 
 def body(
@@ -97,7 +106,10 @@
     )
     running = (row_top, denominator, numerator)
     prefix_both = jnp.concatenate([cached_prefix_keys, cached_prefix_values], axis=1)
-    whole_both = lax.all_gather(prefix_both, SEQ, axis=0, tiled=True)
+    seq_total = prefix_len // prefix_both.shape[0]
+    whole_both = lax.all_to_all(
+        jnp.broadcast_to(prefix_both[None], (seq_total,) + prefix_both.shape), SEQ, 0, 0, tiled=True
+    ).reshape(prefix_len, prefix_both.shape[1])
     kv_cols = cached_prefix_keys.shape[1]
     whole_keys = whole_both[:, :kv_cols]
     whole_values = whole_both[:, kv_cols:]
@@ -126,9 +138,15 @@
     )
     moe_rows = routes.shape[0]
     row_start = lax.axis_index("tp") * moe_rows
-    attn_sum = lax.psum_scatter(
-        jnp.dot(attended, w_out, preferred_element_type=jnp.float32), "tp", scatter_dimension=0, tiled=True
-    )
+    attn_part = jnp.dot(attended, w_out, preferred_element_type=jnp.float32)
+    tp_index = lax.axis_index("tp")
+    tp_count = lax.axis_size("tp")
+    attn_sum = lax.dynamic_slice_in_dim(attn_part, row_start, moe_rows, 0)
+    for shift in range(1, tp_count):
+        target = (tp_index + shift) % tp_count
+        sent = lax.dynamic_slice_in_dim(attn_part, target * moe_rows, moe_rows, 0)
+        ring = [(i, (i + shift) % tp_count) for i in range(tp_count)]
+        attn_sum = attn_sum + lax.ppermute(sent, "tp", ring)
     residual = (
         lax.dynamic_slice_in_dim(hidden_in, row_start, moe_rows, 0).astype(jnp.float32)
         + RESIDUAL * attn_sum
@@ -152,8 +170,8 @@
     outgoing = gathered.reshape(experts, capacity, column_list)
     incoming = lax.all_to_all(outgoing, EXPERT_AXES, split_axis=0, concat_axis=0, tiled=True)
     incoming = incoming.reshape(experts * capacity, column_list)
-    full_in = lax.all_gather(expert_in, PART_AXES, axis=0, tiled=True)
-    full_out = lax.all_gather(expert_out, PART_AXES, axis=0, tiled=True)
+    full_in = group_gather(expert_in)
+    full_out = group_gather(expert_out)
     gate_up = jnp.einsum("rd,pdf->prf", incoming, full_in, preferred_element_type=jnp.float32)
     activated = (jax.nn.silu(gate_up[..., :ff_part]) * gate_up[..., ff_part:]).astype(jnp.bfloat16)
     partial_value = jnp.einsum(

time: 281 us -> 259 us (0.922)
  waiting for transfers between devices: 196 us -> 155 us
  starting transfers between devices: 23.7 us -> 61.5 us
  between operations: 15.7 us -> 1.04 us
  matrix products: 25.6 us -> 18.9 us
  local copies, waits for them, and re-layouts: 7.04 us -> 12.5 us
  other arithmetic: 8.96 us -> 5.58 us
    all_gather x3 -> x0, waiting for transfers between devices: 97 us -> none  [the longest x1 83.4 us: body(): whole_both = lax.all_gather(prefix_both, SEQ, axis=0, tiled=True)]
    ppermute x0 -> x9, waiting for transfers between devices: none -> 67.2 us  [the longest x6 63.8 us: group_gather(): pieces.append(lax.ppermute(local, PART_AXES, ring))]
    all_to_all x0 -> x1, waiting for transfers between devices: none -> 48.7 us  [body(): lax.all_to_all(jnp.broadcast_to(prefix_both[None], (seq_total,) + prefix_...]
    all_to_all x1, waiting for transfers between devices: 33.1 us -> 0.01 us  [body(): lax.all_to_all(outgoing, EXPERT_AXES, split_axis=0, concat_axis=0, tiled=...]
    ppermute x0 -> x9, starting transfers between devices: none -> 25.2 us  [the longest x6 15.2 us: group_gather(): pieces.append(lax.ppermute(local, PART_AXES, ring))]
    reduce_scatter x1 -> x0, waiting for transfers between devices: 20.9 us -> none  [body(): lax.psum_scatter(jnp.dot(attended, w_out, preferred_element_type=jnp.floa...]
    all_to_all x0 -> x1, starting transfers between devices: none -> 18.5 us  [body(): lax.all_to_all(jnp.broadcast_to(prefix_both[None], (seq_total,) + prefix_...]
    all_to_all x1, starting transfers between devices: 12.5 us -> 7.2 us  [body(): lax.all_to_all(outgoing, EXPERT_AXES, split_axis=0, concat_axis=0, tiled=...]
  transfers between devices with their start and end apart: 6 -> 12, of which waited for: 5 -> 8; matrix products, arithmetic and copies ran while one was open for 6% -> 4% of each run, Pallas kernels for 0% -> 0%
where the time goes in v2:
time: 259 us; the launch traced here: 255 us
  waiting for transfers between devices  155 us (60%)
  starting transfers between devices  61.5 us (24%)
  matrix products  18.9 us (7%)
  local copies, waits for them, and re-layouts  12.5 us (5%)
  other arithmetic  5.58 us (2%)
    ppermute x6, waiting for transfers between devices, group_gather(): pieces.append(lax.ppermute(local, PART_AXES, ring))  63.8 us
    all_to_all x1, waiting for transfers between devices, body(): lax.all_to_all(jnp.broadcast_to(prefix_both[None], (seq_total,) + prefix_...  48.7 us
    all_to_all x1, waiting for transfers between devices, body(): lax.all_to_all(part_total.reshape(experts, capacity, column_list), EXPERT...  39.1 us
    all_to_all x1, starting transfers between devices, body(): lax.all_to_all(jnp.broadcast_to(prefix_both[None], (seq_total,) + prefix_...  18.5 us
    ppermute x6, starting transfers between devices, group_gather(): pieces.append(lax.ppermute(local, PART_AXES, ring))  15.2 us
    all_to_all x1, starting transfers between devices, body(): lax.all_to_all(part_total.reshape(experts, capacity, column_list), EXPERT...  10.7 us
    ppermute x3, starting transfers between devices, body(): attn_sum = attn_sum + lax.ppermute(sent, 'tp', ring)  9.94 us
    all_to_all x1, starting transfers between devices, body(): lax.all_to_all(outgoing, EXPERT_AXES, split_axis=0, concat_axis=0, tiled=...  7.2 us
  transfers between devices with their start and end apart: 12, of which 8 were waited for; matrix products, arithmetic and copies ran while one was open for 4% of the time, Pallas kernels for 0%

profile of v2, /device:TPU:6, one launch (start us, length us, event | category | flops | bytes accessed | tf_op | source)
XLA Modules:
  0.0 254.6 jit_solution(12439696578938541600)
XLA Ops:
  1.5 1.6 broadcast_in_dim.35
  3.0 18.5 %all-to-all-start = ((bf16[128,32,256]{2,1,0:T(8,128)(2,1)}), bf16[128,32,256]{2,1,0:T(8,128)(2,1)}, u32[]{:S(2)}, u32[]{:S(2)}) async-start(bf16[128,32,256]{2,1,0:T(8,128)(2,1)} %broadcast_in_dim.35), calls=%async_computation | async-start | bytes 4194304 | tf_op jit(solution)/shard_map/all_to_all | solution.py:110
  24.9 48.7 %all-to-all-done = bf16[128,32,256]{2,1,0:T(8,128)(2,1)} async-done(((bf16[128,32,256]{2,1,0:T(8,128)(2,1)}), bf16[128,32,256]{2,1,0:T(8,128)(2,1)}, u32[]{:S(2)}, u32[]{:S(2)}) %all-to-all-start) | async-done | bytes 2097184 | tf_op jit(solution)/shard_map/all_to_all | solution.py:110
  73.7 3.0 %fusion.60 = (bf16[4096,128]{1,0:T(8,128)(2,1)}, bf16[4096,128]{1,0:T(8,128)(2,1)}) fusion(bf16[4096,256]{1,0:T(8,128)(2,1)} %bitcast.12), kind=kLoop, calls=%fused_computation.93 | loop fusion | bytes 4194304 | tf_op jit(solution)/shard_map/slice | solution.py:114
  76.6 1.5 copy.59
  78.1 2.3 copy.58
  80.4 3.1 %bitcast_reduce_fusion = (f32[128,2,3]{0,2,1:T(4,128)S(1)}, f32[2,4096,128,3]{2,1,3,0:T(8,128)S(1)}) fusion(bf16[4096,2,64,1]{0,2,3,1:T(8,128)(2,1)} %bitcast.79, bf16[128,2,3,32]{0,3,2,1:T(8,128)(2,1)S(1)} %bitcast.87, bf16[128,2,3,32]{0,3,2,1:T(8,128)(2,1)S(1)} %bitcast.85), kind=kOutput, calls=%fused_computation.1 | convolution fusion | flops 409140480 | bytes 13732864 | tf_op jit(solution)/shard_map/tkgd,pkd->tkgp/dot_general | solution.py:120
  83.5 2.0 fusion.1
  85.5 2.3 fusion.28
  88.5 2.7 %collective-permute-start.2 = (f32[32,1536]{1,0:T(8,128)S(1)}, f32[32,1536]{1,0:T(8,128)S(1)}, u32[]{:S(2)}, u32[]{:S(2)}) collective-permute-start(f32[32,1536]{1,0:T(8,128)S(1)} %get-tuple-element.10), channel_id=1, source_target_pairs={{0,3},{1,0},{2,1},{3,2},{4,7},{5,4},{6,5},{7,6},{8,11},{9,8},{10,9... | collective-permute-start | bytes 589832 | tf_op jit(solution)/shard_map/ppermute | solution.py:149
  91.2 3.0 %collective-permute-start.1 = (f32[32,1536]{1,0:T(8,128)S(1)}, f32[32,1536]{1,0:T(8,128)S(1)}, u32[]{:S(2)}, u32[]{:S(2)}) collective-permute-start(f32[32,1536]{1,0:T(8,128)S(1)} %get-tuple-element.11), channel_id=1, source_target_pairs={{0,2},{1,3},{2,0},{3,1},{4,6},{5,7},{6,4},{7,5},{8,10},{9,11},{10,... | collective-permute-start | bytes 589832 | tf_op jit(solution)/shard_map/ppermute | solution.py:149
  94.2 4.2 %collective-permute-start = (f32[32,1536]{1,0:T(8,128)S(1)}, f32[32,1536]{1,0:T(8,128)S(1)}, u32[]{:S(2)}, u32[]{:S(2)}) collective-permute-start(f32[32,1536]{1,0:T(8,128)S(1)} %get-tuple-element.9), channel_id=1, source_target_pairs={{0,1},{1,2},{2,3},{3,0},{4,5},{5,6},{6,7},{7,4},{8,9},{9,10},{10,1... | collective-permute-start | bytes 589832 | tf_op jit(solution)/shard_map/ppermute | solution.py:149
  100.0 1.4 collective-permute-done.2
  101.5 2.0 collective-permute-done
  103.6 1.8 convolution_convert_fusion
  105.4 7.2 %all-to-all-start.1 = ((bf16[32,16,1536]{2,1,0:T(8,128)(2,1)}), bf16[32,16,1536]{2,1,0:T(8,128)(2,1)S(1)}, u32[]{:S(2)}, u32[]{:S(2)}) async-start(bf16[32,16,1536]{2,1,0:T(8,128)(2,1)} %bitcast.22), calls=%async_computation.1 | async-start | bytes 3145728 | tf_op jit(solution)/shard_map/all_to_all | solution.py:171
  112.6 2.3 copy.68
  114.9 1.9 collective-permute-start.5
  116.8 2.5 collective-permute-start.4
  119.3 2.1 collective-permute-start.3
  121.4 3.4 %collective-permute-start.8 = (bf16[1,128,1536]{2,1,0:T(8,128)(2,1)}, bf16[1,128,1536]{2,1,0:T(8,128)(2,1)}, u32[]{:S(2)}, u32[]{:S(2)}) collective-permute-start(bf16[1,128,1536]{2,1,0:T(8,128)(2,1)} %param.23), channel_id=1, source_target_pairs={{0,12},{4,0},{8,4},{12,8},{1,13},{5,1},{9,5},{13,9},{2,14},{6,2},{... | collective-permute-start | bytes 1179656 | tf_op jit(solution)/shard_map/ppermute | solution.py:44
  124.9 3.4 %collective-permute-start.7 = (bf16[1,128,1536]{2,1,0:T(8,128)(2,1)}, bf16[1,128,1536]{2,1,0:T(8,128)(2,1)}, u32[]{:S(2)}, u32[]{:S(2)}) collective-permute-start(bf16[1,128,1536]{2,1,0:T(8,128)(2,1)} %param.23), channel_id=1, source_target_pairs={{0,8},{4,12},{8,0},{12,4},{1,9},{5,13},{9,1},{13,5},{2,10},{6,14},... | collective-permute-start | bytes 1179656 | tf_op jit(solution)/shard_map/ppermute | solution.py:44
  128.3 38.5 %collective-permute-done.5 = bf16[1,1536,256]{1,2,0:T(8,128)(2,1)S(1)} collective-permute-done((bf16[1,1536,256]{1,2,0:T(8,128)(2,1)}, bf16[1,1536,256]{1,2,0:T(8,128)(2,1)S(1)}, u32[]{:S(2)}, u32[]{:S(2)}) %collective-permute-start.5) | collective-permute-done | bytes 786464 | tf_op jit(solution)/shard_map/ppermute | solution.py:44
  166.8 1.9 collective-permute-start.6
  168.7 14.9 %collective-permute-done.4 = bf16[1,1536,256]{1,2,0:T(8,128)(2,1)S(1)} collective-permute-done((bf16[1,1536,256]{1,2,0:T(8,128)(2,1)}, bf16[1,1536,256]{1,2,0:T(8,128)(2,1)S(1)}, u32[]{:S(2)}, u32[]{:S(2)}) %collective-permute-start.4) | collective-permute-done | bytes 786464 | tf_op jit(solution)/shard_map/ppermute | solution.py:44
  184.5 3.5 %fusion.13 = f32[4,512,256]{1,2,0:T(8,128)S(1)} fusion(bf16[512,1536,1]{1,0,2:T(8,128)(2,1)S(1)} %bitcast.80, bf16[1,1536,256]{1,2,0:T(8,128)(2,1)} %copy-done.8, bf16[1,1536,256]{1,2,0:T(8,128)(2,1)} %copy-done.9, bf16[1,1536,256]{1,2,0:T(8,128)(2,1)} %collective-permute-done.3, bf16[1,1536,256]{1,2,0:T(8,128)(2,1)} %copy.68), kind=kOutput, calls=%fused_computation.16 | convolution fusion | flops 1615331328 | bytes 6815744 | tf_op jit(solution)/shard_map/rd,pdf->prf/dot_general | solution.py:175
  188.0 4.1 %collective-permute-done.8 = bf16[1,128,1536]{2,1,0:T(8,128)(2,1)} collective-permute-done((bf16[1,128,1536]{2,1,0:T(8,128)(2,1)}, bf16[1,128,1536]{2,1,0:T(8,128)(2,1)}, u32[]{:S(2)}, u32[]{:S(2)}) %collective-permute-start.8) | collective-permute-done | bytes 393248 | tf_op jit(solution)/shard_map/ppermute | solution.py:44
  192.1 6.3 %collective-permute-done.7 = bf16[1,128,1536]{2,1,0:T(8,128)(2,1)} collective-permute-done((bf16[1,128,1536]{2,1,0:T(8,128)(2,1)}, bf16[1,128,1536]{2,1,0:T(8,128)(2,1)}, u32[]{:S(2)}, u32[]{:S(2)}) %collective-permute-start.7) | collective-permute-done | bytes 393248 | tf_op jit(solution)/shard_map/ppermute | solution.py:44
  198.4 4.6 %convert_reduce_fusion = bf16[512,1536]{1,0:T(8,128)(2,1)} fusion(bf16[1,128,1536]{2,1,0:T(8,128)(2,1)} %collective-permute-done.8, bf16[1,128,1536]{2,1,0:T(8,128)(2,1)} %collective-permute-done.7, bf16[1,128,1536]{2,1,0:T(8,128)(2,1)} %collective-permute-done.6, bf16[1,128,1536]{2,1,0:T(8,128)(2,1)S(1)} %copy-done.10, f32[4,512,256]{1,2,0:T(8,128)S(1)} %fusion.13), kind=kOutput, calls=%fused_computation.5 | convolution fusion | flops 814743552 | bytes 5242880 | tf_op jit(solution)/shard_map/prf,pfd->prd/dot_general | solution.py:177
  203.0 10.7 %all-to-all-start.2 = ((bf16[32,16,1536]{2,1,0:T(8,128)(2,1)}), bf16[32,16,1536]{2,1,0:T(8,128)(2,1)S(1)}, u32[]{:S(2)}, u32[]{:S(2)}) async-start(bf16[32,16,1536]{2,1,0:T(8,128)(2,1)} %bitcast.81), calls=%async_computation.2 | async-start | bytes 3145728 | tf_op jit(solution)/shard_map/all_to_all | solution.py:181
  214.0 39.1 %all-to-all-done.2 = bf16[32,16,1536]{2,1,0:T(8,128)(2,1)S(1)} async-done(((bf16[32,16,1536]{2,1,0:T(8,128)(2,1)}), bf16[32,16,1536]{2,1,0:T(8,128)(2,1)S(1)}, u32[]{:S(2)}, u32[]{:S(2)}) %all-to-all-start.2) | async-done | bytes 1572896 | tf_op jit(solution)/shard_map/all_to_all | solution.py:181
  253.1 1.5 add_convert_fusion
  (59 shorter events, 7.7 us)
Async XLA Ops:
  0.6 87.4 %copy-start = (bf16[384,1536]{1,0:T(8,128)(2,1)S(1)}, bf16[384,1536]{1,0:T(8,128)(2,1)}, u32[]{:S(2)}) copy-start(bf16[384,1536]{1,0:T(8,128)(2,1)} %param.16) | copy-start | bytes 3538948
  3.0 18.6 %copy-start.5 = (s32[32,8]{0,1:T(8,128)S(1)}, s32[32,8]{0,1:T(8,128)}, u32[]{:S(2)}) copy-start(s32[32,8]{0,1:T(8,128)} %param.20) | copy-start | bytes 3076
  3.0 19.6 %copy-start.7 = (s32[1,128]{1,0:T(1,128)S(1)}, s32[1,128]{1,0:T(1,128)}, u32[]{:S(2)}) copy-start(s32[1,128]{1,0:T(1,128)} %param.19) | copy-start | bytes 1540
  3.0 19.7 %copy-start.1 = (bf16[128,1536]{1,0:T(8,128)(2,1)S(1)}, bf16[128,1536]{1,0:T(8,128)(2,1)}, u32[]{:S(2)}) copy-start(bf16[128,1536]{1,0:T(8,128)(2,1)} %param.12) | copy-start | bytes 1179652
  3.0 20.1 %copy-start.3 = (bf16[1536,128]{1,0:T(8,128)(2,1)S(1)}, bf16[1536,128]{1,0:T(8,128)(2,1)}, u32[]{:S(2)}) copy-start(bf16[1536,128]{1,0:T(8,128)(2,1)} %param.14) | copy-start | bytes 1179652
  3.0 20.5 %copy-start.2 = (bf16[1536,384]{1,0:T(8,128)(2,1)S(1)}, bf16[1536,384]{1,0:T(8,128)(2,1)}, u32[]{:S(2)}) copy-start(bf16[1536,384]{1,0:T(8,128)(2,1)} %param.13) | copy-start | bytes 3538948
  3.0 70.6 %all-to-all-start = ((bf16[128,32,256]{2,1,0:T(8,128)(2,1)}), bf16[128,32,256]{2,1,0:T(8,128)(2,1)}, u32[]{:S(2)}, u32[]{:S(2)}) async-start(bf16[128,32,256]{2,1,0:T(8,128)(2,1)} %broadcast_in_dim.35), calls=%async_computation | async-start | bytes 4194304 | tf_op jit(solution)/shard_map/all_to_all | solution.py:110
  22.9 1.7 copy-start.4
  88.5 13.0 %collective-permute-start.2 = (f32[32,1536]{1,0:T(8,128)S(1)}, f32[32,1536]{1,0:T(8,128)S(1)}, u32[]{:S(2)}, u32[]{:S(2)}) collective-permute-start(f32[32,1536]{1,0:T(8,128)S(1)} %get-tuple-element.10), channel_id=1, source_target_pairs={{0,3},{1,0},{2,1},{3,2},{4,7},{5,4},{6,5},{7,6},{8,11},{9,8},{10,9... | collective-permute-start | bytes 589832 | tf_op jit(solution)/shard_map/ppermute | solution.py:149
  91.2 10.3 %collective-permute-start.1 = (f32[32,1536]{1,0:T(8,128)S(1)}, f32[32,1536]{1,0:T(8,128)S(1)}, u32[]{:S(2)}, u32[]{:S(2)}) collective-permute-start(f32[32,1536]{1,0:T(8,128)S(1)} %get-tuple-element.11), channel_id=1, source_target_pairs={{0,2},{1,3},{2,0},{3,1},{4,6},{5,7},{6,4},{7,5},{8,10},{9,11},{10,... | collective-permute-start | bytes 589832 | tf_op jit(solution)/shard_map/ppermute | solution.py:149
  94.2 9.2 %collective-permute-start = (f32[32,1536]{1,0:T(8,128)S(1)}, f32[32,1536]{1,0:T(8,128)S(1)}, u32[]{:S(2)}, u32[]{:S(2)}) collective-permute-start(f32[32,1536]{1,0:T(8,128)S(1)} %get-tuple-element.9), channel_id=1, source_target_pairs={{0,1},{1,2},{2,3},{3,0},{4,5},{5,6},{6,7},{7,4},{8,9},{9,10},{10,1... | collective-permute-start | bytes 589832 | tf_op jit(solution)/shard_map/ppermute | solution.py:149
  105.4 79.1 %all-to-all-start.1 = ((bf16[32,16,1536]{2,1,0:T(8,128)(2,1)}), bf16[32,16,1536]{2,1,0:T(8,128)(2,1)S(1)}, u32[]{:S(2)}, u32[]{:S(2)}) async-start(bf16[32,16,1536]{2,1,0:T(8,128)(2,1)} %bitcast.22), calls=%async_computation.1 | async-start | bytes 3145728 | tf_op jit(solution)/shard_map/all_to_all | solution.py:171
  114.9 51.9 %collective-permute-start.5 = (bf16[1,1536,256]{1,2,0:T(8,128)(2,1)}, bf16[1,1536,256]{1,2,0:T(8,128)(2,1)S(1)}, u32[]{:S(2)}, u32[]{:S(2)}) collective-permute-start(bf16[1,1536,256]{1,2,0:T(8,128)(2,1)} %copy.68), channel_id=1, source_target_pairs={{0,12},{4,0},{8,4},{12,8},{1,13},{5,1},{9,5},{13,9},{2,14},{6,2},{... | collective-permute-start | bytes 2359304 | tf_op jit(solution)/shard_map/ppermute | solution.py:44
  116.8 66.8 %collective-permute-start.4 = (bf16[1,1536,256]{1,2,0:T(8,128)(2,1)}, bf16[1,1536,256]{1,2,0:T(8,128)(2,1)S(1)}, u32[]{:S(2)}, u32[]{:S(2)}) collective-permute-start(bf16[1,1536,256]{1,2,0:T(8,128)(2,1)} %copy.68), channel_id=1, source_target_pairs={{0,8},{4,12},{8,0},{12,4},{1,9},{5,13},{9,1},{13,5},{2,10},{6,14},... | collective-permute-start | bytes 2359304 | tf_op jit(solution)/shard_map/ppermute | solution.py:44
  119.3 65.2 %collective-permute-start.3 = (bf16[1,1536,256]{1,2,0:T(8,128)(2,1)}, bf16[1,1536,256]{1,2,0:T(8,128)(2,1)}, u32[]{:S(2)}, u32[]{:S(2)}) collective-permute-start(bf16[1,1536,256]{1,2,0:T(8,128)(2,1)} %copy.68), channel_id=1, source_target_pairs={{0,4},{4,8},{8,12},{12,0},{1,5},{5,9},{9,13},{13,1},{2,6},{6,10},{... | collective-permute-start | bytes 2359304 | tf_op jit(solution)/shard_map/ppermute | solution.py:44
  121.4 70.6 %collective-permute-start.8 = (bf16[1,128,1536]{2,1,0:T(8,128)(2,1)}, bf16[1,128,1536]{2,1,0:T(8,128)(2,1)}, u32[]{:S(2)}, u32[]{:S(2)}) collective-permute-start(bf16[1,128,1536]{2,1,0:T(8,128)(2,1)} %param.23), channel_id=1, source_target_pairs={{0,12},{4,0},{8,4},{12,8},{1,13},{5,1},{9,5},{13,9},{2,14},{6,2},{... | collective-permute-start | bytes 1179656 | tf_op jit(solution)/shard_map/ppermute | solution.py:44
  124.9 73.5 %collective-permute-start.7 = (bf16[1,128,1536]{2,1,0:T(8,128)(2,1)}, bf16[1,128,1536]{2,1,0:T(8,128)(2,1)}, u32[]{:S(2)}, u32[]{:S(2)}) collective-permute-start(bf16[1,128,1536]{2,1,0:T(8,128)(2,1)} %param.23), channel_id=1, source_target_pairs={{0,8},{4,12},{8,0},{12,4},{1,9},{5,13},{9,1},{13,5},{2,10},{6,14},... | collective-permute-start | bytes 1179656 | tf_op jit(solution)/shard_map/ppermute | solution.py:44
  166.8 16.9 %copy-start.8 = (bf16[1,1536,256]{1,2,0:T(8,128)(2,1)}, bf16[1,1536,256]{1,2,0:T(8,128)(2,1)S(1)}, u32[]{:S(2)}) copy-start(bf16[1,1536,256]{1,2,0:T(8,128)(2,1)S(1)} %collective-permute-done.5) | copy-start | bytes 2359300
  166.8 31.6 %collective-permute-start.6 = (bf16[1,128,1536]{2,1,0:T(8,128)(2,1)}, bf16[1,128,1536]{2,1,0:T(8,128)(2,1)}, u32[]{:S(2)}, u32[]{:S(2)}) collective-permute-start(bf16[1,128,1536]{2,1,0:T(8,128)(2,1)} %param.23), channel_id=1, source_target_pairs={{0,4},{4,8},{8,12},{12,0},{1,5},{5,9},{9,13},{13,1},{2,6},{6,10},{... | collective-permute-start | bytes 1179656 | tf_op jit(solution)/shard_map/ppermute | solution.py:44
  183.7 0.9 copy-start.9
  184.5 13.8 %copy-start.10 = (bf16[1,128,1536]{2,1,0:T(8,128)(2,1)S(1)}, bf16[1,128,1536]{2,1,0:T(8,128)(2,1)}, u32[]{:S(2)}) copy-start(bf16[1,128,1536]{2,1,0:T(8,128)(2,1)} %param.23) | copy-start | bytes 1179652
  203.0 10.7 %copy-start.6 = (f32[32,8]{0,1:T(8,128)S(1)}, f32[32,8]{0,1:T(8,128)}, u32[]{:S(2)}) copy-start(f32[32,8]{0,1:T(8,128)} %param.21) | copy-start | bytes 3076
  203.0 50.1 %all-to-all-start.2 = ((bf16[32,16,1536]{2,1,0:T(8,128)(2,1)}), bf16[32,16,1536]{2,1,0:T(8,128)(2,1)S(1)}, u32[]{:S(2)}, u32[]{:S(2)}) async-start(bf16[32,16,1536]{2,1,0:T(8,128)(2,1)} %bitcast.81), calls=%async_computation.2 | async-start | bytes 3145728 | tf_op jit(solution)/shard_map/all_to_all | solution.py:181

commit v3 on v2

--- a/solution.py
+++ b/solution.py
@@ -34,15 +34,6 @@
         [first_half * cosine - second * sine_part, second * cosine + first_half * sine_part],
         axis=-1,
     )
-
-
-def group_gather(local):
-    count = lax.axis_size(PART_AXES)
-    pieces = [local]
-    for shift in range(1, count):
-        ring = [(i, (i + shift) % count) for i in range(count)]
-        pieces.append(lax.ppermute(local, PART_AXES, ring))
-    return jnp.concatenate(pieces, axis=0)
 
 
 def body(
@@ -59,6 +50,13 @@
     expert_in,
     expert_out,
 ):
+    in_cols = expert_in.shape[2]
+    packed = jnp.concatenate(
+        [expert_in, expert_out.reshape(expert_out.shape[0], expert_in.shape[1], -1)], axis=2
+    )
+    packed = lax.all_gather(packed, PART_AXES, axis=0, tiled=True)
+    full_in = packed[..., :in_cols]
+    full_out = packed[..., in_cols:].reshape((packed.shape[0],) + expert_out.shape[1:])
     rows_dev = hidden_in.shape[0]
     column_list = hidden_in.shape[1]
     head_size = HEAD_WIDTH
@@ -170,8 +168,6 @@
     outgoing = gathered.reshape(experts, capacity, column_list)
     incoming = lax.all_to_all(outgoing, EXPERT_AXES, split_axis=0, concat_axis=0, tiled=True)
     incoming = incoming.reshape(experts * capacity, column_list)
-    full_in = group_gather(expert_in)
-    full_out = group_gather(expert_out)
     gate_up = jnp.einsum("rd,pdf->prf", incoming, full_in, preferred_element_type=jnp.float32)
     activated = (jax.nn.silu(gate_up[..., :ff_part]) * gate_up[..., ff_part:]).astype(jnp.bfloat16)
     partial_value = jnp.einsum(

time: 259 us -> 249 us (0.961)
  the two profiles are of different devices: /device:TPU:6 before, /device:TPU:80 now
where the time goes in v3:
time: 249 us; the launch traced here: 248 us
  waiting for transfers between devices  148 us (59%)
  starting transfers between devices  45.2 us (18%)
  matrix products  18.4 us (7%)
  between operations  14.4 us (6%)
  local copies, waits for them, and re-layouts  14.2 us (6%)
  other arithmetic  7.97 us (3%)
    all_to_all x1, waiting for transfers between devices, body(): lax.all_to_all(jnp.broadcast_to(prefix_both[None], (seq_total,) + prefix_...  57.3 us
    all_to_all x1, waiting for transfers between devices, body(): lax.all_to_all(part_total.reshape(experts, capacity, column_list), EXPERT...  43.4 us
    all_to_all x1, waiting for transfers between devices, body(): lax.all_to_all(outgoing, EXPERT_AXES, split_axis=0, concat_axis=0, tiled=...  41.8 us
    all_to_all x1, starting transfers between devices, body(): lax.all_to_all(jnp.broadcast_to(prefix_both[None], (seq_total,) + prefix_...  16.9 us
    all_to_all x1, starting transfers between devices, body(): lax.all_to_all(part_total.reshape(experts, capacity, column_list), EXPERT...  11 us
    ppermute x3, starting transfers between devices, body(): attn_sum = attn_sum + lax.ppermute(sent, 'tp', ring)  10.2 us
    all_to_all x1, starting transfers between devices, body(): lax.all_to_all(outgoing, EXPERT_AXES, split_axis=0, concat_axis=0, tiled=...  7 us
    ppermute x3, waiting for transfers between devices, body(): attn_sum = attn_sum + lax.ppermute(sent, 'tp', ring)  5.56 us
  transfers between devices with their start and end apart: 7, of which 6 were waited for; matrix products, arithmetic and copies ran while one was open for 11% of the time, Pallas kernels for 0%

profile of v3, /device:TPU:80, one launch (start us, length us, event | category | flops | bytes accessed | tf_op | source)
XLA Modules:
  0.0 248.2 jit_solution(14403359115709240363)
XLA Ops:
  7.2 0.8 pad_maximum_fusion.4
  8.0 1.7 broadcast_in_dim.35
  9.7 16.9 %all-to-all-start = ((bf16[128,32,256]{2,1,0:T(8,128)(2,1)}), bf16[128,32,256]{2,1,0:T(8,128)(2,1)}, u32[]{:S(2)}, u32[]{:S(2)}) async-start(bf16[128,32,256]{2,1,0:T(8,128)(2,1)} %broadcast_in_dim.35), calls=%async_computation | async-start | bytes 4194304 | tf_op jit(solution)/shard_map/all_to_all | solution.py:108
  26.7 0.5 reshape.207
  27.2 2.4 pad_maximum_fusion
  29.9 0.7 select_reduce_fusion.1
  31.6 0.6 fusion.40
  33.0 57.3 %all-to-all-done = bf16[128,32,256]{2,1,0:T(8,128)(2,1)} async-done(((bf16[128,32,256]{2,1,0:T(8,128)(2,1)}), bf16[128,32,256]{2,1,0:T(8,128)(2,1)}, u32[]{:S(2)}, u32[]{:S(2)}) %all-to-all-start) | async-done | bytes 2097184 | tf_op jit(solution)/shard_map/all_to_all | solution.py:108
  90.3 3.1 %fusion.45 = (bf16[4096,128]{1,0:T(8,128)(2,1)}, bf16[4096,128]{1,0:T(8,128)(2,1)}) fusion(bf16[4096,256]{1,0:T(8,128)(2,1)} %bitcast.12), kind=kLoop, calls=%fused_computation.79 | loop fusion | bytes 4194304 | tf_op jit(solution)/shard_map/slice | solution.py:112
  93.4 1.5 copy.62
  94.9 2.3 copy.61
  97.3 3.1 %bitcast_reduce_fusion = (f32[128,2,3]{0,2,1:T(4,128)S(1)}, f32[2,4096,128,3]{2,1,3,0:T(8,128)S(1)}) fusion(bf16[4096,2,64,1]{0,2,3,1:T(8,128)(2,1)} %bitcast.80, bf16[128,2,3,32]{0,3,2,1:T(8,128)(2,1)S(1)} %bitcast.87, bf16[128,2,3,32]{0,3,2,1:T(8,128)(2,1)S(1)} %bitcast.85), kind=kOutput, calls=%fused_computation.1 | convolution fusion | flops 409140480 | bytes 13732864 | tf_op jit(solution)/shard_map/tkgd,pkd->tkgp/dot_general | solution.py:118
  100.3 2.0 fusion.1
  102.4 2.3 fusion.15
  104.9 0.4 fusion.47
  105.4 4.7 %collective-permute-start.2 = (f32[32,1536]{1,0:T(8,128)S(1)}, f32[32,1536]{1,0:T(8,128)S(1)}, u32[]{:S(2)}, u32[]{:S(2)}) collective-permute-start(f32[32,1536]{1,0:T(8,128)S(1)} %get-tuple-element.10), channel_id=1, source_target_pairs={{0,3},{1,0},{2,1},{3,2},{4,7},{5,4},{6,5},{7,6},{8,11},{9,8},{10,9... | collective-permute-start | bytes 589832 | tf_op jit(solution)/shard_map/ppermute | solution.py:147
  110.1 2.7 %collective-permute-start.1 = (f32[32,1536]{1,0:T(8,128)S(1)}, f32[32,1536]{1,0:T(8,128)S(1)}, u32[]{:S(2)}, u32[]{:S(2)}) collective-permute-start(f32[32,1536]{1,0:T(8,128)S(1)} %get-tuple-element.11), channel_id=1, source_target_pairs={{0,2},{1,3},{2,0},{3,1},{4,6},{5,7},{6,4},{7,5},{8,10},{9,11},{10,... | collective-permute-start | bytes 589832 | tf_op jit(solution)/shard_map/ppermute | solution.py:147
  112.8 2.8 %collective-permute-start = (f32[32,1536]{1,0:T(8,128)S(1)}, f32[32,1536]{1,0:T(8,128)S(1)}, u32[]{:S(2)}, u32[]{:S(2)}) collective-permute-start(f32[32,1536]{1,0:T(8,128)S(1)} %get-tuple-element.9), channel_id=1, source_target_pairs={{0,1},{1,2},{2,3},{3,0},{4,5},{5,6},{6,7},{7,4},{8,9},{9,10},{10,1... | collective-permute-start | bytes 589832 | tf_op jit(solution)/shard_map/ppermute | solution.py:147
  115.6 0.6 multiply_add_fusion.2
  116.2 0.8 copy.66
  117.5 3.2 %collective-permute-done.1 = f32[32,1536]{1,0:T(8,128)S(1)} collective-permute-done((f32[32,1536]{1,0:T(8,128)S(1)}, f32[32,1536]{1,0:T(8,128)S(1)}, u32[]{:S(2)}, u32[]{:S(2)}) %collective-permute-start.1) | collective-permute-done | bytes 196640 | tf_op jit(solution)/shard_map/ppermute | solution.py:147
  120.7 2.0 collective-permute-done
  122.9 1.9 convolution_convert_fusion
  124.8 7.0 %all-to-all-start.1 = ((bf16[32,16,1536]{2,1,0:T(8,128)(2,1)}), bf16[32,16,1536]{2,1,0:T(8,128)(2,1)}, u32[]{:S(2)}, u32[]{:S(2)}) async-start(bf16[32,16,1536]{2,1,0:T(8,128)(2,1)} %bitcast.22), calls=%async_computation.1 | async-start | bytes 3145728 | tf_op jit(solution)/shard_map/all_to_all | solution.py:169
  131.8 1.4 slice-done
  133.2 2.6 %reshape.210 = bf16[4,128,1536]{2,1,0:T(8,128)(2,1)} reshape(bf16[4,1536,128]{2,1,0:T(8,128)(2,1)S(1)} %slice-done) | data formatting | bytes 3145728 | tf_op jit(solution)/shard_map/reshape | solution.py:59
  135.9 41.8 %all-to-all-done.1 = bf16[32,16,1536]{2,1,0:T(8,128)(2,1)} async-done(((bf16[32,16,1536]{2,1,0:T(8,128)(2,1)}), bf16[32,16,1536]{2,1,0:T(8,128)(2,1)}, u32[]{:S(2)}, u32[]{:S(2)}) %all-to-all-start.1) | async-done | bytes 1572896 | tf_op jit(solution)/shard_map/all_to_all | solution.py:169
  177.6 4.3 %fusion.7 = f32[4,512,256]{1,2,0:T(8,128)S(1)} fusion(bf16[512,1536,1]{1,0,2:T(8,128)(2,1)} %bitcast.24, bf16[4,1536,384]{2,1,0:T(8,128)(2,1)} %all-gather.2.cloned.1.call-done), kind=kOutput, calls=%fused_computation.10 | convolution fusion | flops 1610612736 | bytes 6815744 | tf_op jit(solution)/shard_map/rd,pdf->prf/dot_general | solution.py:171
  181.9 3.1 %convert_reduce_fusion = bf16[512,1536]{1,0:T(8,128)(2,1)} fusion(bf16[4,128,1536]{2,1,0:T(8,128)(2,1)S(1)} %copy-done.2, f32[4,512,256]{1,2,0:T(8,128)S(1)} %fusion.7), kind=kOutput, calls=%fused_computation.5 | convolution fusion | flops 812384256 | bytes 5242880 | tf_op jit(solution)/shard_map/prf,pfd->prd/dot_general | solution.py:173
  185.1 11.0 %all-to-all-start.2 = ((bf16[32,16,1536]{2,1,0:T(8,128)(2,1)}), bf16[32,16,1536]{2,1,0:T(8,128)(2,1)S(1)}, u32[]{:S(2)}, u32[]{:S(2)}) async-start(bf16[32,16,1536]{2,1,0:T(8,128)(2,1)} %bitcast.81), calls=%async_computation.2 | async-start | bytes 3145728 | tf_op jit(solution)/shard_map/all_to_all | solution.py:177
  196.4 43.4 %all-to-all-done.2 = bf16[32,16,1536]{2,1,0:T(8,128)(2,1)S(1)} async-done(((bf16[32,16,1536]{2,1,0:T(8,128)(2,1)}), bf16[32,16,1536]{2,1,0:T(8,128)(2,1)S(1)}, u32[]{:S(2)}, u32[]{:S(2)}) %all-to-all-start.2) | async-done | bytes 1572896 | tf_op jit(solution)/shard_map/all_to_all | solution.py:177
  239.8 1.5 add_convert_fusion
  (52 shorter events, 3.3 us)
Async XLA Ops:
  7.2 97.7 %copy-start = (bf16[384,1536]{1,0:T(8,128)(2,1)S(1)}, bf16[384,1536]{1,0:T(8,128)(2,1)}, u32[]{:S(2)}) copy-start(bf16[384,1536]{1,0:T(8,128)(2,1)} %param.16) | copy-start | bytes 3538948
  9.6 17.0 %copy-start.4 = (bf16[1,128,1536]{2,1,0:T(8,128)(2,1)S(1)}, bf16[1,128,1536]{2,1,0:T(8,128)(2,1)}, u32[]{:S(2)}) copy-start(bf16[1,128,1536]{2,1,0:T(8,128)(2,1)} %param.23) | copy-start | bytes 1179652
  9.7 80.7 %all-to-all-start = ((bf16[128,32,256]{2,1,0:T(8,128)(2,1)}), bf16[128,32,256]{2,1,0:T(8,128)(2,1)}, u32[]{:S(2)}, u32[]{:S(2)}) async-start(bf16[128,32,256]{2,1,0:T(8,128)(2,1)} %broadcast_in_dim.35), calls=%async_computation | async-start | bytes 4194304 | tf_op jit(solution)/shard_map/all_to_all | solution.py:108
  26.6 3.1 %copy-start.7 = (s32[32,8]{0,1:T(8,128)S(1)}, s32[32,8]{0,1:T(8,128)}, u32[]{:S(2)}) copy-start(s32[32,8]{0,1:T(8,128)} %param.20) | copy-start | bytes 3076
  26.6 105.2 %all-gather.2.cloned.1.call-start = ((), (), s32[]{:S(2)}) async-start(), calls=%async_computation.3 | async-start | bytes 5898240 | tf_op jit(solution)/shard_map/all_gather | solution.py:57
  27.2 3.5 %copy-start.9 = (s32[1,128]{1,0:T(1,128)S(1)}, s32[1,128]{1,0:T(1,128)}, u32[]{:S(2)}) copy-start(s32[1,128]{1,0:T(1,128)} %param.19) | copy-start | bytes 1540
  27.2 3.6 %copy-start.1 = (bf16[128,1536]{1,0:T(8,128)(2,1)S(1)}, bf16[128,1536]{1,0:T(8,128)(2,1)}, u32[]{:S(2)}) copy-start(bf16[128,1536]{1,0:T(8,128)(2,1)} %param.12) | copy-start | bytes 1179652
  27.2 4.1 %copy-start.5 = (bf16[1536,128]{1,0:T(8,128)(2,1)S(1)}, bf16[1536,128]{1,0:T(8,128)(2,1)}, u32[]{:S(2)}) copy-start(bf16[1536,128]{1,0:T(8,128)(2,1)} %param.14) | copy-start | bytes 1179652
  27.2 4.4 %copy-start.3 = (bf16[1536,384]{1,0:T(8,128)(2,1)S(1)}, bf16[1536,384]{1,0:T(8,128)(2,1)}, u32[]{:S(2)}) copy-start(bf16[1536,384]{1,0:T(8,128)(2,1)} %param.13) | copy-start | bytes 3538948
  31.0 1.7 copy-start.6
  105.4 12.1 %collective-permute-start.2 = (f32[32,1536]{1,0:T(8,128)S(1)}, f32[32,1536]{1,0:T(8,128)S(1)}, u32[]{:S(2)}, u32[]{:S(2)}) collective-permute-start(f32[32,1536]{1,0:T(8,128)S(1)} %get-tuple-element.10), channel_id=1, source_target_pairs={{0,3},{1,0},{2,1},{3,2},{4,7},{5,4},{6,5},{7,6},{8,11},{9,8},{10,9... | collective-permute-start | bytes 589832 | tf_op jit(solution)/shard_map/ppermute | solution.py:147
  110.1 10.6 %collective-permute-start.1 = (f32[32,1536]{1,0:T(8,128)S(1)}, f32[32,1536]{1,0:T(8,128)S(1)}, u32[]{:S(2)}, u32[]{:S(2)}) collective-permute-start(f32[32,1536]{1,0:T(8,128)S(1)} %get-tuple-element.11), channel_id=1, source_target_pairs={{0,2},{1,3},{2,0},{3,1},{4,6},{5,7},{6,4},{7,5},{8,10},{9,11},{10,... | collective-permute-start | bytes 589832 | tf_op jit(solution)/shard_map/ppermute | solution.py:147
  112.8 9.9 %collective-permute-start = (f32[32,1536]{1,0:T(8,128)S(1)}, f32[32,1536]{1,0:T(8,128)S(1)}, u32[]{:S(2)}, u32[]{:S(2)}) collective-permute-start(f32[32,1536]{1,0:T(8,128)S(1)} %get-tuple-element.9), channel_id=1, source_target_pairs={{0,1},{1,2},{2,3},{3,0},{4,5},{5,6},{6,7},{7,4},{8,9},{9,10},{10,1... | collective-permute-start | bytes 589832 | tf_op jit(solution)/shard_map/ppermute | solution.py:147
  124.8 52.8 %all-to-all-start.1 = ((bf16[32,16,1536]{2,1,0:T(8,128)(2,1)}), bf16[32,16,1536]{2,1,0:T(8,128)(2,1)}, u32[]{:S(2)}, u32[]{:S(2)}) async-start(bf16[32,16,1536]{2,1,0:T(8,128)(2,1)} %bitcast.22), calls=%async_computation.1 | async-start | bytes 3145728 | tf_op jit(solution)/shard_map/all_to_all | solution.py:169
  131.8 1.4 slice-start
  177.6 4.3 %copy-start.2 = (bf16[4,128,1536]{2,1,0:T(8,128)(2,1)S(1)}, bf16[4,128,1536]{2,1,0:T(8,128)(2,1)}, u32[]{:S(2)}) copy-start(bf16[4,128,1536]{2,1,0:T(8,128)(2,1)} %reshape.210) | copy-start | bytes 4718596
  185.1 11.1 %copy-start.8 = (f32[32,8]{0,1:T(8,128)S(1)}, f32[32,8]{0,1:T(8,128)}, u32[]{:S(2)}) copy-start(f32[32,8]{0,1:T(8,128)} %param.21) | copy-start | bytes 3076
  185.1 54.7 %all-to-all-start.2 = ((bf16[32,16,1536]{2,1,0:T(8,128)(2,1)}), bf16[32,16,1536]{2,1,0:T(8,128)(2,1)S(1)}, u32[]{:S(2)}, u32[]{:S(2)}) async-start(bf16[32,16,1536]{2,1,0:T(8,128)(2,1)} %bitcast.81), calls=%async_computation.2 | async-start | bytes 3145728 | tf_op jit(solution)/shard_map/all_to_all | solution.py:177
Sparse Core Ops, SparseCore 0:
  29.7 81.0 all-gather.1

commit v4 on v2

--- a/solution.py
+++ b/solution.py
@@ -110,6 +110,9 @@
     whole_both = lax.all_to_all(
         jnp.broadcast_to(prefix_both[None], (seq_total,) + prefix_both.shape), SEQ, 0, 0, tiled=True
     ).reshape(prefix_len, prefix_both.shape[1])
+    full_in = group_gather(expert_in)
+    full_out = group_gather(expert_out)
+    whole_both, full_in, full_out = lax.optimization_barrier((whole_both, full_in, full_out))
     kv_cols = cached_prefix_keys.shape[1]
     whole_keys = whole_both[:, :kv_cols]
     whole_values = whole_both[:, kv_cols:]
@@ -170,8 +173,6 @@
     outgoing = gathered.reshape(experts, capacity, column_list)
     incoming = lax.all_to_all(outgoing, EXPERT_AXES, split_axis=0, concat_axis=0, tiled=True)
     incoming = incoming.reshape(experts * capacity, column_list)
-    full_in = group_gather(expert_in)
-    full_out = group_gather(expert_out)
     gate_up = jnp.einsum("rd,pdf->prf", incoming, full_in, preferred_element_type=jnp.float32)
     activated = (jax.nn.silu(gate_up[..., :ff_part]) * gate_up[..., ff_part:]).astype(jnp.bfloat16)
     partial_value = jnp.einsum(

time: 259 us -> 274 us (1.058); the launches traced: 255 us -> 273 us
  blocking collectives: 0 us -> 52.8 us
  waiting for transfers between devices: 155 us -> 122 us
  other arithmetic: 5.58 us -> 13.1 us
  starting transfers between devices: 61.5 us -> 54.2 us
    all_to_all x0 -> x1, blocking collectives: none -> 52.8 us  [body(): lax.all_to_all(outgoing, EXPERT_AXES, split_axis=0, concat_axis=0, tiled=...]
    all_to_all x1, waiting for transfers between devices: 48.7 us -> 0.01 us  [body(): lax.all_to_all(jnp.broadcast_to(prefix_both[None], (seq_total,) + prefix_...]
    all_to_all x1, waiting for transfers between devices: 39.1 us -> 50.6 us  [body(): lax.all_to_all(part_total.reshape(experts, capacity, column_list), EXPERT...]
    all_to_all x1 -> x0, starting transfers between devices: 7.2 us -> none  [body(): lax.all_to_all(outgoing, EXPERT_AXES, split_axis=0, concat_axis=0, tiled=...]
    concatenate x0 -> x2, other arithmetic: none -> 5.63 us  [group_gather(): return jnp.concatenate(pieces, axis=0)]
    ppermute x6, waiting for transfers between devices: 63.8 us -> 67.7 us  [group_gather(): pieces.append(lax.ppermute(local, PART_AXES, ring))]
    ppermute x6, starting transfers between devices: 15.2 us -> 18.1 us  [group_gather(): pieces.append(lax.ppermute(local, PART_AXES, ring))]
    all_to_all x1, starting transfers between devices: 10.7 us -> 7.84 us  [body(): lax.all_to_all(part_total.reshape(experts, capacity, column_list), EXPERT...]
  transfers between devices with their start and end apart: 12 -> 11, of which waited for: 8 -> 5; matrix products, arithmetic and copies ran while one was open for 4% -> 7% of each run, Pallas kernels for 0% -> 0%
where the time goes in v4:
time: 274 us; the launch traced here: 273 us
  waiting for transfers between devices  122 us (45%)
  starting transfers between devices  54.2 us (20%)
  blocking collectives  52.8 us (19%)
  matrix products  18.6 us (7%)
  other arithmetic  13.1 us (5%)
  local copies, waits for them, and re-layouts  10.9 us (4%)
    ppermute x6, waiting for transfers between devices, group_gather(): pieces.append(lax.ppermute(local, PART_AXES, ring))  67.7 us
    all_to_all x1, blocking collectives, body(): lax.all_to_all(outgoing, EXPERT_AXES, split_axis=0, concat_axis=0, tiled=...  52.8 us
    all_to_all x1, waiting for transfers between devices, body(): lax.all_to_all(part_total.reshape(experts, capacity, column_list), EXPERT...  50.6 us
    all_to_all x1, starting transfers between devices, body(): lax.all_to_all(jnp.broadcast_to(prefix_both[None], (seq_total,) + prefix_...  18.5 us
    ppermute x6, starting transfers between devices, group_gather(): pieces.append(lax.ppermute(local, PART_AXES, ring))  18.1 us
    ppermute x3, starting transfers between devices, body(): attn_sum = attn_sum + lax.ppermute(sent, 'tp', ring)  9.76 us
    all_to_all x1, starting transfers between devices, body(): lax.all_to_all(part_total.reshape(experts, capacity, column_list), EXPERT...  7.84 us
    concatenate x2, other arithmetic, group_gather(): return jnp.concatenate(pieces, axis=0)  5.63 us
  transfers between devices with their start and end apart: 11, of which 5 were waited for; matrix products, arithmetic and copies ran while one was open for 7% of the time, Pallas kernels for 0%

profile of v4, /device:TPU:6, one launch (start us, length us, event | category | flops | bytes accessed | tf_op | source)
XLA Modules:
  0.0 272.7 jit_solution(3878558291810890478)
XLA Ops:
  1.5 1.6 broadcast_in_dim.35
  3.1 18.5 %all-to-all-start = ((bf16[128,32,256]{2,1,0:T(8,128)(2,1)}), bf16[128,32,256]{2,1,0:T(8,128)(2,1)}, u32[]{:S(2)}, u32[]{:S(2)}) async-start(bf16[128,32,256]{2,1,0:T(8,128)(2,1)} %broadcast_in_dim.35), calls=%async_computation | async-start | bytes 4194304 | tf_op jit(solution)/shard_map/all_to_all | solution.py:110
  21.6 2.7 collective-permute-start.2
  24.3 2.3 collective-permute-start.1
  26.6 2.0 collective-permute-start
  28.6 3.5 %collective-permute-start.5 = (bf16[1,128,1536]{2,1,0:T(8,128)(2,1)}, bf16[1,128,1536]{2,1,0:T(8,128)(2,1)}, u32[]{:S(2)}, u32[]{:S(2)}) collective-permute-start(bf16[1,128,1536]{2,1,0:T(8,128)(2,1)} %param.23), channel_id=1, source_target_pairs={{0,12},{4,0},{8,4},{12,8},{1,13},{5,1},{9,5},{13,9},{2,14},{6,2},{... | collective-permute-start | bytes 1179656 | tf_op jit(solution)/shard_map/ppermute | solution.py:44
  32.2 3.5 %collective-permute-start.4 = (bf16[1,128,1536]{2,1,0:T(8,128)(2,1)}, bf16[1,128,1536]{2,1,0:T(8,128)(2,1)}, u32[]{:S(2)}, u32[]{:S(2)}) collective-permute-start(bf16[1,128,1536]{2,1,0:T(8,128)(2,1)} %param.23), channel_id=1, source_target_pairs={{0,8},{4,12},{8,0},{12,4},{1,9},{5,13},{9,1},{13,5},{2,10},{6,14},... | collective-permute-start | bytes 1179656 | tf_op jit(solution)/shard_map/ppermute | solution.py:44
  36.2 1.3 fusion.37
  39.7 1.6 fusion.41
  41.5 66.0 %collective-permute-done.5 = bf16[1,128,1536]{2,1,0:T(8,128)(2,1)} collective-permute-done((bf16[1,128,1536]{2,1,0:T(8,128)(2,1)}, bf16[1,128,1536]{2,1,0:T(8,128)(2,1)}, u32[]{:S(2)}, u32[]{:S(2)}) %collective-permute-start.5) | collective-permute-done | bytes 393248 | tf_op jit(solution)/shard_map/ppermute | solution.py:44
  107.6 4.0 %collective-permute-start.3 = (bf16[1,128,1536]{2,1,0:T(8,128)(2,1)}, bf16[1,128,1536]{2,1,0:T(8,128)(2,1)S(1)}, u32[]{:S(2)}, u32[]{:S(2)}) collective-permute-start(bf16[1,128,1536]{2,1,0:T(8,128)(2,1)} %param.23), channel_id=1, source_target_pairs={{0,4},{4,8},{8,12},{12,0},{1,5},{5,9},{9,13},{13,1},{2,6},{6,10},{... | collective-permute-start | bytes 1179656 | tf_op jit(solution)/shard_map/ppermute | solution.py:44
  114.4 2.0 convolution_convert_fusion.1
  116.4 1.6 collective-permute-done.3
  118.0 2.5 pad_maximum_fusion.1
  120.6 3.1 %pad_maximum_fusion = bf16[4,1536,256]{2,1,0:T(8,128)(2,1)} fusion(bf16[1,1536,256]{2,1,0:T(8,128)(2,1)} %collective-permute-done.2, bf16[1,1536,256]{2,1,0:T(8,128)(2,1)} %collective-permute-done.1, bf16[1,1536,256]{2,1,0:T(8,128)(2,1)} %collective-permute-done, bf16[1,1536,256]{2,1,0:T(8,128)(2,1)S(1)} %copy-done.5), kind=kLoop, calls=%fused_computation.7 | loop fusion | flops 4718592 | bytes 6291456 | tf_op jit(solution)/shard_map/concatenate | solution.py:45
  123.6 3.0 %fusion.40 = (bf16[4096,128]{1,0:T(8,128)(2,1)}, bf16[4096,128]{1,0:T(8,128)(2,1)}) fusion(bf16[4096,256]{1,0:T(8,128)(2,1)} %bitcast.12), kind=kLoop, calls=%fused_computation.78 | loop fusion | bytes 4194304 | tf_op jit(solution)/shard_map/slice | solution.py:117
  126.7 1.5 copy.50
  128.2 2.3 copy.49
  130.5 3.1 %bitcast_reduce_fusion = (f32[128,2,3]{0,2,1:T(4,128)S(1)}, f32[2,4096,128,3]{2,1,3,0:T(8,128)S(1)}) fusion(bf16[4096,2,64,1]{0,2,3,1:T(8,128)(2,1)} %bitcast.82, bf16[128,2,3,32]{0,3,2,1:T(8,128)(2,1)S(1)} %bitcast.90, bf16[128,2,3,32]{0,3,2,1:T(8,128)(2,1)S(1)} %bitcast.88), kind=kOutput, calls=%fused_computation.1 | convolution fusion | flops 409140480 | bytes 13732864 | tf_op jit(solution)/shard_map/tkgd,pkd->tkgp/dot_general | solution.py:123
  133.6 2.0 fusion.1
  135.6 2.3 fusion.10
  138.6 2.7 %collective-permute-start.8 = (f32[32,1536]{1,0:T(8,128)S(1)}, f32[32,1536]{1,0:T(8,128)S(1)}, u32[]{:S(2)}, u32[]{:S(2)}) collective-permute-start(f32[32,1536]{1,0:T(8,128)S(1)} %get-tuple-element.16), channel_id=1, source_target_pairs={{0,3},{1,0},{2,1},{3,2},{4,7},{5,4},{6,5},{7,6},{8,11},{9,8},{10,9... | collective-permute-start | bytes 589832 | tf_op jit(solution)/shard_map/ppermute | solution.py:152
  141.4 3.0 %collective-permute-start.7 = (f32[32,1536]{1,0:T(8,128)S(1)}, f32[32,1536]{1,0:T(8,128)S(1)}, u32[]{:S(2)}, u32[]{:S(2)}) collective-permute-start(f32[32,1536]{1,0:T(8,128)S(1)} %get-tuple-element.17), channel_id=1, source_target_pairs={{0,2},{1,3},{2,0},{3,1},{4,6},{5,7},{6,4},{7,5},{8,10},{9,11},{10,... | collective-permute-start | bytes 589832 | tf_op jit(solution)/shard_map/ppermute | solution.py:152
  144.4 4.0 %collective-permute-start.6 = (f32[32,1536]{1,0:T(8,128)S(1)}, f32[32,1536]{1,0:T(8,128)S(1)}, u32[]{:S(2)}, u32[]{:S(2)}) collective-permute-start(f32[32,1536]{1,0:T(8,128)S(1)} %get-tuple-element.15), channel_id=1, source_target_pairs={{0,1},{1,2},{2,3},{3,0},{4,5},{5,6},{6,7},{7,4},{8,9},{9,10},{10,1... | collective-permute-start | bytes 589832 | tf_op jit(solution)/shard_map/ppermute | solution.py:152
  150.0 1.6 collective-permute-done.8
  151.6 2.1 collective-permute-done.6
  154.5 52.8 %all_to_all.15 = bf16[32,16,1536]{2,1,0:T(8,128)(2,1)S(1)} all-to-all(bf16[32,16,1536]{2,1,0:T(8,128)(2,1)S(1)} %bitcast.80), channel_id=1, replica_groups=mesh['z'=8,'yh'=4,'yl'=2,'c'=2,'tp'=4] {'z','yh'}, dimensions={0} | all-to-all | bytes 3145728 | tf_op jit(solution)/shard_map/all_to_all | solution.py:174
  207.4 1.8 convolution_bitcast_fusion
  209.2 3.2 %convert_reduce_fusion = bf16[512,1536]{1,0:T(8,128)(2,1)} fusion(bf16[4,128,1536]{2,1,0:T(8,128)(2,1)S(1)} %copy-done.3, f32[4,512,256]{1,2,0:T(8,128)S(1)} %convolution_bitcast_fusion), kind=kOutput, calls=%fused_computation.5 | convolution fusion | flops 812384256 | bytes 5242880 | tf_op jit(solution)/shard_map/prf,pfd->prd/dot_general | solution.py:178
  212.4 7.8 %all-to-all-start.2 = ((bf16[32,16,1536]{2,1,0:T(8,128)(2,1)}), bf16[32,16,1536]{2,1,0:T(8,128)(2,1)S(1)}, u32[]{:S(2)}, u32[]{:S(2)}) async-start(bf16[32,16,1536]{2,1,0:T(8,128)(2,1)} %bitcast.83), calls=%async_computation.2 | async-start | bytes 3145728 | tf_op jit(solution)/shard_map/all_to_all | solution.py:182
  220.5 50.6 %all-to-all-done.2 = bf16[32,16,1536]{2,1,0:T(8,128)(2,1)S(1)} async-done(((bf16[32,16,1536]{2,1,0:T(8,128)(2,1)}), bf16[32,16,1536]{2,1,0:T(8,128)(2,1)S(1)}, u32[]{:S(2)}, u32[]{:S(2)}) %all-to-all-start.2) | async-done | bytes 1572896 | tf_op jit(solution)/shard_map/all_to_all | solution.py:182
  271.2 1.5 add_convert_fusion
  (75 shorter events, 9.8 us)
Async XLA Ops:
  0.6 137.5 %copy-start = (bf16[384,1536]{1,0:T(8,128)(2,1)S(1)}, bf16[384,1536]{1,0:T(8,128)(2,1)}, u32[]{:S(2)}) copy-start(bf16[384,1536]{1,0:T(8,128)(2,1)} %param.16) | copy-start | bytes 3538948
  3.1 18.5 %copy-start.5 = (bf16[1,1536,256]{2,1,0:T(8,128)(2,1)S(1)}, bf16[1,1536,256]{2,1,0:T(8,128)(2,1)}, u32[]{:S(2)}) copy-start(bf16[1,1536,256]{2,1,0:T(8,128)(2,1)} %param.22) | copy-start | bytes 2359300
  3.1 32.7 %copy-start.18 = (s32[1,128]{1,0:T(1,128)S(1)}, s32[1,128]{1,0:T(1,128)}, u32[]{:S(2)}) copy-start(s32[1,128]{1,0:T(1,128)} %param.19) | copy-start | bytes 1540
  3.1 32.8 %copy-start.1 = (bf16[128,1536]{1,0:T(8,128)(2,1)S(1)}, bf16[128,1536]{1,0:T(8,128)(2,1)}, u32[]{:S(2)}) copy-start(bf16[128,1536]{1,0:T(8,128)(2,1)} %param.12) | copy-start | bytes 1179652
  3.1 35.1 %copy-start.4 = (bf16[1536,384]{1,0:T(8,128)(2,1)S(1)}, bf16[1536,384]{1,0:T(8,128)(2,1)}, u32[]{:S(2)}) copy-start(bf16[1536,384]{1,0:T(8,128)(2,1)} %param.13) | copy-start | bytes 3538948
  3.1 120.5 %all-to-all-start = ((bf16[128,32,256]{2,1,0:T(8,128)(2,1)}), bf16[128,32,256]{2,1,0:T(8,128)(2,1)}, u32[]{:S(2)}, u32[]{:S(2)}) async-start(bf16[128,32,256]{2,1,0:T(8,128)(2,1)} %broadcast_in_dim.35), calls=%async_computation | async-start | bytes 4194304 | tf_op jit(solution)/shard_map/all_to_all | solution.py:110
  21.6 98.9 %collective-permute-start.2 = (bf16[1,1536,256]{2,1,0:T(8,128)(2,1)S(1)}, bf16[1,1536,256]{2,1,0:T(8,128)(2,1)}, u32[]{:S(2)}, u32[]{:S(2)}) collective-permute-start(bf16[1,1536,256]{2,1,0:T(8,128)(2,1)S(1)} %copy-done.5), channel_id=1, source_target_pairs={{0,12},{4,0},{8,4},{12,8},{1,13},{5,1},{9,5},{13,9},{2,14},{6,2},{... | collective-permute-start | bytes 2359304 | tf_op jit(solution)/shard_map/ppermute | solution.py:44
  24.3 96.2 %collective-permute-start.1 = (bf16[1,1536,256]{2,1,0:T(8,128)(2,1)S(1)}, bf16[1,1536,256]{2,1,0:T(8,128)(2,1)}, u32[]{:S(2)}, u32[]{:S(2)}) collective-permute-start(bf16[1,1536,256]{2,1,0:T(8,128)(2,1)S(1)} %copy-done.5), channel_id=1, source_target_pairs={{0,8},{4,12},{8,0},{12,4},{1,9},{5,13},{9,1},{13,5},{2,10},{6,14},... | collective-permute-start | bytes 2359304 | tf_op jit(solution)/shard_map/ppermute | solution.py:44
  26.6 93.9 %collective-permute-start = (bf16[1,1536,256]{2,1,0:T(8,128)(2,1)S(1)}, bf16[1,1536,256]{2,1,0:T(8,128)(2,1)}, u32[]{:S(2)}, u32[]{:S(2)}) collective-permute-start(bf16[1,1536,256]{2,1,0:T(8,128)(2,1)S(1)} %copy-done.5), channel_id=1, source_target_pairs={{0,4},{4,8},{8,12},{12,0},{1,5},{5,9},{9,13},{13,1},{2,6},{6,10},{... | collective-permute-start | bytes 2359304 | tf_op jit(solution)/shard_map/ppermute | solution.py:44
  28.6 78.9 %collective-permute-start.5 = (bf16[1,128,1536]{2,1,0:T(8,128)(2,1)}, bf16[1,128,1536]{2,1,0:T(8,128)(2,1)}, u32[]{:S(2)}, u32[]{:S(2)}) collective-permute-start(bf16[1,128,1536]{2,1,0:T(8,128)(2,1)} %param.23), channel_id=1, source_target_pairs={{0,12},{4,0},{8,4},{12,8},{1,13},{5,1},{9,5},{13,9},{2,14},{6,2},{... | collective-permute-start | bytes 1179656 | tf_op jit(solution)/shard_map/ppermute | solution.py:44
  32.2 84.2 %collective-permute-start.4 = (bf16[1,128,1536]{2,1,0:T(8,128)(2,1)}, bf16[1,128,1536]{2,1,0:T(8,128)(2,1)}, u32[]{:S(2)}, u32[]{:S(2)}) collective-permute-start(bf16[1,128,1536]{2,1,0:T(8,128)(2,1)} %param.23), channel_id=1, source_target_pairs={{0,8},{4,12},{8,0},{12,4},{1,9},{5,13},{9,1},{13,5},{2,10},{6,14},... | collective-permute-start | bytes 1179656 | tf_op jit(solution)/shard_map/ppermute | solution.py:44
  36.0 2.8 %copy-start.16 = (f32[128]{0:T(128)}, f32[128]{0:T(128)S(1)}, u32[]{:S(2)}) copy-start(f32[128]{0:T(128)S(1)} %add_rsqrt_fusion.1) | copy-start | bytes 1540
  38.8 79.2 %copy-start.6 = (bf16[1,128,1536]{2,1,0:T(8,128)(2,1)S(1)}, bf16[1,128,1536]{2,1,0:T(8,128)(2,1)}, u32[]{:S(2)}) copy-start(bf16[1,128,1536]{2,1,0:T(8,128)(2,1)} %param.23) | copy-start | bytes 1179652
  38.9 2.7 copy-start.9
  38.9 2.7 copy-start.11
  41.3 79.2 %copy-start.7 = (f32[128,2,3,128]{0,3,2,1:T(8,128)}, f32[128,2,3,128]{0,3,2,1:T(8,128)S(1)}, u32[]{:S(2)}) copy-start(f32[128,2,3,128]{0,3,2,1:T(8,128)S(1)} %get-tuple-element.28) | copy-start | bytes 1179652
  107.6 10.4 %collective-permute-start.3 = (bf16[1,128,1536]{2,1,0:T(8,128)(2,1)}, bf16[1,128,1536]{2,1,0:T(8,128)(2,1)S(1)}, u32[]{:S(2)}, u32[]{:S(2)}) collective-permute-start(bf16[1,128,1536]{2,1,0:T(8,128)(2,1)} %param.23), channel_id=1, source_target_pairs={{0,4},{4,8},{8,12},{12,0},{1,5},{5,9},{9,13},{13,1},{2,6},{6,10},{... | collective-permute-start | bytes 1179656 | tf_op jit(solution)/shard_map/ppermute | solution.py:44
  126.7 3.8 %copy-start.10 = (bf16[128,6,32]{0,2,1:T(8,128)(2,1)S(1)}, bf16[128,6,32]{0,2,1:T(8,128)(2,1)}, u32[]{:S(2)}) copy-start(bf16[128,6,32]{0,2,1:T(8,128)(2,1)} %copy-done.9) | copy-start | bytes 147460
  126.7 3.8 %copy-start.12 = (bf16[128,6,32]{0,2,1:T(8,128)(2,1)S(1)}, bf16[128,6,32]{0,2,1:T(8,128)(2,1)}, u32[]{:S(2)}) copy-start(bf16[128,6,32]{0,2,1:T(8,128)(2,1)} %copy-done.11) | copy-start | bytes 147460
  130.5 3.1 %copy-start.13 = (f32[128,2,3]{0,2,1:T(4,128)S(1)}, f32[128,2,3]{0,2,1:T(4,128)}, u32[]{:S(2)}) copy-start(f32[128,2,3]{0,2,1:T(4,128)} %get-tuple-element.27) | copy-start | bytes 9220
  135.6 2.3 copy-start.8
  135.6 2.3 copy-start.14
  137.9 10.5 %copy-start.15 = (s32[32,8]{0,1:T(8,128)S(1)}, s32[32,8]{0,1:T(8,128)}, u32[]{:S(2)}) copy-start(s32[32,8]{0,1:T(8,128)} %param.20) | copy-start | bytes 3076
  138.6 13.0 %collective-permute-start.8 = (f32[32,1536]{1,0:T(8,128)S(1)}, f32[32,1536]{1,0:T(8,128)S(1)}, u32[]{:S(2)}, u32[]{:S(2)}) collective-permute-start(f32[32,1536]{1,0:T(8,128)S(1)} %get-tuple-element.16), channel_id=1, source_target_pairs={{0,3},{1,0},{2,1},{3,2},{4,7},{5,4},{6,5},{7,6},{8,11},{9,8},{10,9... | collective-permute-start | bytes 589832 | tf_op jit(solution)/shard_map/ppermute | solution.py:152
  141.4 10.2 %collective-permute-start.7 = (f32[32,1536]{1,0:T(8,128)S(1)}, f32[32,1536]{1,0:T(8,128)S(1)}, u32[]{:S(2)}, u32[]{:S(2)}) collective-permute-start(f32[32,1536]{1,0:T(8,128)S(1)} %get-tuple-element.17), channel_id=1, source_target_pairs={{0,2},{1,3},{2,0},{3,1},{4,6},{5,7},{6,4},{7,5},{8,10},{9,11},{10,... | collective-permute-start | bytes 589832 | tf_op jit(solution)/shard_map/ppermute | solution.py:152
  144.4 9.3 %collective-permute-start.6 = (f32[32,1536]{1,0:T(8,128)S(1)}, f32[32,1536]{1,0:T(8,128)S(1)}, u32[]{:S(2)}, u32[]{:S(2)}) collective-permute-start(f32[32,1536]{1,0:T(8,128)S(1)} %get-tuple-element.15), channel_id=1, source_target_pairs={{0,1},{1,2},{2,3},{3,0},{4,5},{5,6},{6,7},{7,4},{8,9},{9,10},{10,1... | collective-permute-start | bytes 589832 | tf_op jit(solution)/shard_map/ppermute | solution.py:152
  153.9 53.5 %copy-start.2 = (bf16[4,1536,256]{2,1,0:T(8,128)(2,1)S(1)}, bf16[4,1536,256]{2,1,0:T(8,128)(2,1)}, u32[]{:S(2)}) copy-start(bf16[4,1536,256]{2,1,0:T(8,128)(2,1)} %pad_maximum_fusion) | copy-start | bytes 9437188
  207.4 1.8 copy-start.3
  212.4 7.9 %copy-start.17 = (f32[32,8]{0,1:T(8,128)S(1)}, f32[32,8]{0,1:T(8,128)}, u32[]{:S(2)}) copy-start(f32[32,8]{0,1:T(8,128)} %param.21) | copy-start | bytes 3076
  212.4 58.8 %all-to-all-start.2 = ((bf16[32,16,1536]{2,1,0:T(8,128)(2,1)}), bf16[32,16,1536]{2,1,0:T(8,128)(2,1)S(1)}, u32[]{:S(2)}, u32[]{:S(2)}) async-start(bf16[32,16,1536]{2,1,0:T(8,128)(2,1)} %bitcast.83), calls=%async_computation.2 | async-start | bytes 3145728 | tf_op jit(solution)/shard_map/all_to_all | solution.py:182

commit v5 on v3

--- a/solution.py
+++ b/solution.py
@@ -137,14 +137,11 @@
     moe_rows = routes.shape[0]
     row_start = lax.axis_index("tp") * moe_rows
     attn_part = jnp.dot(attended, w_out, preferred_element_type=jnp.float32)
-    tp_index = lax.axis_index("tp")
     tp_count = lax.axis_size("tp")
-    attn_sum = lax.dynamic_slice_in_dim(attn_part, row_start, moe_rows, 0)
-    for shift in range(1, tp_count):
-        target = (tp_index + shift) % tp_count
-        sent = lax.dynamic_slice_in_dim(attn_part, target * moe_rows, moe_rows, 0)
-        ring = [(i, (i + shift) % tp_count) for i in range(tp_count)]
-        attn_sum = attn_sum + lax.ppermute(sent, "tp", ring)
+    exchanged = lax.all_to_all(
+        attn_part.reshape(tp_count, moe_rows, column_list), "tp", 0, 0, tiled=True
+    )
+    attn_sum = jnp.sum(exchanged, axis=0)
     residual = (
         lax.dynamic_slice_in_dim(hidden_in, row_start, moe_rows, 0).astype(jnp.float32)
         + RESIDUAL * attn_sum

time: 249 us -> 247 us (level)
  the two profiles are of different devices: /device:TPU:80 before, /device:TPU:6 now
where the time goes in v5:
time: 247 us; the launch traced here: 243 us
  waiting for transfers between devices  152 us (62%)
  starting transfers between devices  35.8 us (14%)
  matrix products  19.3 us (8%)
  between operations  14.4 us (6%)
  local copies, waits for them, and re-layouts  13.9 us (6%)
  other arithmetic  7.39 us (3%)
    all_to_all x1, waiting for transfers between devices, body(): lax.all_to_all(jnp.broadcast_to(prefix_both[None], (seq_total,) + prefix_...  57.2 us
    all_to_all x1, waiting for transfers between devices, body(): lax.all_to_all(outgoing, EXPERT_AXES, split_axis=0, concat_axis=0, tiled=...  48.5 us
    all_to_all x1, waiting for transfers between devices, body(): lax.all_to_all(part_total.reshape(experts, capacity, column_list), EXPERT...  38.7 us
    all_to_all x1, starting transfers between devices, body(): lax.all_to_all(jnp.broadcast_to(prefix_both[None], (seq_total,) + prefix_...  18.5 us
    all_to_all x1, starting transfers between devices, body(): lax.all_to_all(outgoing, EXPERT_AXES, split_axis=0, concat_axis=0, tiled=...  7.81 us
    all_to_all x1, waiting for transfers between devices, body(): lax.all_to_all(attn_part.reshape(tp_count, moe_rows, column_list), 'tp',...  7.52 us
    slice x2, local copies, waits for them, and re-layouts, body(): whole_keys = whole_both[:, :kv_cols]  5.43 us
  transfers between devices with their start and end apart: 5, of which 4 were waited for; matrix products, arithmetic and copies ran while one was open for 11% of the time, Pallas kernels for 0%

profile of v5, /device:TPU:6, one launch (start us, length us, event | category | flops | bytes accessed | tf_op | source)
XLA Modules:
  0.0 242.5 jit_solution(3994952502707024811)
XLA Ops:
  7.2 0.8 pad_maximum_fusion.4
  8.0 1.7 broadcast_in_dim.35
  9.7 18.5 %all-to-all-start = ((bf16[128,32,256]{2,1,0:T(8,128)(2,1)}), bf16[128,32,256]{2,1,0:T(8,128)(2,1)}, u32[]{:S(2)}, u32[]{:S(2)}) async-start(bf16[128,32,256]{2,1,0:T(8,128)(2,1)} %broadcast_in_dim.35), calls=%async_computation | async-start | bytes 4194304 | tf_op jit(solution)/shard_map/all_to_all | solution.py:108
  28.2 0.5 reshape.207
  28.7 2.4 pad_maximum_fusion
  31.7 0.3 fusion.44
  32.1 0.6 fusion.42
  32.7 0.3 fusion.48
  33.1 0.4 convolution_convert_fusion.1
  33.4 57.2 %all-to-all-done = bf16[128,32,256]{2,1,0:T(8,128)(2,1)} async-done(((bf16[128,32,256]{2,1,0:T(8,128)(2,1)}), bf16[128,32,256]{2,1,0:T(8,128)(2,1)}, u32[]{:S(2)}, u32[]{:S(2)}) %all-to-all-start) | async-done | bytes 2097184 | tf_op jit(solution)/shard_map/all_to_all | solution.py:108
  90.6 3.1 %fusion.47 = (bf16[4096,128]{1,0:T(8,128)(2,1)}, bf16[4096,128]{1,0:T(8,128)(2,1)}) fusion(bf16[4096,256]{1,0:T(8,128)(2,1)} %bitcast.12), kind=kLoop, calls=%fused_computation.77 | loop fusion | bytes 4194304 | tf_op jit(solution)/shard_map/slice | solution.py:112
  93.7 1.5 copy.66
  95.2 2.3 copy.65
  97.5 3.1 %bitcast_reduce_fusion = (f32[128,2,3]{0,2,1:T(4,128)S(1)}, f32[2,4096,128,3]{2,1,3,0:T(8,128)S(1)}) fusion(bf16[4096,2,64,1]{0,2,3,1:T(8,128)(2,1)} %bitcast.81, bf16[128,2,3,32]{0,3,2,1:T(8,128)(2,1)S(1)} %bitcast.88, bf16[128,2,3,32]{0,3,2,1:T(8,128)(2,1)S(1)} %bitcast.86), kind=kOutput, calls=%fused_computation.1 | convolution fusion | flops 409140480 | bytes 13732864 | tf_op jit(solution)/shard_map/tkgd,pkd->tkgp/dot_general | solution.py:118
  100.6 2.0 fusion.1
  102.7 2.3 fusion.17
  105.4 0.2 dot_general.45
  105.6 1.3 fusion.12
  106.9 4.8 %all-to-all-start.1 = ((f32[4,32,1536]{2,1,0:T(8,128)}), f32[4,32,1536]{2,1,0:T(8,128)S(1)}, u32[]{:S(2)}, u32[]{:S(2)}) async-start(f32[4,32,1536]{2,1,0:T(8,128)} %fusion.12), calls=%async_computation.1 | async-start | bytes 1572864 | tf_op jit(solution)/shard_map/all_to_all | solution.py:141
  111.9 0.7 select_reduce_fusion.1
  112.7 0.2 fusion.26
  113.0 7.5 %all-to-all-done.1 = f32[4,32,1536]{2,1,0:T(8,128)S(1)} async-done(((f32[4,32,1536]{2,1,0:T(8,128)}), f32[4,32,1536]{2,1,0:T(8,128)S(1)}, u32[]{:S(2)}, u32[]{:S(2)}) %all-to-all-start.1) | async-done | bytes 786464 | tf_op jit(solution)/shard_map/all_to_all | solution.py:141
  120.7 1.9 convolution_convert_fusion
  122.6 7.8 %all-to-all-start.2 = ((bf16[32,16,1536]{2,1,0:T(8,128)(2,1)}), bf16[32,16,1536]{2,1,0:T(8,128)(2,1)}, u32[]{:S(2)}, u32[]{:S(2)}) async-start(bf16[32,16,1536]{2,1,0:T(8,128)(2,1)} %bitcast.22), calls=%async_computation.2 | async-start | bytes 3145728 | tf_op jit(solution)/shard_map/all_to_all | solution.py:166
  130.4 1.4 slice-done
  131.8 2.6 %reshape.210 = bf16[4,128,1536]{2,1,0:T(8,128)(2,1)} reshape(bf16[4,1536,128]{2,1,0:T(8,128)(2,1)S(1)} %slice-done) | data formatting | bytes 3145728 | tf_op jit(solution)/shard_map/reshape | solution.py:59
  134.5 48.5 %all-to-all-done.2 = bf16[32,16,1536]{2,1,0:T(8,128)(2,1)} async-done(((bf16[32,16,1536]{2,1,0:T(8,128)(2,1)}), bf16[32,16,1536]{2,1,0:T(8,128)(2,1)}, u32[]{:S(2)}, u32[]{:S(2)}) %all-to-all-start.2) | async-done | bytes 1572896 | tf_op jit(solution)/shard_map/all_to_all | solution.py:166
  182.9 4.3 %fusion.7 = f32[4,512,256]{1,2,0:T(8,128)S(1)} fusion(bf16[512,1536,1]{1,0,2:T(8,128)(2,1)} %bitcast.24, bf16[4,1536,384]{2,1,0:T(8,128)(2,1)} %all-gather.2.cloned.1.call-done), kind=kOutput, calls=%fused_computation.10 | convolution fusion | flops 1610612736 | bytes 6815744 | tf_op jit(solution)/shard_map/rd,pdf->prf/dot_general | solution.py:168
  187.3 3.1 %convert_reduce_fusion = bf16[512,1536]{1,0:T(8,128)(2,1)} fusion(bf16[4,128,1536]{2,1,0:T(8,128)(2,1)S(1)} %copy-done.2, f32[4,512,256]{1,2,0:T(8,128)S(1)} %fusion.7), kind=kOutput, calls=%fused_computation.5 | convolution fusion | flops 812384256 | bytes 5242880 | tf_op jit(solution)/shard_map/prf,pfd->prd/dot_general | solution.py:170
  190.4 4.7 %all-to-all-start.3 = ((bf16[32,16,1536]{2,1,0:T(8,128)(2,1)}), bf16[32,16,1536]{2,1,0:T(8,128)(2,1)S(1)}, u32[]{:S(2)}, u32[]{:S(2)}) async-start(bf16[32,16,1536]{2,1,0:T(8,128)(2,1)} %bitcast.82), calls=%async_computation.3 | async-start | bytes 3145728 | tf_op jit(solution)/shard_map/all_to_all | solution.py:174
  195.4 38.7 %all-to-all-done.3 = bf16[32,16,1536]{2,1,0:T(8,128)(2,1)S(1)} async-done(((bf16[32,16,1536]{2,1,0:T(8,128)(2,1)}), bf16[32,16,1536]{2,1,0:T(8,128)(2,1)S(1)}, u32[]{:S(2)}, u32[]{:S(2)}) %all-to-all-start.3) | async-done | bytes 1572896 | tf_op jit(solution)/shard_map/all_to_all | solution.py:174
  234.2 1.5 add_convert_fusion
  (50 shorter events, 2.1 us)
Async XLA Ops:
  7.2 98.4 %copy-start = (bf16[384,1536]{1,0:T(8,128)(2,1)S(1)}, bf16[384,1536]{1,0:T(8,128)(2,1)}, u32[]{:S(2)}) copy-start(bf16[384,1536]{1,0:T(8,128)(2,1)} %param.16) | copy-start | bytes 3538948
  9.6 18.6 %copy-start.4 = (bf16[1,128,1536]{2,1,0:T(8,128)(2,1)S(1)}, bf16[1,128,1536]{2,1,0:T(8,128)(2,1)}, u32[]{:S(2)}) copy-start(bf16[1,128,1536]{2,1,0:T(8,128)(2,1)} %param.23) | copy-start | bytes 1179652
  9.7 81.0 %all-to-all-start = ((bf16[128,32,256]{2,1,0:T(8,128)(2,1)}), bf16[128,32,256]{2,1,0:T(8,128)(2,1)}, u32[]{:S(2)}, u32[]{:S(2)}) async-start(bf16[128,32,256]{2,1,0:T(8,128)(2,1)} %broadcast_in_dim.35), calls=%async_computation | async-start | bytes 4194304 | tf_op jit(solution)/shard_map/all_to_all | solution.py:108
  28.1 3.0 %copy-start.9 = (s32[1,128]{1,0:T(1,128)S(1)}, s32[1,128]{1,0:T(1,128)}, u32[]{:S(2)}) copy-start(s32[1,128]{1,0:T(1,128)} %param.19) | copy-start | bytes 1540
  28.1 3.1 %copy-start.1 = (bf16[128,1536]{1,0:T(8,128)(2,1)S(1)}, bf16[128,1536]{1,0:T(8,128)(2,1)}, u32[]{:S(2)}) copy-start(bf16[128,1536]{1,0:T(8,128)(2,1)} %param.12) | copy-start | bytes 1179652
  28.2 102.3 %all-gather.2.cloned.1.call-start = ((), (), s32[]{:S(2)}) async-start(), calls=%async_computation.4 | async-start | bytes 5898240 | tf_op jit(solution)/shard_map/all_gather | solution.py:57
  28.7 3.0 %copy-start.5 = (bf16[1536,128]{1,0:T(8,128)(2,1)S(1)}, bf16[1536,128]{1,0:T(8,128)(2,1)}, u32[]{:S(2)}) copy-start(bf16[1536,128]{1,0:T(8,128)(2,1)} %param.14) | copy-start | bytes 1179652
  28.7 3.3 %copy-start.3 = (bf16[1536,384]{1,0:T(8,128)(2,1)S(1)}, bf16[1536,384]{1,0:T(8,128)(2,1)}, u32[]{:S(2)}) copy-start(bf16[1536,384]{1,0:T(8,128)(2,1)} %param.13) | copy-start | bytes 3538948
  31.4 1.7 copy-start.6
  105.2 6.5 %copy-start.7 = (s32[32,8]{0,1:T(8,128)S(1)}, s32[32,8]{0,1:T(8,128)}, u32[]{:S(2)}) copy-start(s32[32,8]{0,1:T(8,128)} %param.20) | copy-start | bytes 3076
  106.9 13.6 %all-to-all-start.1 = ((f32[4,32,1536]{2,1,0:T(8,128)}), f32[4,32,1536]{2,1,0:T(8,128)S(1)}, u32[]{:S(2)}, u32[]{:S(2)}) async-start(f32[4,32,1536]{2,1,0:T(8,128)} %fusion.12), calls=%async_computation.1 | async-start | bytes 1572864 | tf_op jit(solution)/shard_map/all_to_all | solution.py:141
  122.6 60.4 %all-to-all-start.2 = ((bf16[32,16,1536]{2,1,0:T(8,128)(2,1)}), bf16[32,16,1536]{2,1,0:T(8,128)(2,1)}, u32[]{:S(2)}, u32[]{:S(2)}) async-start(bf16[32,16,1536]{2,1,0:T(8,128)(2,1)} %bitcast.22), calls=%async_computation.2 | async-start | bytes 3145728 | tf_op jit(solution)/shard_map/all_to_all | solution.py:166
  130.4 1.4 slice-start
  182.9 4.3 %copy-start.2 = (bf16[4,128,1536]{2,1,0:T(8,128)(2,1)S(1)}, bf16[4,128,1536]{2,1,0:T(8,128)(2,1)}, u32[]{:S(2)}) copy-start(bf16[4,128,1536]{2,1,0:T(8,128)(2,1)} %reshape.210) | copy-start | bytes 4718596
  190.4 4.7 %copy-start.8 = (f32[32,8]{0,1:T(8,128)S(1)}, f32[32,8]{0,1:T(8,128)}, u32[]{:S(2)}) copy-start(f32[32,8]{0,1:T(8,128)} %param.21) | copy-start | bytes 3076
  190.4 43.8 %all-to-all-start.3 = ((bf16[32,16,1536]{2,1,0:T(8,128)(2,1)}), bf16[32,16,1536]{2,1,0:T(8,128)(2,1)S(1)}, u32[]{:S(2)}, u32[]{:S(2)}) async-start(bf16[32,16,1536]{2,1,0:T(8,128)(2,1)} %bitcast.82), calls=%async_computation.3 | async-start | bytes 3145728 | tf_op jit(solution)/shard_map/all_to_all | solution.py:174
Sparse Core Ops, SparseCore 0:
  31.2 80.6 all-gather.1

commit v6 on v5

--- a/solution.py
+++ b/solution.py
@@ -1,6 +1,7 @@
 import jax
 import jax.numpy as jnp
 from jax import lax
+from jax.experimental import pallas as pl
 from jax.sharding import Mesh, PartitionSpec as P
 
 HEAD_WIDTH = 64
@@ -34,6 +35,32 @@
         [first_half * cosine - second * sine_part, second * cosine + first_half * sine_part],
         axis=-1,
     )
+
+
+def prefix_attention(queries, keys_values, top_old, denom_old, numer_old, head_size):
+    kv_local = queries.shape[0]
+    value_base = keys_values.shape[1] // 2
+
+    def kernel(q_ref, kv_ref, top_ref, den_ref, num_ref, out_ref):
+        for head in range(kv_local):
+            keys = kv_ref[:, head * head_size : (head + 1) * head_size]
+            values = kv_ref[:, value_base + head * head_size : value_base + (head + 1) * head_size]
+            scores = lax.dot_general(
+                q_ref[head], keys, (((1,), (1,)), ((), ())), preferred_element_type=jnp.float32
+            ) * (1.0 / head_size)
+            top_prev = top_ref[head]
+            top_new = jnp.maximum(top_prev, jnp.max(scores, axis=1, keepdims=True))
+            shrink = jnp.exp(top_prev - top_new)
+            weights = jnp.exp(scores - top_new)
+            denom = den_ref[head] * shrink + jnp.sum(weights, axis=1, keepdims=True)
+            numer = num_ref[head] * shrink + jnp.dot(
+                weights.astype(jnp.bfloat16), values, preferred_element_type=jnp.float32
+            )
+            out_ref[head] = (numer / denom).astype(jnp.bfloat16)
+
+    return pl.pallas_call(
+        kernel, out_shape=jax.ShapeDtypeStruct(queries.shape, jnp.bfloat16)
+    )(queries, keys_values, top_old, denom_old, numer_old)
 
 
 def body(
@@ -108,32 +135,23 @@
     whole_both = lax.all_to_all(
         jnp.broadcast_to(prefix_both[None], (seq_total,) + prefix_both.shape), SEQ, 0, 0, tiled=True
     ).reshape(prefix_len, prefix_both.shape[1])
-    kv_cols = cached_prefix_keys.shape[1]
-    whole_keys = whole_both[:, :kv_cols]
-    whole_values = whole_both[:, kv_cols:]
     top_old, denom_old, numer_old = running
-    key_rows = whole_keys.reshape(-1, kv_local, head_size)
-    value_rows = whole_values.reshape(-1, kv_local, head_size)
-    scores = (
-        jnp.einsum("tkgd,pkd->tkgp", query_rows_all, key_rows, preferred_element_type=jnp.float32)
-        / head_size
-    )
-    top_new = jnp.maximum(top_old, jnp.max(scores, axis=-1))
-    shrink = jnp.exp(top_old - top_new)
-    part_weights = jnp.exp(scores - top_new[..., None])
-    denom_new = denom_old * shrink + jnp.sum(part_weights, axis=-1)
-    numer_new = numer_old * shrink[..., None] + jnp.einsum(
-        "tkgp,pkd->tkgd",
-        part_weights.astype(jnp.bfloat16),
-        value_rows,
-        preferred_element_type=jnp.float32,
-    )
-    running = (top_new, denom_new, numer_new)
-    attended = (
-        (running[2] / running[1][..., None])
-        .astype(jnp.bfloat16)
-        .reshape(rows_dev, kv_local * group_width * head_size)
-    )
+    rows_q = rows_dev * group_width
+
+    def heads_first(values):
+        return jnp.swapaxes(values, 0, 1).reshape((kv_local, rows_q) + values.shape[3:])
+
+    attended = prefix_attention(
+        heads_first(query_rows_all),
+        whole_both,
+        heads_first(top_old[..., None]),
+        heads_first(denom_old[..., None]),
+        heads_first(numer_old),
+        head_size,
+    )
+    attended = jnp.swapaxes(
+        attended.reshape(kv_local, rows_dev, group_width, head_size), 0, 1
+    ).reshape(rows_dev, kv_local * group_width * head_size)
     moe_rows = routes.shape[0]
     row_start = lax.axis_index("tp") * moe_rows
     attn_part = jnp.dot(attended, w_out, preferred_element_type=jnp.float32)

time: 247 us -> 249 us (level)
  the two profiles are of different devices: /device:TPU:6 before, /device:TPU:82 now
where the time goes in v6:
time: 249 us; the launch traced here: 248 us
  waiting for transfers between devices  161 us (65%)
  starting transfers between devices  35.2 us (14%)
  between operations  14.3 us (6%)
  matrix products  13.8 us (6%)
  local copies, waits for them, and re-layouts  12.4 us (5%)
  Pallas kernels  7.73 us (3%)
  other arithmetic  4.14 us (2%)
    all_to_all x1, waiting for transfers between devices, body(): lax.all_to_all(jnp.broadcast_to(prefix_both[None], (seq_total,) + prefix_...  55.2 us
    all_to_all x1, waiting for transfers between devices, body(): lax.all_to_all(part_total.reshape(experts, capacity, column_list), EXPERT...  51.7 us
    all_to_all x1, waiting for transfers between devices, body(): lax.all_to_all(outgoing, EXPERT_AXES, split_axis=0, concat_axis=0, tiled=...  45.6 us
    all_to_all x1, starting transfers between devices, body(): lax.all_to_all(jnp.broadcast_to(prefix_both[None], (seq_total,) + prefix_...  16.9 us
    all_to_all x1, waiting for transfers between devices, body(): lax.all_to_all(attn_part.reshape(tp_count, moe_rows, column_list), 'tp',...  8.18 us
    pallas_call x1, Pallas kernels, prefix_attention(): pl.pallas_call(kernel, out_shape=jax.ShapeDtypeStruct(queries.shape, jnp....  7.73 us
    all_to_all x1, starting transfers between devices, body(): lax.all_to_all(outgoing, EXPERT_AXES, split_axis=0, concat_axis=0, tiled=...  6.9 us
    all_to_all x1, starting transfers between devices, body(): lax.all_to_all(part_total.reshape(experts, capacity, column_list), EXPERT...  6.44 us
  transfers between devices with their start and end apart: 5, of which 4 were waited for; matrix products, arithmetic and copies ran while one was open for 7% of the time, Pallas kernels for 3%

profile of v6, /device:TPU:82, one launch (start us, length us, event | category | flops | bytes accessed | tf_op | source)
XLA Modules:
  0.0 248.3 jit_solution(2370802175171382518)
XLA Ops:
  7.2 0.8 pad_maximum_fusion.3
  8.0 1.7 broadcast_in_dim.42
  9.7 16.9 %all-to-all-start = ((bf16[128,32,256]{2,1,0:T(8,128)(2,1)}), bf16[128,32,256]{2,1,0:T(8,128)(2,1)}, u32[]{:S(2)}, u32[]{:S(2)}) async-start(bf16[128,32,256]{2,1,0:T(8,128)(2,1)} %broadcast_in_dim.42), calls=%async_computation | async-start | bytes 4194304 | tf_op jit(solution)/shard_map/all_to_all | solution.py:135
  26.7 0.5 reshape.198
  27.2 1.2 pad_maximum_fusion
  28.9 0.4 fusion.30
  29.3 0.3 copy-done.3
  29.7 0.6 fusion.32
  30.3 0.3 fusion.34
  30.6 0.4 convolution_convert_fusion.1
  31.2 0.3 copy.86
  31.4 0.8 copy.90.num_ref
  32.4 0.9 reshape.209.den_ref
  33.5 0.9 reshape.208.top_ref
  34.6 0.7 copy.87.q_ref
  35.3 55.2 %all-to-all-done = bf16[128,32,256]{2,1,0:T(8,128)(2,1)} async-done(((bf16[128,32,256]{2,1,0:T(8,128)(2,1)}), bf16[128,32,256]{2,1,0:T(8,128)(2,1)}, u32[]{:S(2)}, u32[]{:S(2)}) %all-to-all-start) | async-done | bytes 2097184 | tf_op jit(solution)/shard_map/all_to_all | solution.py:135
  90.5 7.7 %shard_map.139 = bf16[2,384,64]{2,1,0:T(8,128)(2,1)} custom-call(bf16[2,384,64]{2,1,0:T(8,128)(2,1)} %copy.87.q_ref, bf16[4096,256]{1,0:T(8,128)(2,1)} %bitcast.6.kv_ref, f32[2,384,1]{2,1,0:T(8,128)} %reshape.208.top_ref, f32[2,384,1]{2,1,0:T(8,128)} %reshape.209.den_ref, f32[2,384,64]{2,1,0:T(8,128)} %copy.90.num_ref), custom_call_target="tpu_custom_call" | custom-call | tf_op jit(solution)/shard_map/pallas_call | solution.py:61
  98.2 1.1 copy.91
  99.7 1.3 fusion.7
  101.0 4.8 %all-to-all-start.1 = ((f32[4,32,1536]{2,1,0:T(8,128)}), f32[4,32,1536]{2,1,0:T(8,128)S(1)}, u32[]{:S(2)}, u32[]{:S(2)}) async-start(f32[4,32,1536]{2,1,0:T(8,128)} %fusion.7), calls=%async_computation.1 | async-start | bytes 1572864 | tf_op jit(solution)/shard_map/all_to_all | solution.py:159
  106.1 0.7 select_reduce_fusion.1
  107.2 8.2 %all-to-all-done.1 = f32[4,32,1536]{2,1,0:T(8,128)S(1)} async-done(((f32[4,32,1536]{2,1,0:T(8,128)}), f32[4,32,1536]{2,1,0:T(8,128)S(1)}, u32[]{:S(2)}, u32[]{:S(2)}) %all-to-all-start.1) | async-done | bytes 786464 | tf_op jit(solution)/shard_map/all_to_all | solution.py:159
  115.5 1.8 convolution_convert_fusion
  117.3 6.9 %all-to-all-start.2 = ((bf16[32,16,1536]{2,1,0:T(8,128)(2,1)}), bf16[32,16,1536]{2,1,0:T(8,128)(2,1)}, u32[]{:S(2)}, u32[]{:S(2)}) async-start(bf16[32,16,1536]{2,1,0:T(8,128)(2,1)} %bitcast.22), calls=%async_computation.2 | async-start | bytes 3145728 | tf_op jit(solution)/shard_map/all_to_all | solution.py:184
  124.3 1.4 slice-done
  125.7 2.7 %reshape.201 = bf16[4,128,1536]{2,1,0:T(8,128)(2,1)} reshape(bf16[4,1536,128]{2,1,0:T(8,128)(2,1)S(1)} %slice-done) | data formatting | bytes 3145728 | tf_op jit(solution)/shard_map/reshape | solution.py:86
  128.4 45.6 %all-to-all-done.2 = bf16[32,16,1536]{2,1,0:T(8,128)(2,1)} async-done(((bf16[32,16,1536]{2,1,0:T(8,128)(2,1)}), bf16[32,16,1536]{2,1,0:T(8,128)(2,1)}, u32[]{:S(2)}, u32[]{:S(2)}) %all-to-all-start.2) | async-done | bytes 1572896 | tf_op jit(solution)/shard_map/all_to_all | solution.py:184
  174.0 4.3 %fusion.2 = f32[4,512,256]{1,2,0:T(8,128)S(1)} fusion(bf16[512,1536,1]{1,0,2:T(8,128)(2,1)} %bitcast.24, bf16[4,1536,384]{2,1,0:T(8,128)(2,1)} %all-gather.2.cloned.1.call-done), kind=kOutput, calls=%fused_computation.4 | convolution fusion | flops 1610612736 | bytes 6815744 | tf_op jit(solution)/shard_map/rd,pdf->prf/dot_general | solution.py:186
  178.3 3.1 %convert_reduce_fusion = bf16[512,1536]{1,0:T(8,128)(2,1)} fusion(bf16[4,128,1536]{2,1,0:T(8,128)(2,1)S(1)} %copy-done.2, f32[4,512,256]{1,2,0:T(8,128)S(1)} %fusion.2), kind=kOutput, calls=%fused_computation | convolution fusion | flops 812384256 | bytes 5242880 | tf_op jit(solution)/shard_map/prf,pfd->prd/dot_general | solution.py:188
  181.4 6.4 %all-to-all-start.3 = ((bf16[32,16,1536]{2,1,0:T(8,128)(2,1)}), bf16[32,16,1536]{2,1,0:T(8,128)(2,1)S(1)}, u32[]{:S(2)}, u32[]{:S(2)}) async-start(bf16[32,16,1536]{2,1,0:T(8,128)(2,1)} %bitcast.65), calls=%async_computation.3 | async-start | bytes 3145728 | tf_op jit(solution)/shard_map/all_to_all | solution.py:192
  188.2 51.7 %all-to-all-done.3 = bf16[32,16,1536]{2,1,0:T(8,128)(2,1)S(1)} async-done(((bf16[32,16,1536]{2,1,0:T(8,128)(2,1)}), bf16[32,16,1536]{2,1,0:T(8,128)(2,1)S(1)}, u32[]{:S(2)}, u32[]{:S(2)}) %all-to-all-start.3) | async-done | bytes 1572896 | tf_op jit(solution)/shard_map/all_to_all | solution.py:192
  239.9 1.5 add_convert_fusion
  (55 shorter events, 2.8 us)
Async XLA Ops:
  7.2 92.5 %copy-start = (bf16[384,1536]{1,0:T(8,128)(2,1)S(1)}, bf16[384,1536]{1,0:T(8,128)(2,1)}, u32[]{:S(2)}) copy-start(bf16[384,1536]{1,0:T(8,128)(2,1)} %param.16) | copy-start | bytes 3538948
  9.6 17.0 %copy-start.5 = (bf16[1,128,1536]{2,1,0:T(8,128)(2,1)S(1)}, bf16[1,128,1536]{2,1,0:T(8,128)(2,1)}, u32[]{:S(2)}) copy-start(bf16[1,128,1536]{2,1,0:T(8,128)(2,1)} %param.23) | copy-start | bytes 1179652
  9.6 17.5 %copy-start.4 = (bf16[1,1536,256]{2,1,0:T(8,128)(2,1)S(1)}, bf16[1,1536,256]{2,1,0:T(8,128)(2,1)}, u32[]{:S(2)}) copy-start(bf16[1,1536,256]{2,1,0:T(8,128)(2,1)} %param.22) | copy-start | bytes 2359300
  9.7 80.8 %all-to-all-start = ((bf16[128,32,256]{2,1,0:T(8,128)(2,1)}), bf16[128,32,256]{2,1,0:T(8,128)(2,1)}, u32[]{:S(2)}, u32[]{:S(2)}) async-start(bf16[128,32,256]{2,1,0:T(8,128)(2,1)} %broadcast_in_dim.42), calls=%async_computation | async-start | bytes 4194304 | tf_op jit(solution)/shard_map/all_to_all | solution.py:135
  26.6 97.7 %all-gather.2.cloned.1.call-start = ((), (), s32[]{:S(2)}) async-start(), calls=%async_computation.4 | async-start | bytes 5898240 | tf_op jit(solution)/shard_map/all_gather | solution.py:84
  27.2 1.2 copy-start.10
  27.2 1.3 copy-start.1
  27.2 1.8 copy-start.6
  28.4 1.3 copy-start.3
  29.3 1.3 copy-start.7
  99.7 6.1 %copy-start.8 = (s32[32,8]{0,1:T(8,128)S(1)}, s32[32,8]{0,1:T(8,128)}, u32[]{:S(2)}) copy-start(s32[32,8]{0,1:T(8,128)} %param.20) | copy-start | bytes 3076
  101.0 14.4 %all-to-all-start.1 = ((f32[4,32,1536]{2,1,0:T(8,128)}), f32[4,32,1536]{2,1,0:T(8,128)S(1)}, u32[]{:S(2)}, u32[]{:S(2)}) async-start(f32[4,32,1536]{2,1,0:T(8,128)} %fusion.7), calls=%async_computation.1 | async-start | bytes 1572864 | tf_op jit(solution)/shard_map/all_to_all | solution.py:159
  117.3 56.6 %all-to-all-start.2 = ((bf16[32,16,1536]{2,1,0:T(8,128)(2,1)}), bf16[32,16,1536]{2,1,0:T(8,128)(2,1)}, u32[]{:S(2)}, u32[]{:S(2)}) async-start(bf16[32,16,1536]{2,1,0:T(8,128)(2,1)} %bitcast.22), calls=%async_computation.2 | async-start | bytes 3145728 | tf_op jit(solution)/shard_map/all_to_all | solution.py:184
  124.3 1.4 slice-start
  174.0 4.3 %copy-start.2 = (bf16[4,128,1536]{2,1,0:T(8,128)(2,1)S(1)}, bf16[4,128,1536]{2,1,0:T(8,128)(2,1)}, u32[]{:S(2)}) copy-start(bf16[4,128,1536]{2,1,0:T(8,128)(2,1)} %reshape.201) | copy-start | bytes 4718596
  181.4 6.5 %copy-start.9 = (f32[32,8]{0,1:T(8,128)S(1)}, f32[32,8]{0,1:T(8,128)}, u32[]{:S(2)}) copy-start(f32[32,8]{0,1:T(8,128)} %param.21) | copy-start | bytes 3076
  181.4 58.5 %all-to-all-start.3 = ((bf16[32,16,1536]{2,1,0:T(8,128)(2,1)}), bf16[32,16,1536]{2,1,0:T(8,128)(2,1)S(1)}, u32[]{:S(2)}, u32[]{:S(2)}) async-start(bf16[32,16,1536]{2,1,0:T(8,128)(2,1)} %bitcast.65), calls=%async_computation.3 | async-start | bytes 3145728 | tf_op jit(solution)/shard_map/all_to_all | solution.py:192
Sparse Core Ops, SparseCore 0:
  29.5 81.3 all-gather.1

commit v7 on v6

--- a/solution.py
+++ b/solution.py
@@ -11,6 +11,8 @@
 SEQ = ("z", "yh", "yl", "c")
 EXPERT_AXES = ("z", "yh")
 PART_AXES = ("yl", "c")
+CHIP_AXES = ("z", "yh", "yl")
+CORE_AXIS = "c"
 
 EPSILON = 1e-06
 RESIDUAL = 0.22
@@ -131,10 +133,12 @@
     )
     running = (row_top, denominator, numerator)
     prefix_both = jnp.concatenate([cached_prefix_keys, cached_prefix_values], axis=1)
-    seq_total = prefix_len // prefix_both.shape[0]
-    whole_both = lax.all_to_all(
-        jnp.broadcast_to(prefix_both[None], (seq_total,) + prefix_both.shape), SEQ, 0, 0, tiled=True
-    ).reshape(prefix_len, prefix_both.shape[1])
+    chip_total = prefix_len // prefix_both.shape[0] // lax.axis_size(CORE_AXIS)
+    same_core = lax.all_to_all(
+        jnp.broadcast_to(prefix_both[None], (chip_total,) + prefix_both.shape), CHIP_AXES, 0, 0, tiled=True
+    ).reshape(-1, prefix_both.shape[1])
+    other_core = lax.ppermute(same_core, CORE_AXIS, [(0, 1), (1, 0)])
+    whole_both = jnp.concatenate([same_core, other_core], axis=0)
     top_old, denom_old, numer_old = running
     rows_q = rows_dev * group_width
 

time: 249 us -> 217 us (0.87)
  the two profiles are of different devices: /device:TPU:82 before, /device:TPU:80 now
where the time goes in v7:
time: 217 us
  waiting for transfers between devices  123 us (57%)
  starting transfers between devices  35.9 us (17%)
  matrix products  14.6 us (7%)
  between operations  14.4 us (7%)
  local copies, waits for them, and re-layouts  12.8 us (6%)
  other arithmetic  8.04 us (4%)
  Pallas kernels  7.82 us (4%)
    all_to_all x1, waiting for transfers between devices, body(): lax.all_to_all(outgoing, EXPERT_AXES, split_axis=0, concat_axis=0, tiled=...  46.3 us
    all_to_all x1, waiting for transfers between devices, body(): lax.all_to_all(part_total.reshape(experts, capacity, column_list), EXPERT...  41.9 us
    all_to_all x1, waiting for transfers between devices, body(): lax.all_to_all(jnp.broadcast_to(prefix_both[None], (chip_total,) + prefix...  23.3 us
    all_to_all x1, starting transfers between devices, body(): lax.all_to_all(jnp.broadcast_to(prefix_both[None], (chip_total,) + prefix...  15.6 us
    all_to_all x1, waiting for transfers between devices, body(): lax.all_to_all(attn_part.reshape(tp_count, moe_rows, column_list), 'tp',...  11.6 us
    pallas_call x1, Pallas kernels, prefix_attention(): pl.pallas_call(kernel, out_shape=jax.ShapeDtypeStruct(queries.shape, jnp....  7.82 us
    all_to_all x1, starting transfers between devices, body(): lax.all_to_all(outgoing, EXPERT_AXES, split_axis=0, concat_axis=0, tiled=...  7.65 us
    all_to_all x1, starting transfers between devices, body(): lax.all_to_all(part_total.reshape(experts, capacity, column_list), EXPERT...  6.44 us
  transfers between devices with their start and end apart: 6, of which 4 were waited for; matrix products, arithmetic and copies ran while one was open for 10% of the time, Pallas kernels for 4%

profile of v7, /device:TPU:80, one launch (start us, length us, event | category | flops | bytes accessed | tf_op | source)
XLA Modules:
  0.0 216.7 jit_solution(14237398899796612885)
XLA Ops:
  7.2 0.8 pad_maximum_fusion.4
  8.0 1.1 broadcast_in_dim.42
  9.1 15.6 %all-to-all-start = ((bf16[64,32,256]{2,1,0:T(8,128)(2,1)}), bf16[64,32,256]{2,1,0:T(8,128)(2,1)S(1)}, u32[]{:S(2)}, u32[]{:S(2)}) async-start(bf16[64,32,256]{2,1,0:T(8,128)(2,1)} %broadcast_in_dim.42), calls=%async_computation | async-start | bytes 2097152 | tf_op jit(solution)/shard_map/all_to_all | solution.py:137
  24.8 0.5 reshape.198
  25.3 2.3 %pad_maximum_fusion.1 = bf16[1,1536,384]{2,1,0:T(8,128)(2,1)} fusion(bf16[1,1536,128]{2,1,0:T(8,128)(2,1)S(1)} %reshape.198, bf16[1,1536,256]{2,1,0:T(8,128)(2,1)} %param.22), kind=kLoop, calls=%fused_computation.9 | loop fusion | flops 2359296 | bytes 2359296 | tf_op jit(solution)/shard_map/concatenate | solution.py:83
  28.5 0.4 copy-done.3
  28.9 0.6 fusion.32
  29.6 23.3 %all-to-all-done = bf16[64,32,256]{2,1,0:T(8,128)(2,1)S(1)} async-done(((bf16[64,32,256]{2,1,0:T(8,128)(2,1)}), bf16[64,32,256]{2,1,0:T(8,128)(2,1)S(1)}, u32[]{:S(2)}, u32[]{:S(2)}) %all-to-all-start) | async-done | bytes 1048608 | tf_op jit(solution)/shard_map/all_to_all | solution.py:137
  52.9 1.9 collective-permute-start
  55.6 0.9 fusion.17
  56.4 1.2 copy.86
  57.6 0.8 copy.90.num_ref
  58.6 0.9 reshape.209.den_ref
  59.7 0.9 reshape.208.top_ref
  60.8 0.7 copy.87.q_ref
  61.5 2.7 %pad_maximum_fusion.kv_ref = bf16[4096,256]{1,0:T(8,128)(2,1)} fusion(bf16[2048,256]{1,0:T(8,128)(2,1)} %collective-permute-done, bf16[2048,256]{1,0:T(8,128)(2,1)S(1)} %bitcast.66), kind=kLoop, calls=%fused_computation.4 | loop fusion | flops 4194304 | bytes 4194304 | tf_op jit(solution)/shard_map/concatenate | solution.py:141
  64.2 7.8 %shard_map.139 = bf16[2,384,64]{2,1,0:T(8,128)(2,1)} custom-call(bf16[2,384,64]{2,1,0:T(8,128)(2,1)} %copy.87.q_ref, bf16[4096,256]{1,0:T(8,128)(2,1)} %pad_maximum_fusion.kv_ref, f32[2,384,1]{2,1,0:T(8,128)} %reshape.208.top_ref, f32[2,384,1]{2,1,0:T(8,128)} %reshape.209.den_ref, f32[2,384,64]{2,1,0:T(8,128)} %copy.90.num_ref), custom_call_target="tpu_custom_call" | custom-call | tf_op jit(solution)/shard_map/pallas_call | solution.py:63
  72.1 1.1 copy.91
  73.5 1.3 fusion.7
  74.8 4.3 %all-to-all-start.1 = ((f32[4,32,1536]{2,1,0:T(8,128)}), f32[4,32,1536]{2,1,0:T(8,128)S(1)}, u32[]{:S(2)}, u32[]{:S(2)}) async-start(f32[4,32,1536]{2,1,0:T(8,128)} %fusion.7), calls=%async_computation.1 | async-start | bytes 1572864 | tf_op jit(solution)/shard_map/all_to_all | solution.py:163
  79.4 0.7 select_reduce_fusion.1
  80.4 11.6 %all-to-all-done.1 = f32[4,32,1536]{2,1,0:T(8,128)S(1)} async-done(((f32[4,32,1536]{2,1,0:T(8,128)}), f32[4,32,1536]{2,1,0:T(8,128)S(1)}, u32[]{:S(2)}, u32[]{:S(2)}) %all-to-all-start.1) | async-done | bytes 786464 | tf_op jit(solution)/shard_map/all_to_all | solution.py:163
  92.2 1.9 convolution_convert_fusion
  94.1 7.6 %all-to-all-start.2 = ((bf16[32,16,1536]{2,1,0:T(8,128)(2,1)}), bf16[32,16,1536]{2,1,0:T(8,128)(2,1)}, u32[]{:S(2)}, u32[]{:S(2)}) async-start(bf16[32,16,1536]{2,1,0:T(8,128)(2,1)} %bitcast.22), calls=%async_computation.2 | async-start | bytes 3145728 | tf_op jit(solution)/shard_map/all_to_all | solution.py:188
  101.8 1.4 slice-done
  103.2 2.6 %reshape.201 = bf16[4,128,1536]{2,1,0:T(8,128)(2,1)} reshape(bf16[4,1536,128]{2,1,0:T(8,128)(2,1)S(1)} %slice-done) | data formatting | bytes 3145728 | tf_op jit(solution)/shard_map/reshape | solution.py:88
  105.8 46.3 %all-to-all-done.2 = bf16[32,16,1536]{2,1,0:T(8,128)(2,1)} async-done(((bf16[32,16,1536]{2,1,0:T(8,128)(2,1)}), bf16[32,16,1536]{2,1,0:T(8,128)(2,1)}, u32[]{:S(2)}, u32[]{:S(2)}) %all-to-all-start.2) | async-done | bytes 1572896 | tf_op jit(solution)/shard_map/all_to_all | solution.py:188
  152.2 4.3 %fusion.2 = f32[4,512,256]{1,2,0:T(8,128)S(1)} fusion(bf16[512,1536,1]{1,0,2:T(8,128)(2,1)} %bitcast.24, bf16[4,1536,384]{2,1,0:T(8,128)(2,1)} %all-gather.2.cloned.1.call-done), kind=kOutput, calls=%fused_computation.5 | convolution fusion | flops 1610612736 | bytes 6815744 | tf_op jit(solution)/shard_map/rd,pdf->prf/dot_general | solution.py:190
  156.5 3.1 %convert_reduce_fusion = bf16[512,1536]{1,0:T(8,128)(2,1)} fusion(bf16[4,128,1536]{2,1,0:T(8,128)(2,1)S(1)} %copy-done.2, f32[4,512,256]{1,2,0:T(8,128)S(1)} %fusion.2), kind=kOutput, calls=%fused_computation | convolution fusion | flops 812384256 | bytes 5242880 | tf_op jit(solution)/shard_map/prf,pfd->prd/dot_general | solution.py:192
  159.7 6.4 %all-to-all-start.3 = ((bf16[32,16,1536]{2,1,0:T(8,128)(2,1)}), bf16[32,16,1536]{2,1,0:T(8,128)(2,1)S(1)}, u32[]{:S(2)}, u32[]{:S(2)}) async-start(bf16[32,16,1536]{2,1,0:T(8,128)(2,1)} %bitcast.67), calls=%async_computation.3 | async-start | bytes 3145728 | tf_op jit(solution)/shard_map/all_to_all | solution.py:196
  166.4 41.9 %all-to-all-done.3 = bf16[32,16,1536]{2,1,0:T(8,128)(2,1)S(1)} async-done(((bf16[32,16,1536]{2,1,0:T(8,128)(2,1)}), bf16[32,16,1536]{2,1,0:T(8,128)(2,1)S(1)}, u32[]{:S(2)}, u32[]{:S(2)}) %all-to-all-start.3) | async-done | bytes 1572896 | tf_op jit(solution)/shard_map/all_to_all | solution.py:196
  208.3 1.5 add_convert_fusion
  (56 shorter events, 3.6 us)
Async XLA Ops:
  7.2 66.4 %copy-start = (bf16[384,1536]{1,0:T(8,128)(2,1)S(1)}, bf16[384,1536]{1,0:T(8,128)(2,1)}, u32[]{:S(2)}) copy-start(bf16[384,1536]{1,0:T(8,128)(2,1)} %param.16) | copy-start | bytes 3538948
  8.0 16.8 %copy-start.4 = (bf16[1,128,1536]{2,1,0:T(8,128)(2,1)S(1)}, bf16[1,128,1536]{2,1,0:T(8,128)(2,1)}, u32[]{:S(2)}) copy-start(bf16[1,128,1536]{2,1,0:T(8,128)(2,1)} %param.23) | copy-start | bytes 1179652
  9.1 43.8 %all-to-all-start = ((bf16[64,32,256]{2,1,0:T(8,128)(2,1)}), bf16[64,32,256]{2,1,0:T(8,128)(2,1)S(1)}, u32[]{:S(2)}, u32[]{:S(2)}) async-start(bf16[64,32,256]{2,1,0:T(8,128)(2,1)} %broadcast_in_dim.42), calls=%async_computation | async-start | bytes 2097152 | tf_op jit(solution)/shard_map/all_to_all | solution.py:137
  24.7 77.1 %all-gather.2.cloned.1.call-start = ((), (), s32[]{:S(2)}) async-start(), calls=%async_computation.4 | async-start | bytes 5898240 | tf_op jit(solution)/shard_map/all_gather | solution.py:86
  25.2 2.4 %copy-start.9 = (s32[1,128]{1,0:T(1,128)S(1)}, s32[1,128]{1,0:T(1,128)}, u32[]{:S(2)}) copy-start(s32[1,128]{1,0:T(1,128)} %param.19) | copy-start | bytes 1540
  25.3 2.5 %copy-start.1 = (bf16[128,1536]{1,0:T(8,128)(2,1)S(1)}, bf16[128,1536]{1,0:T(8,128)(2,1)}, u32[]{:S(2)}) copy-start(bf16[128,1536]{1,0:T(8,128)(2,1)} %param.12) | copy-start | bytes 1179652
  25.3 2.7 %copy-start.5 = (bf16[1536,128]{1,0:T(8,128)(2,1)S(1)}, bf16[1536,128]{1,0:T(8,128)(2,1)}, u32[]{:S(2)}) copy-start(bf16[1536,128]{1,0:T(8,128)(2,1)} %param.14) | copy-start | bytes 1179652
  27.6 1.3 copy-start.3
  28.3 26.9 %copy-start.6 = (bf16[1536,128]{1,0:T(8,128)(2,1)S(1)}, bf16[1536,128]{1,0:T(8,128)(2,1)}, u32[]{:S(2)}) copy-start(bf16[1536,128]{1,0:T(8,128)(2,1)} %param.15) | copy-start | bytes 1179652
  52.9 8.6 %collective-permute-start = (bf16[2048,256]{1,0:T(8,128)(2,1)S(1)}, bf16[2048,256]{1,0:T(8,128)(2,1)}, u32[]{:S(2)}, u32[]{:S(2)}) collective-permute-start(bf16[2048,256]{1,0:T(8,128)(2,1)S(1)} %bitcast.65), channel_id=1, source_target_pairs={{0,4},{4,0},{1,5},{5,1},{2,6},{6,2},{3,7},{7,3},{8,12},{12,8},{9,1... | collective-permute-start | bytes 3145736 | tf_op jit(solution)/shard_map/ppermute | solution.py:140
  73.5 5.6 %copy-start.7 = (s32[32,8]{0,1:T(8,128)S(1)}, s32[32,8]{0,1:T(8,128)}, u32[]{:S(2)}) copy-start(s32[32,8]{0,1:T(8,128)} %param.20) | copy-start | bytes 3076
  74.8 17.2 %all-to-all-start.1 = ((f32[4,32,1536]{2,1,0:T(8,128)}), f32[4,32,1536]{2,1,0:T(8,128)S(1)}, u32[]{:S(2)}, u32[]{:S(2)}) async-start(f32[4,32,1536]{2,1,0:T(8,128)} %fusion.7), calls=%async_computation.1 | async-start | bytes 1572864 | tf_op jit(solution)/shard_map/all_to_all | solution.py:163
  94.1 58.1 %all-to-all-start.2 = ((bf16[32,16,1536]{2,1,0:T(8,128)(2,1)}), bf16[32,16,1536]{2,1,0:T(8,128)(2,1)}, u32[]{:S(2)}, u32[]{:S(2)}) async-start(bf16[32,16,1536]{2,1,0:T(8,128)(2,1)} %bitcast.22), calls=%async_computation.2 | async-start | bytes 3145728 | tf_op jit(solution)/shard_map/all_to_all | solution.py:188
  101.8 1.4 slice-start
  152.2 4.3 %copy-start.2 = (bf16[4,128,1536]{2,1,0:T(8,128)(2,1)S(1)}, bf16[4,128,1536]{2,1,0:T(8,128)(2,1)}, u32[]{:S(2)}) copy-start(bf16[4,128,1536]{2,1,0:T(8,128)(2,1)} %reshape.201) | copy-start | bytes 4718596
  159.6 6.5 %copy-start.8 = (f32[32,8]{0,1:T(8,128)S(1)}, f32[32,8]{0,1:T(8,128)}, u32[]{:S(2)}) copy-start(f32[32,8]{0,1:T(8,128)} %param.21) | copy-start | bytes 3076
  159.7 48.7 %all-to-all-start.3 = ((bf16[32,16,1536]{2,1,0:T(8,128)(2,1)}), bf16[32,16,1536]{2,1,0:T(8,128)(2,1)S(1)}, u32[]{:S(2)}, u32[]{:S(2)}) async-start(bf16[32,16,1536]{2,1,0:T(8,128)(2,1)} %bitcast.67), calls=%async_computation.3 | async-start | bytes 3145728 | tf_op jit(solution)/shard_map/all_to_all | solution.py:196
Sparse Core Ops, SparseCore 0:
  27.8 58.6 all-gather.1

commit v8 on v7

--- a/solution.py
+++ b/solution.py
@@ -83,7 +83,8 @@
     packed = jnp.concatenate(
         [expert_in, expert_out.reshape(expert_out.shape[0], expert_in.shape[1], -1)], axis=2
     )
-    packed = lax.all_gather(packed, PART_AXES, axis=0, tiled=True)
+    packed = lax.all_gather(packed, PART_AXES[0], axis=0, tiled=True)
+    packed = lax.all_gather(packed, PART_AXES[1], axis=0, tiled=True)
     full_in = packed[..., :in_cols]
     full_out = packed[..., in_cols:].reshape((packed.shape[0],) + expert_out.shape[1:])
     rows_dev = hidden_in.shape[0]

time: 217 us -> 234 us (1.078)
  the two profiles are of different devices: /device:TPU:80 before, /device:TPU:4 now
where the time goes in v8:
time: 234 us; the launch traced here: 233 us
  waiting for transfers between devices  134 us (57%)
  starting transfers between devices  41.1 us (18%)
  matrix products  14.6 us (6%)
  between operations  14.4 us (6%)
  local copies, waits for them, and re-layouts  12.8 us (5%)
  other arithmetic  8.07 us (3%)
  Pallas kernels  7.74 us (3%)
    all_to_all x1, waiting for transfers between devices, body(): lax.all_to_all(part_total.reshape(experts, capacity, column_list), EXPERT...  51.7 us
    all_to_all x1, waiting for transfers between devices, body(): lax.all_to_all(outgoing, EXPERT_AXES, split_axis=0, concat_axis=0, tiled=...  38.4 us
    all_to_all x1, waiting for transfers between devices, body(): lax.all_to_all(jnp.broadcast_to(prefix_both[None], (chip_total,) + prefix...  24.9 us
    all_to_all x1, starting transfers between devices, body(): lax.all_to_all(jnp.broadcast_to(prefix_both[None], (chip_total,) + prefix...  16.6 us
    all_to_all x1, starting transfers between devices, body(): lax.all_to_all(outgoing, EXPERT_AXES, split_axis=0, concat_axis=0, tiled=...  11.3 us
    all_gather x1, waiting for transfers between devices, body(): packed = lax.all_gather(packed, PART_AXES[0], axis=0, tiled=True)  11.1 us
    all_to_all x1, waiting for transfers between devices, body(): lax.all_to_all(attn_part.reshape(tp_count, moe_rows, column_list), 'tp',...  8.05 us
    pallas_call x1, Pallas kernels, prefix_attention(): pl.pallas_call(kernel, out_shape=jax.ShapeDtypeStruct(queries.shape, jnp....  7.74 us
  transfers between devices with their start and end apart: 7, of which 5 were waited for; matrix products, arithmetic and copies ran while one was open for 10% of the time, Pallas kernels for 3%

profile of v8, /device:TPU:4, one launch (start us, length us, event | category | flops | bytes accessed | tf_op | source)
XLA Modules:
  0.0 232.9 jit_solution(3285407276124641892)
XLA Ops:
  7.2 0.8 pad_maximum_fusion.4
  8.0 1.2 broadcast_in_dim.42
  9.2 16.6 %all-to-all-start = ((bf16[64,32,256]{2,1,0:T(8,128)(2,1)}), bf16[64,32,256]{2,1,0:T(8,128)(2,1)S(1)}, u32[]{:S(2)}, u32[]{:S(2)}) async-start(bf16[64,32,256]{2,1,0:T(8,128)(2,1)} %broadcast_in_dim.42), calls=%async_computation | async-start | bytes 2097152 | tf_op jit(solution)/shard_map/all_to_all | solution.py:138
  25.8 0.5 reshape.198
  26.3 2.3 %pad_maximum_fusion.1 = bf16[1,1536,384]{2,1,0:T(8,128)(2,1)} fusion(bf16[1,1536,128]{2,1,0:T(8,128)(2,1)S(1)} %reshape.198, bf16[1,1536,256]{2,1,0:T(8,128)(2,1)} %param.22), kind=kLoop, calls=%fused_computation.9 | loop fusion | flops 2359296 | bytes 2359296 | tf_op jit(solution)/shard_map/concatenate | solution.py:83
  30.0 0.6 fusion.32
  30.7 24.9 %all-to-all-done = bf16[64,32,256]{2,1,0:T(8,128)(2,1)S(1)} async-done(((bf16[64,32,256]{2,1,0:T(8,128)(2,1)}), bf16[64,32,256]{2,1,0:T(8,128)(2,1)S(1)}, u32[]{:S(2)}, u32[]{:S(2)}) %all-to-all-start) | async-done | bytes 1048608 | tf_op jit(solution)/shard_map/all_to_all | solution.py:138
  55.6 1.9 collective-permute-start
  58.3 0.9 fusion.17
  59.1 1.2 copy.86
  60.3 0.8 copy.90.num_ref
  61.3 0.9 reshape.209.den_ref
  62.4 0.9 reshape.208.top_ref
  63.4 0.7 copy.87.q_ref
  64.1 11.1 %all-gather.3.cloned.1.call-done = bf16[2,1536,384]{2,1,0:T(8,128)(2,1)} async-done(((bf16[1,1536,384]{2,1,0:T(8,128)(2,1)}), bf16[2,1536,384]{2,1,0:T(8,128)(2,1)}) %all-gather.3.cloned.1.call-update) | async-done | bytes 2359312 | tf_op jit(solution)/shard_map/all_gather | solution.py:86
  75.3 2.8 %pad_maximum_fusion.kv_ref = bf16[4096,256]{1,0:T(8,128)(2,1)} fusion(bf16[2048,256]{1,0:T(8,128)(2,1)} %collective-permute-done, bf16[2048,256]{1,0:T(8,128)(2,1)S(1)} %bitcast.66), kind=kLoop, calls=%fused_computation.4 | loop fusion | flops 4194304 | bytes 4194304 | tf_op jit(solution)/shard_map/concatenate | solution.py:142
  78.1 7.7 %shard_map.139 = bf16[2,384,64]{2,1,0:T(8,128)(2,1)} custom-call(bf16[2,384,64]{2,1,0:T(8,128)(2,1)} %copy.87.q_ref, bf16[4096,256]{1,0:T(8,128)(2,1)} %pad_maximum_fusion.kv_ref, f32[2,384,1]{2,1,0:T(8,128)} %reshape.208.top_ref, f32[2,384,1]{2,1,0:T(8,128)} %reshape.209.den_ref, f32[2,384,64]{2,1,0:T(8,128)} %copy.90.num_ref), custom_call_target="tpu_custom_call" | custom-call | tf_op jit(solution)/shard_map/pallas_call | solution.py:63
  85.8 1.1 copy.91
  87.3 1.3 fusion.7
  88.6 4.8 %all-to-all-start.1 = ((f32[4,32,1536]{2,1,0:T(8,128)}), f32[4,32,1536]{2,1,0:T(8,128)S(1)}, u32[]{:S(2)}, u32[]{:S(2)}) async-start(f32[4,32,1536]{2,1,0:T(8,128)} %fusion.7), calls=%async_computation.1 | async-start | bytes 1572864 | tf_op jit(solution)/shard_map/all_to_all | solution.py:164
  93.6 0.7 select_reduce_fusion.1
  94.7 8.1 %all-to-all-done.1 = f32[4,32,1536]{2,1,0:T(8,128)S(1)} async-done(((f32[4,32,1536]{2,1,0:T(8,128)}), f32[4,32,1536]{2,1,0:T(8,128)S(1)}, u32[]{:S(2)}, u32[]{:S(2)}) %all-to-all-start.1) | async-done | bytes 786464 | tf_op jit(solution)/shard_map/all_to_all | solution.py:164
  103.0 1.9 convolution_convert_fusion
  104.8 11.3 %all-to-all-start.2 = ((bf16[32,16,1536]{2,1,0:T(8,128)(2,1)}), bf16[32,16,1536]{2,1,0:T(8,128)(2,1)}, u32[]{:S(2)}, u32[]{:S(2)}) async-start(bf16[32,16,1536]{2,1,0:T(8,128)(2,1)} %bitcast.22), calls=%async_computation.2 | async-start | bytes 3145728 | tf_op jit(solution)/shard_map/all_to_all | solution.py:189
  116.1 1.4 slice-done
  117.5 2.7 %reshape.201 = bf16[4,128,1536]{2,1,0:T(8,128)(2,1)} reshape(bf16[4,1536,128]{2,1,0:T(8,128)(2,1)S(1)} %slice-done) | data formatting | bytes 3145728 | tf_op jit(solution)/shard_map/reshape | solution.py:89
  120.2 38.4 %all-to-all-done.2 = bf16[32,16,1536]{2,1,0:T(8,128)(2,1)} async-done(((bf16[32,16,1536]{2,1,0:T(8,128)(2,1)}), bf16[32,16,1536]{2,1,0:T(8,128)(2,1)}, u32[]{:S(2)}, u32[]{:S(2)}) %all-to-all-start.2) | async-done | bytes 1572896 | tf_op jit(solution)/shard_map/all_to_all | solution.py:189
  158.6 4.3 %fusion.2 = f32[4,512,256]{1,2,0:T(8,128)S(1)} fusion(bf16[512,1536,1]{1,0,2:T(8,128)(2,1)} %bitcast.24, bf16[4,1536,384]{2,1,0:T(8,128)(2,1)} %all-gather.5.cloned.1.call-done), kind=kOutput, calls=%fused_computation.5 | convolution fusion | flops 1610612736 | bytes 6815744 | tf_op jit(solution)/shard_map/rd,pdf->prf/dot_general | solution.py:191
  162.9 3.1 %convert_reduce_fusion = bf16[512,1536]{1,0:T(8,128)(2,1)} fusion(bf16[4,128,1536]{2,1,0:T(8,128)(2,1)S(1)} %copy-done.2, f32[4,512,256]{1,2,0:T(8,128)S(1)} %fusion.2), kind=kOutput, calls=%fused_computation | convolution fusion | flops 812384256 | bytes 5242880 | tf_op jit(solution)/shard_map/prf,pfd->prd/dot_general | solution.py:193
  166.1 6.5 %all-to-all-start.3 = ((bf16[32,16,1536]{2,1,0:T(8,128)(2,1)}), bf16[32,16,1536]{2,1,0:T(8,128)(2,1)S(1)}, u32[]{:S(2)}, u32[]{:S(2)}) async-start(bf16[32,16,1536]{2,1,0:T(8,128)(2,1)} %bitcast.67), calls=%async_computation.3 | async-start | bytes 3145728 | tf_op jit(solution)/shard_map/all_to_all | solution.py:197
  172.9 51.7 %all-to-all-done.3 = bf16[32,16,1536]{2,1,0:T(8,128)(2,1)S(1)} async-done(((bf16[32,16,1536]{2,1,0:T(8,128)(2,1)}), bf16[32,16,1536]{2,1,0:T(8,128)(2,1)S(1)}, u32[]{:S(2)}, u32[]{:S(2)}) %all-to-all-start.3) | async-done | bytes 1572896 | tf_op jit(solution)/shard_map/all_to_all | solution.py:197
  224.6 1.5 add_convert_fusion
  (59 shorter events, 4.1 us)
Async XLA Ops:
  7.2 80.1 %copy-start = (bf16[384,1536]{1,0:T(8,128)(2,1)S(1)}, bf16[384,1536]{1,0:T(8,128)(2,1)}, u32[]{:S(2)}) copy-start(bf16[384,1536]{1,0:T(8,128)(2,1)} %param.16) | copy-start | bytes 3538948
  8.0 17.8 %copy-start.4 = (bf16[1,128,1536]{2,1,0:T(8,128)(2,1)S(1)}, bf16[1,128,1536]{2,1,0:T(8,128)(2,1)}, u32[]{:S(2)}) copy-start(bf16[1,128,1536]{2,1,0:T(8,128)(2,1)} %param.23) | copy-start | bytes 1179652
  9.2 46.4 %all-to-all-start = ((bf16[64,32,256]{2,1,0:T(8,128)(2,1)}), bf16[64,32,256]{2,1,0:T(8,128)(2,1)S(1)}, u32[]{:S(2)}, u32[]{:S(2)}) async-start(bf16[64,32,256]{2,1,0:T(8,128)(2,1)} %broadcast_in_dim.42), calls=%async_computation | async-start | bytes 2097152 | tf_op jit(solution)/shard_map/all_to_all | solution.py:138
  25.7 49.5 %all-gather.3.cloned.1.call-start = ((), (), s32[]{:S(2)}) async-start(), calls=%async_computation.4 | async-start | bytes 3538944 | tf_op jit(solution)/shard_map/all_gather | solution.py:86
  26.3 2.5 %copy-start.9 = (s32[1,128]{1,0:T(1,128)S(1)}, s32[1,128]{1,0:T(1,128)}, u32[]{:S(2)}) copy-start(s32[1,128]{1,0:T(1,128)} %param.19) | copy-start | bytes 1540
  26.3 2.6 %copy-start.1 = (bf16[128,1536]{1,0:T(8,128)(2,1)S(1)}, bf16[128,1536]{1,0:T(8,128)(2,1)}, u32[]{:S(2)}) copy-start(bf16[128,1536]{1,0:T(8,128)(2,1)} %param.12) | copy-start | bytes 1179652
  26.3 2.9 %copy-start.5 = (bf16[1536,128]{1,0:T(8,128)(2,1)S(1)}, bf16[1536,128]{1,0:T(8,128)(2,1)}, u32[]{:S(2)}) copy-start(bf16[1536,128]{1,0:T(8,128)(2,1)} %param.14) | copy-start | bytes 1179652
  28.7 87.4 %all-gather.5.cloned.1.call-start = ((), (), s32[]{:S(2)}) async-start(), calls=%async_computation.5 | async-start | bytes 7077888 | tf_op jit(solution)/shard_map/all_gather | solution.py:87
  28.7 1.3 copy-start.3
  29.6 28.3 %copy-start.6 = (bf16[1536,128]{1,0:T(8,128)(2,1)S(1)}, bf16[1536,128]{1,0:T(8,128)(2,1)}, u32[]{:S(2)}) copy-start(bf16[1536,128]{1,0:T(8,128)(2,1)} %param.15) | copy-start | bytes 1179652
  55.6 19.7 %collective-permute-start = (bf16[2048,256]{1,0:T(8,128)(2,1)S(1)}, bf16[2048,256]{1,0:T(8,128)(2,1)}, u32[]{:S(2)}, u32[]{:S(2)}) collective-permute-start(bf16[2048,256]{1,0:T(8,128)(2,1)S(1)} %bitcast.65), channel_id=1, source_target_pairs={{0,4},{4,0},{1,5},{5,1},{2,6},{6,2},{3,7},{7,3},{8,12},{12,8},{9,1... | collective-permute-start | bytes 3145736 | tf_op jit(solution)/shard_map/ppermute | solution.py:141
  87.3 6.1 %copy-start.7 = (s32[32,8]{0,1:T(8,128)S(1)}, s32[32,8]{0,1:T(8,128)}, u32[]{:S(2)}) copy-start(s32[32,8]{0,1:T(8,128)} %param.20) | copy-start | bytes 3076
  88.6 14.2 %all-to-all-start.1 = ((f32[4,32,1536]{2,1,0:T(8,128)}), f32[4,32,1536]{2,1,0:T(8,128)S(1)}, u32[]{:S(2)}, u32[]{:S(2)}) async-start(f32[4,32,1536]{2,1,0:T(8,128)} %fusion.7), calls=%async_computation.1 | async-start | bytes 1572864 | tf_op jit(solution)/shard_map/all_to_all | solution.py:164
  104.8 53.8 %all-to-all-start.2 = ((bf16[32,16,1536]{2,1,0:T(8,128)(2,1)}), bf16[32,16,1536]{2,1,0:T(8,128)(2,1)}, u32[]{:S(2)}, u32[]{:S(2)}) async-start(bf16[32,16,1536]{2,1,0:T(8,128)(2,1)} %bitcast.22), calls=%async_computation.2 | async-start | bytes 3145728 | tf_op jit(solution)/shard_map/all_to_all | solution.py:189
  116.1 1.4 slice-start
  158.6 4.3 %copy-start.2 = (bf16[4,128,1536]{2,1,0:T(8,128)(2,1)S(1)}, bf16[4,128,1536]{2,1,0:T(8,128)(2,1)}, u32[]{:S(2)}) copy-start(bf16[4,128,1536]{2,1,0:T(8,128)(2,1)} %reshape.201) | copy-start | bytes 4718596
  166.1 6.5 %copy-start.8 = (f32[32,8]{0,1:T(8,128)S(1)}, f32[32,8]{0,1:T(8,128)}, u32[]{:S(2)}) copy-start(f32[32,8]{0,1:T(8,128)} %param.21) | copy-start | bytes 3076
  166.1 58.5 %all-to-all-start.3 = ((bf16[32,16,1536]{2,1,0:T(8,128)(2,1)}), bf16[32,16,1536]{2,1,0:T(8,128)(2,1)S(1)}, u32[]{:S(2)}, u32[]{:S(2)}) async-start(bf16[32,16,1536]{2,1,0:T(8,128)(2,1)} %bitcast.67), calls=%async_computation.3 | async-start | bytes 3145728 | tf_op jit(solution)/shard_map/all_to_all | solution.py:197
Sparse Core Ops, SparseCore 0:
  28.8 46.4 all-gather.2
  77.4 22.2 all-gather.4

commit v9 on v8

--- a/solution.py
+++ b/solution.py
@@ -84,7 +84,7 @@
         [expert_in, expert_out.reshape(expert_out.shape[0], expert_in.shape[1], -1)], axis=2
     )
     packed = lax.all_gather(packed, PART_AXES[0], axis=0, tiled=True)
-    packed = lax.all_gather(packed, PART_AXES[1], axis=0, tiled=True)
+    packed = jnp.concatenate([packed, lax.ppermute(packed, CORE_AXIS, [(0, 1), (1, 0)])], axis=0)
     full_in = packed[..., :in_cols]
     full_out = packed[..., in_cols:].reshape((packed.shape[0],) + expert_out.shape[1:])
     rows_dev = hidden_in.shape[0]

time: 234 us -> 223 us (0.953)
  the two profiles are of different devices: /device:TPU:4 before, /device:TPU:16 now
where the time goes in v9:
time: 223 us; the launch traced here: 222 us
  waiting for transfers between devices  108 us (48%)
  starting transfers between devices  46.3 us (21%)
  local copies, waits for them, and re-layouts  19.4 us (9%)
  matrix products  17.2 us (8%)
  between operations  14.4 us (6%)
  other arithmetic  9.32 us (4%)
  Pallas kernels  7.73 us (3%)
    all_to_all x1, waiting for transfers between devices, body(): lax.all_to_all(part_total.reshape(experts, capacity, column_list), EXPERT...  42.7 us
    all_to_all x1, waiting for transfers between devices, body(): lax.all_to_all(outgoing, EXPERT_AXES, split_axis=0, concat_axis=0, tiled=...  25.4 us
    all_to_all x1, waiting for transfers between devices, body(): lax.all_to_all(jnp.broadcast_to(prefix_both[None], (chip_total,) + prefix...  23.5 us
    all_to_all x1, starting transfers between devices, body(): lax.all_to_all(jnp.broadcast_to(prefix_both[None], (chip_total,) + prefix...  16.5 us
    all_to_all x1, starting transfers between devices, body(): lax.all_to_all(part_total.reshape(experts, capacity, column_list), EXPERT...  15 us
    all_to_all x1, waiting for transfers between devices, body(): lax.all_to_all(attn_part.reshape(tp_count, moe_rows, column_list), 'tp',...  11.6 us
    pallas_call x1, Pallas kernels, prefix_attention(): pl.pallas_call(kernel, out_shape=jax.ShapeDtypeStruct(queries.shape, jnp....  7.73 us
    all_to_all x1, starting transfers between devices, body(): lax.all_to_all(outgoing, EXPERT_AXES, split_axis=0, concat_axis=0, tiled=...  6.7 us
  transfers between devices with their start and end apart: 7, of which 5 were waited for; matrix products, arithmetic and copies ran while one was open for 15% of the time, Pallas kernels for 3%

profile of v9, /device:TPU:16, one launch (start us, length us, event | category | flops | bytes accessed | tf_op | source)
XLA Modules:
  0.0 222.0 jit_solution(17200666701347412584)
XLA Ops:
  8.0 1.1 broadcast_in_dim.42
  9.1 16.5 %all-to-all-start = ((bf16[64,32,256]{2,1,0:T(8,128)(2,1)}), bf16[64,32,256]{2,1,0:T(8,128)(2,1)S(1)}, u32[]{:S(2)}, u32[]{:S(2)}) async-start(bf16[64,32,256]{2,1,0:T(8,128)(2,1)} %broadcast_in_dim.42), calls=%async_computation | async-start | bytes 2097152 | tf_op jit(solution)/shard_map/all_to_all | solution.py:138
  26.2 2.3 %pad_maximum_fusion.2 = bf16[1,1536,384]{2,1,0:T(8,128)(2,1)} fusion(bf16[1,1536,128]{2,1,0:T(8,128)(2,1)S(1)} %reshape.198, bf16[1,1536,256]{2,1,0:T(8,128)(2,1)} %param.22), kind=kLoop, calls=%fused_computation.12 | loop fusion | flops 2359296 | bytes 2359296 | tf_op jit(solution)/shard_map/concatenate | solution.py:83
  29.4 1.9 fusion.34
  31.3 23.5 %all-to-all-done = bf16[64,32,256]{2,1,0:T(8,128)(2,1)S(1)} async-done(((bf16[64,32,256]{2,1,0:T(8,128)(2,1)}), bf16[64,32,256]{2,1,0:T(8,128)(2,1)S(1)}, u32[]{:S(2)}, u32[]{:S(2)}) %all-to-all-start) | async-done | bytes 1048608 | tf_op jit(solution)/shard_map/all_to_all | solution.py:138
  54.8 1.9 collective-permute-start
  57.1 1.3 convolution_convert_fusion.1
  58.4 0.9 fusion.18
  59.3 1.2 copy.90
  61.5 0.9 reshape.209.den_ref
  62.5 0.9 reshape.208.top_ref
  64.3 2.7 %pad_maximum_fusion.kv_ref = bf16[4096,256]{1,0:T(8,128)(2,1)} fusion(bf16[2048,256]{1,0:T(8,128)(2,1)} %collective-permute-done, bf16[2048,256]{1,0:T(8,128)(2,1)S(1)} %bitcast.66), kind=kLoop, calls=%fused_computation.6 | loop fusion | flops 4194304 | bytes 4194304 | tf_op jit(solution)/shard_map/concatenate | solution.py:142
  67.0 7.7 %shard_map.139 = bf16[2,384,64]{2,1,0:T(8,128)(2,1)} custom-call(bf16[2,384,64]{2,1,0:T(8,128)(2,1)} %copy.91.q_ref, bf16[4096,256]{1,0:T(8,128)(2,1)} %pad_maximum_fusion.kv_ref, f32[2,384,1]{2,1,0:T(8,128)} %reshape.208.top_ref, f32[2,384,1]{2,1,0:T(8,128)} %reshape.209.den_ref, f32[2,384,64]{2,1,0:T(8,128)} %copy.94.num_ref), custom_call_target="tpu_custom_call" | custom-call | tf_op jit(solution)/shard_map/pallas_call | solution.py:63
  74.7 1.1 copy.95
  76.2 1.3 fusion.8
  77.4 4.3 %all-to-all-start.1 = ((f32[4,32,1536]{2,1,0:T(8,128)}), f32[4,32,1536]{2,1,0:T(8,128)S(1)}, u32[]{:S(2)}, u32[]{:S(2)}) async-start(f32[4,32,1536]{2,1,0:T(8,128)} %fusion.8), calls=%async_computation.1 | async-start | bytes 1572864 | tf_op jit(solution)/shard_map/all_to_all | solution.py:164
  83.1 11.6 %all-to-all-done.1 = f32[4,32,1536]{2,1,0:T(8,128)S(1)} async-done(((f32[4,32,1536]{2,1,0:T(8,128)}), f32[4,32,1536]{2,1,0:T(8,128)S(1)}, u32[]{:S(2)}, u32[]{:S(2)}) %all-to-all-start.1) | async-done | bytes 786464 | tf_op jit(solution)/shard_map/all_to_all | solution.py:164
  94.9 1.8 convolution_convert_fusion
  96.7 6.7 %all-to-all-start.2 = ((bf16[32,16,1536]{2,1,0:T(8,128)(2,1)}), bf16[32,16,1536]{2,1,0:T(8,128)(2,1)}, u32[]{:S(2)}, u32[]{:S(2)}) async-start(bf16[32,16,1536]{2,1,0:T(8,128)(2,1)} %bitcast.22), calls=%async_computation.2 | async-start | bytes 3145728 | tf_op jit(solution)/shard_map/all_to_all | solution.py:189
  103.5 2.8 %copy.102 = bf16[2,1536,384]{1,2,0:T(8,128)(2,1)S(1)} copy(bf16[2,1536,384]{2,1,0:T(8,128)(2,1)} %all-gather.2.cloned.1.call-done) | data formatting | bytes 4718592 | tf_op jit(solution)/shard_map/all_gather | solution.py:86
  106.3 1.9 collective-permute-start.1
  108.2 4.5 %collective-permute-done.1 = bf16[2,1536,384]{1,2,0:T(8,128)(2,1)S(1)} collective-permute-done((bf16[2,1536,384]{1,2,0:T(8,128)(2,1)S(1)}, bf16[2,1536,384]{1,2,0:T(8,128)(2,1)S(1)}, u32[]{:S(2)}, u32[]{:S(2)}) %collective-permute-start.1) | collective-permute-done | bytes 2359328 | tf_op jit(solution)/shard_map/ppermute | solution.py:87
  112.7 1.4 copy-done.4
  114.1 1.3 pad_maximum_fusion.1
  115.4 2.6 %copy.103 = bf16[4,1536,128]{2,1,0:T(8,128)(2,1)} copy(bf16[4,1536,128]{1,2,0:T(8,128)(2,1)} %pad_maximum_fusion.1) | data formatting | bytes 3145728 | tf_op jit(solution)/shard_map/slice | solution.py:89
  118.1 4.3 %reshape.201 = bf16[4,128,1536]{2,1,0:T(8,128)(2,1)} reshape(bf16[4,1536,128]{2,1,0:T(8,128)(2,1)} %copy.103) | data formatting | bytes 3145728 | tf_op jit(solution)/shard_map/reshape | solution.py:89
  122.3 25.4 %all-to-all-done.2 = bf16[32,16,1536]{2,1,0:T(8,128)(2,1)} async-done(((bf16[32,16,1536]{2,1,0:T(8,128)(2,1)}), bf16[32,16,1536]{2,1,0:T(8,128)(2,1)}, u32[]{:S(2)}, u32[]{:S(2)}) %all-to-all-start.2) | async-done | bytes 1572896 | tf_op jit(solution)/shard_map/all_to_all | solution.py:189
  147.8 3.8 %fusion.3 = f32[4,512,256]{1,2,0:T(8,128)S(1)} fusion(bf16[512,1536,1]{1,0,2:T(8,128)(2,1)} %bitcast.24, bf16[2,1536,384]{1,2,0:T(8,128)(2,1)S(1)} %copy.102, bf16[2,1536,384]{1,2,0:T(8,128)(2,1)} %copy-done.4), kind=kOutput, calls=%fused_computation.7 | convolution fusion | flops 1612185600 | bytes 8388608 | tf_op jit(solution)/shard_map/rd,pdf->prf/dot_general | solution.py:191
  151.6 3.1 %convert_reduce_fusion = bf16[512,1536]{1,0:T(8,128)(2,1)} fusion(bf16[4,128,1536]{2,1,0:T(8,128)(2,1)S(1)} %copy-done.5, f32[4,512,256]{1,2,0:T(8,128)S(1)} %fusion.3), kind=kOutput, calls=%fused_computation | convolution fusion | flops 812384256 | bytes 5242880 | tf_op jit(solution)/shard_map/prf,pfd->prd/dot_general | solution.py:193
  154.7 15.0 %all-to-all-start.3 = ((bf16[32,16,1536]{2,1,0:T(8,128)(2,1)}), bf16[32,16,1536]{2,1,0:T(8,128)(2,1)S(1)}, u32[]{:S(2)}, u32[]{:S(2)}) async-start(bf16[32,16,1536]{2,1,0:T(8,128)(2,1)} %bitcast.67), calls=%async_computation.3 | async-start | bytes 3145728 | tf_op jit(solution)/shard_map/all_to_all | solution.py:197
  170.0 42.7 %all-to-all-done.3 = bf16[32,16,1536]{2,1,0:T(8,128)(2,1)S(1)} async-done(((bf16[32,16,1536]{2,1,0:T(8,128)(2,1)}), bf16[32,16,1536]{2,1,0:T(8,128)(2,1)S(1)}, u32[]{:S(2)}, u32[]{:S(2)}) %all-to-all-start.3) | async-done | bytes 1572896 | tf_op jit(solution)/shard_map/all_to_all | solution.py:197
  212.7 2.4 %add_convert_fusion = (bf16[32,1536]{1,0:T(8,128)(2,1)}, bf16[32,1536]{1,0:T(8,128)(2,1)}, bf16[32,1536]{1,0:T(8,128)(2,1)}) fusion(f32[32,1536]{1,0:T(8,128)S(1)} %copy-done.3, bf16[128,1536]{1,0:T(8,128)(2,1)} %param.12, s32[]{:T(128)S(6)} %select_n.18, f32[32,512]{1,0:T(8,128)S(1)} %select_reduce_fusion, bf16[512,1536]{1,0:T(8,128)(2,1)S(1)} %bitcast.64), kind=kOutput, calls=%fused_computation.30 | convolution fusion | flops 302383104 | bytes 2228228 | tf_op jit(solution)/shard_map/dot_general | solution.py:201
  (61 shorter events, 6.7 us)
Async XLA Ops:
  7.2 69.0 %copy-start = (bf16[384,1536]{1,0:T(8,128)(2,1)S(1)}, bf16[384,1536]{1,0:T(8,128)(2,1)}, u32[]{:S(2)}) copy-start(bf16[384,1536]{1,0:T(8,128)(2,1)} %param.16) | copy-start | bytes 3538948
  7.2 18.5 %copy-start.6 = (bf16[1,128,1536]{2,1,0:T(8,128)(2,1)S(1)}, bf16[1,128,1536]{2,1,0:T(8,128)(2,1)}, u32[]{:S(2)}) copy-start(bf16[1,128,1536]{2,1,0:T(8,128)(2,1)} %param.23) | copy-start | bytes 1179652
  9.1 45.7 %all-to-all-start = ((bf16[64,32,256]{2,1,0:T(8,128)(2,1)}), bf16[64,32,256]{2,1,0:T(8,128)(2,1)S(1)}, u32[]{:S(2)}, u32[]{:S(2)}) async-start(bf16[64,32,256]{2,1,0:T(8,128)(2,1)} %broadcast_in_dim.42), calls=%async_computation | async-start | bytes 2097152 | tf_op jit(solution)/shard_map/all_to_all | solution.py:138
  25.6 3.0 %copy-start.10 = (s32[1,128]{1,0:T(1,128)S(1)}, s32[1,128]{1,0:T(1,128)}, u32[]{:S(2)}) copy-start(s32[1,128]{1,0:T(1,128)} %param.19) | copy-start | bytes 1540
  25.6 3.1 %copy-start.1 = (bf16[128,1536]{1,0:T(8,128)(2,1)S(1)}, bf16[128,1536]{1,0:T(8,128)(2,1)}, u32[]{:S(2)}) copy-start(bf16[128,1536]{1,0:T(8,128)(2,1)} %param.12) | copy-start | bytes 1179652
  25.6 77.8 %all-gather.2.cloned.1.call-start = ((), (), s32[]{:S(2)}) async-start(), calls=%async_computation.4 | async-start | bytes 3538944 | tf_op jit(solution)/shard_map/all_gather | solution.py:86
  26.2 2.8 %copy-start.7 = (bf16[1536,128]{1,0:T(8,128)(2,1)S(1)}, bf16[1536,128]{1,0:T(8,128)(2,1)}, u32[]{:S(2)}) copy-start(bf16[1536,128]{1,0:T(8,128)(2,1)} %param.14) | copy-start | bytes 1179652
  54.8 9.5 %collective-permute-start = (bf16[2048,256]{1,0:T(8,128)(2,1)S(1)}, bf16[2048,256]{1,0:T(8,128)(2,1)}, u32[]{:S(2)}, u32[]{:S(2)}) collective-permute-start(bf16[2048,256]{1,0:T(8,128)(2,1)S(1)} %bitcast.65), channel_id=1, source_target_pairs={{0,4},{4,0},{1,5},{5,1},{2,6},{6,2},{3,7},{7,3},{8,12},{12,8},{9,1... | collective-permute-start | bytes 3145736 | tf_op jit(solution)/shard_map/ppermute | solution.py:141
  75.9 5.8 %copy-start.8 = (s32[32,8]{0,1:T(8,128)S(1)}, s32[32,8]{0,1:T(8,128)}, u32[]{:S(2)}) copy-start(s32[32,8]{0,1:T(8,128)} %param.20) | copy-start | bytes 3076
  77.4 17.2 %all-to-all-start.1 = ((f32[4,32,1536]{2,1,0:T(8,128)}), f32[4,32,1536]{2,1,0:T(8,128)S(1)}, u32[]{:S(2)}, u32[]{:S(2)}) async-start(f32[4,32,1536]{2,1,0:T(8,128)} %fusion.8), calls=%async_computation.1 | async-start | bytes 1572864 | tf_op jit(solution)/shard_map/all_to_all | solution.py:164
  94.7 2.0 copy-start.2
  96.7 51.0 %all-to-all-start.2 = ((bf16[32,16,1536]{2,1,0:T(8,128)(2,1)}), bf16[32,16,1536]{2,1,0:T(8,128)(2,1)}, u32[]{:S(2)}, u32[]{:S(2)}) async-start(bf16[32,16,1536]{2,1,0:T(8,128)(2,1)} %bitcast.22), calls=%async_computation.2 | async-start | bytes 3145728 | tf_op jit(solution)/shard_map/all_to_all | solution.py:189
  106.3 6.4 %collective-permute-start.1 = (bf16[2,1536,384]{1,2,0:T(8,128)(2,1)S(1)}, bf16[2,1536,384]{1,2,0:T(8,128)(2,1)S(1)}, u32[]{:S(2)}, u32[]{:S(2)}) collective-permute-start(bf16[2,1536,384]{1,2,0:T(8,128)(2,1)S(1)} %copy.102), channel_id=1, source_target_pairs={{0,4},{4,0},{1,5},{5,1},{2,6},{6,2},{3,7},{7,3},{8,12},{12,8},{9,1... | collective-permute-start | bytes 7077896 | tf_op jit(solution)/shard_map/ppermute | solution.py:87
  112.7 1.4 copy-start.4
  147.8 3.8 %copy-start.5 = (bf16[4,128,1536]{2,1,0:T(8,128)(2,1)S(1)}, bf16[4,128,1536]{2,1,0:T(8,128)(2,1)}, u32[]{:S(2)}) copy-start(bf16[4,128,1536]{2,1,0:T(8,128)(2,1)} %reshape.201) | copy-start | bytes 4718596
  154.7 15.0 %copy-start.9 = (f32[32,8]{0,1:T(8,128)S(1)}, f32[32,8]{0,1:T(8,128)}, u32[]{:S(2)}) copy-start(f32[32,8]{0,1:T(8,128)} %param.21) | copy-start | bytes 3076
  154.7 58.0 %copy-start.3 = (f32[32,1536]{1,0:T(8,128)S(1)}, f32[32,1536]{1,0:T(8,128)}, u32[]{:S(2)}) copy-start(f32[32,1536]{1,0:T(8,128)} %copy-done.2) | copy-start | bytes 589828
  154.7 58.0 %all-to-all-start.3 = ((bf16[32,16,1536]{2,1,0:T(8,128)(2,1)}), bf16[32,16,1536]{2,1,0:T(8,128)(2,1)S(1)}, u32[]{:S(2)}, u32[]{:S(2)}) async-start(bf16[32,16,1536]{2,1,0:T(8,128)(2,1)} %bitcast.67), calls=%async_computation.3 | async-start | bytes 3145728 | tf_op jit(solution)/shard_map/all_to_all | solution.py:197
Sparse Core Ops, SparseCore 0:
  28.7 46.5 all-gather.1

commit v10 on v7

--- a/solution.py
+++ b/solution.py
@@ -39,30 +39,42 @@
     )
 
 
-def prefix_attention(queries, keys_values, top_old, denom_old, numer_old, head_size):
+def prefix_attention(queries, kv_halves, top_old, denom_old, numer_old, head_size):
     kv_local = queries.shape[0]
-    value_base = keys_values.shape[1] // 2
-
-    def kernel(q_ref, kv_ref, top_ref, den_ref, num_ref, out_ref):
+    value_base = kv_halves[0].shape[1] // 2
+    halves = len(kv_halves)
+
+    def kernel(q_ref, *refs):
+        kv_refs = refs[:halves]
+        top_ref, den_ref, num_ref, out_ref = refs[halves:]
         for head in range(kv_local):
-            keys = kv_ref[:, head * head_size : (head + 1) * head_size]
-            values = kv_ref[:, value_base + head * head_size : value_base + (head + 1) * head_size]
-            scores = lax.dot_general(
-                q_ref[head], keys, (((1,), (1,)), ((), ())), preferred_element_type=jnp.float32
-            ) * (1.0 / head_size)
+            key_cols = slice(head * head_size, (head + 1) * head_size)
+            value_cols = slice(value_base + head * head_size, value_base + (head + 1) * head_size)
+            scores = [
+                lax.dot_general(
+                    q_ref[head], kv_ref[:, key_cols], (((1,), (1,)), ((), ())),
+                    preferred_element_type=jnp.float32,
+                ) * (1.0 / head_size)
+                for kv_ref in kv_refs
+            ]
             top_prev = top_ref[head]
-            top_new = jnp.maximum(top_prev, jnp.max(scores, axis=1, keepdims=True))
+            top_new = top_prev
+            for part in scores:
+                top_new = jnp.maximum(top_new, jnp.max(part, axis=1, keepdims=True))
             shrink = jnp.exp(top_prev - top_new)
-            weights = jnp.exp(scores - top_new)
-            denom = den_ref[head] * shrink + jnp.sum(weights, axis=1, keepdims=True)
-            numer = num_ref[head] * shrink + jnp.dot(
-                weights.astype(jnp.bfloat16), values, preferred_element_type=jnp.float32
-            )
+            denom = den_ref[head] * shrink
+            numer = num_ref[head] * shrink
+            for part, kv_ref in zip(scores, kv_refs):
+                weights = jnp.exp(part - top_new)
+                denom = denom + jnp.sum(weights, axis=1, keepdims=True)
+                numer = numer + jnp.dot(
+                    weights.astype(jnp.bfloat16), kv_ref[:, value_cols], preferred_element_type=jnp.float32
+                )
             out_ref[head] = (numer / denom).astype(jnp.bfloat16)
 
     return pl.pallas_call(
         kernel, out_shape=jax.ShapeDtypeStruct(queries.shape, jnp.bfloat16)
-    )(queries, keys_values, top_old, denom_old, numer_old)
+    )(queries, *kv_halves, top_old, denom_old, numer_old)
 
 
 def body(
@@ -138,7 +150,6 @@
         jnp.broadcast_to(prefix_both[None], (chip_total,) + prefix_both.shape), CHIP_AXES, 0, 0, tiled=True
     ).reshape(-1, prefix_both.shape[1])
     other_core = lax.ppermute(same_core, CORE_AXIS, [(0, 1), (1, 0)])
-    whole_both = jnp.concatenate([same_core, other_core], axis=0)
     top_old, denom_old, numer_old = running
     rows_q = rows_dev * group_width
 
@@ -147,7 +158,7 @@
 
     attended = prefix_attention(
         heads_first(query_rows_all),
-        whole_both,
+        (same_core, other_core),
         heads_first(top_old[..., None]),
         heads_first(denom_old[..., None]),
         heads_first(numer_old),

time: 217 us -> 221 us (1.018)
  the two profiles are of different devices: /device:TPU:80 before, /device:TPU:6 now
where the time goes in v10:
time: 221 us; the launch traced here: 218 us
  waiting for transfers between devices  128 us (58%)
  starting transfers between devices  34 us (15%)
  matrix products  14.6 us (7%)
  between operations  14.4 us (7%)
  local copies, waits for them, and re-layouts  12.8 us (6%)
  Pallas kernels  9.07 us (4%)
  other arithmetic  5.33 us (2%)
    all_to_all x1, waiting for transfers between devices, body(): lax.all_to_all(outgoing, EXPERT_AXES, split_axis=0, concat_axis=0, tiled=...  49 us
    all_to_all x1, waiting for transfers between devices, body(): lax.all_to_all(part_total.reshape(experts, capacity, column_list), EXPERT...  44.1 us
    all_to_all x1, waiting for transfers between devices, body(): lax.all_to_all(jnp.broadcast_to(prefix_both[None], (chip_total,) + prefix...  24.9 us
    all_to_all x1, starting transfers between devices, body(): lax.all_to_all(jnp.broadcast_to(prefix_both[None], (chip_total,) + prefix...  16.6 us
    all_to_all x1, waiting for transfers between devices, body(): lax.all_to_all(attn_part.reshape(tp_count, moe_rows, column_list), 'tp',...  9.55 us
    pallas_call x1, Pallas kernels, prefix_attention(): pl.pallas_call(kernel, out_shape=jax.ShapeDtypeStruct(queries.shape, jnp....  9.07 us
    all_to_all x1, starting transfers between devices, body(): lax.all_to_all(outgoing, EXPERT_AXES, split_axis=0, concat_axis=0, tiled=...  5.98 us
    all_to_all x1, starting transfers between devices, body(): lax.all_to_all(attn_part.reshape(tp_count, moe_rows, column_list), 'tp',...  4.77 us
  transfers between devices with their start and end apart: 6, of which 4 were waited for; matrix products, arithmetic and copies ran while one was open for 9% of the time, Pallas kernels for 4%

profile of v10, /device:TPU:6, one launch (start us, length us, event | category | flops | bytes accessed | tf_op | source)
XLA Modules:
  0.0 217.7 jit_solution(13999174122678020056)
XLA Ops:
  7.2 0.8 pad_maximum_fusion.3
  8.0 1.1 broadcast_in_dim.42
  9.1 16.6 %all-to-all-start = ((bf16[64,32,256]{2,1,0:T(8,128)(2,1)}), bf16[64,32,256]{2,1,0:T(8,128)(2,1)S(1)}, u32[]{:S(2)}, u32[]{:S(2)}) async-start(bf16[64,32,256]{2,1,0:T(8,128)(2,1)} %broadcast_in_dim.42), calls=%async_computation | async-start | bytes 2097152 | tf_op jit(solution)/shard_map/all_to_all | solution.py:149
  25.8 0.5 reshape.198
  26.3 2.4 %pad_maximum_fusion = bf16[1,1536,384]{2,1,0:T(8,128)(2,1)} fusion(bf16[1,1536,128]{2,1,0:T(8,128)(2,1)S(1)} %reshape.198, bf16[1,1536,256]{2,1,0:T(8,128)(2,1)} %param.22), kind=kLoop, calls=%fused_computation.8 | loop fusion | flops 2359296 | bytes 2359296 | tf_op jit(solution)/shard_map/concatenate | solution.py:95
  29.6 0.4 copy-done.4
  30.0 0.6 fusion.32
  30.6 24.9 %all-to-all-done = bf16[64,32,256]{2,1,0:T(8,128)(2,1)S(1)} async-done(((bf16[64,32,256]{2,1,0:T(8,128)(2,1)}), bf16[64,32,256]{2,1,0:T(8,128)(2,1)S(1)}, u32[]{:S(2)}, u32[]{:S(2)}) %all-to-all-start) | async-done | bytes 1048608 | tf_op jit(solution)/shard_map/all_to_all | solution.py:149
  55.5 1.9 collective-permute-start
  57.8 0.4 convolution_convert_fusion.1
  58.1 0.9 fusion.17
  59.0 1.2 copy.86
  60.2 0.8 copy.90.refs_4_
  61.3 0.9 reshape.209.refs_3_
  62.3 0.9 reshape.208.refs_2_
  63.4 0.7 copy.87.q_ref
  64.1 9.1 %shard_map.139 = bf16[2,384,64]{2,1,0:T(8,128)(2,1)} custom-call(bf16[2,384,64]{2,1,0:T(8,128)(2,1)} %copy.87.q_ref, bf16[2048,256]{1,0:T(8,128)(2,1)} %bitcast.66, bf16[2048,256]{1,0:T(8,128)(2,1)} %collective-permute-done.refs_1_, f32[2,384,1]{2,1,0:T(8,128)} %reshape.208.refs_2_, f32[2,384,1]{2,1,0:T(8,128)} %reshape.209.refs_3_, f32[2,384,64]{2,1,0:T(8,128)} %copy.90.refs_4_), custom_call_target="tpu_custom_call" | custom-call | tf_op jit(solution)/shard_map/pallas_call | solution.py:75
  73.2 1.1 copy.91
  74.7 1.3 fusion.7
  75.9 4.8 %all-to-all-start.1 = ((f32[4,32,1536]{2,1,0:T(8,128)}), f32[4,32,1536]{2,1,0:T(8,128)S(1)}, u32[]{:S(2)}, u32[]{:S(2)}) async-start(f32[4,32,1536]{2,1,0:T(8,128)} %fusion.7), calls=%async_computation.1 | async-start | bytes 1572864 | tf_op jit(solution)/shard_map/all_to_all | solution.py:174
  81.0 0.7 select_reduce_fusion.1
  82.0 9.5 %all-to-all-done.1 = f32[4,32,1536]{2,1,0:T(8,128)S(1)} async-done(((f32[4,32,1536]{2,1,0:T(8,128)}), f32[4,32,1536]{2,1,0:T(8,128)S(1)}, u32[]{:S(2)}, u32[]{:S(2)}) %all-to-all-start.1) | async-done | bytes 786464 | tf_op jit(solution)/shard_map/all_to_all | solution.py:174
  91.8 1.9 convolution_convert_fusion
  93.7 6.0 %all-to-all-start.2 = ((bf16[32,16,1536]{2,1,0:T(8,128)(2,1)}), bf16[32,16,1536]{2,1,0:T(8,128)(2,1)}, u32[]{:S(2)}, u32[]{:S(2)}) async-start(bf16[32,16,1536]{2,1,0:T(8,128)(2,1)} %bitcast.22), calls=%async_computation.2 | async-start | bytes 3145728 | tf_op jit(solution)/shard_map/all_to_all | solution.py:199
  99.7 1.4 slice-done
  101.1 2.6 %reshape.201 = bf16[4,128,1536]{2,1,0:T(8,128)(2,1)} reshape(bf16[4,1536,128]{2,1,0:T(8,128)(2,1)S(1)} %slice-done) | data formatting | bytes 3145728 | tf_op jit(solution)/shard_map/reshape | solution.py:100
  103.7 49.0 %all-to-all-done.2 = bf16[32,16,1536]{2,1,0:T(8,128)(2,1)} async-done(((bf16[32,16,1536]{2,1,0:T(8,128)(2,1)}), bf16[32,16,1536]{2,1,0:T(8,128)(2,1)}, u32[]{:S(2)}, u32[]{:S(2)}) %all-to-all-start.2) | async-done | bytes 1572896 | tf_op jit(solution)/shard_map/all_to_all | solution.py:199
  152.7 4.3 %fusion.2 = f32[4,512,256]{1,2,0:T(8,128)S(1)} fusion(bf16[512,1536,1]{1,0,2:T(8,128)(2,1)} %bitcast.24, bf16[4,1536,384]{2,1,0:T(8,128)(2,1)} %all-gather.2.cloned.1.call-done), kind=kOutput, calls=%fused_computation.4 | convolution fusion | flops 1610612736 | bytes 6815744 | tf_op jit(solution)/shard_map/rd,pdf->prf/dot_general | solution.py:201
  157.1 3.1 %convert_reduce_fusion = bf16[512,1536]{1,0:T(8,128)(2,1)} fusion(bf16[4,128,1536]{2,1,0:T(8,128)(2,1)S(1)} %copy-done.3, f32[4,512,256]{1,2,0:T(8,128)S(1)} %fusion.2), kind=kOutput, calls=%fused_computation | convolution fusion | flops 812384256 | bytes 5242880 | tf_op jit(solution)/shard_map/prf,pfd->prd/dot_general | solution.py:203
  160.2 4.7 %all-to-all-start.3 = ((bf16[32,16,1536]{2,1,0:T(8,128)(2,1)}), bf16[32,16,1536]{2,1,0:T(8,128)(2,1)S(1)}, u32[]{:S(2)}, u32[]{:S(2)}) async-start(bf16[32,16,1536]{2,1,0:T(8,128)(2,1)} %bitcast.67), calls=%async_computation.3 | async-start | bytes 3145728 | tf_op jit(solution)/shard_map/all_to_all | solution.py:207
  165.2 44.1 %all-to-all-done.3 = bf16[32,16,1536]{2,1,0:T(8,128)(2,1)S(1)} async-done(((bf16[32,16,1536]{2,1,0:T(8,128)(2,1)}), bf16[32,16,1536]{2,1,0:T(8,128)(2,1)S(1)}, u32[]{:S(2)}, u32[]{:S(2)}) %all-to-all-start.3) | async-done | bytes 1572896 | tf_op jit(solution)/shard_map/all_to_all | solution.py:207
  209.3 1.5 add_convert_fusion
  (57 shorter events, 3.3 us)
Async XLA Ops:
  7.2 67.5 %copy-start = (bf16[384,1536]{1,0:T(8,128)(2,1)S(1)}, bf16[384,1536]{1,0:T(8,128)(2,1)}, u32[]{:S(2)}) copy-start(bf16[384,1536]{1,0:T(8,128)(2,1)} %param.16) | copy-start | bytes 3538948
  8.0 17.8 %copy-start.5 = (bf16[1,128,1536]{2,1,0:T(8,128)(2,1)S(1)}, bf16[1,128,1536]{2,1,0:T(8,128)(2,1)}, u32[]{:S(2)}) copy-start(bf16[1,128,1536]{2,1,0:T(8,128)(2,1)} %param.23) | copy-start | bytes 1179652
  9.1 46.3 %all-to-all-start = ((bf16[64,32,256]{2,1,0:T(8,128)(2,1)}), bf16[64,32,256]{2,1,0:T(8,128)(2,1)S(1)}, u32[]{:S(2)}, u32[]{:S(2)}) async-start(bf16[64,32,256]{2,1,0:T(8,128)(2,1)} %broadcast_in_dim.42), calls=%async_computation | async-start | bytes 2097152 | tf_op jit(solution)/shard_map/all_to_all | solution.py:149
  25.7 73.9 %all-gather.2.cloned.1.call-start = ((), (), s32[]{:S(2)}) async-start(), calls=%async_computation.4 | async-start | bytes 5898240 | tf_op jit(solution)/shard_map/all_gather | solution.py:98
  26.3 2.4 %copy-start.10 = (s32[1,128]{1,0:T(1,128)S(1)}, s32[1,128]{1,0:T(1,128)}, u32[]{:S(2)}) copy-start(s32[1,128]{1,0:T(1,128)} %param.19) | copy-start | bytes 1540
  26.3 2.5 %copy-start.1 = (bf16[128,1536]{1,0:T(8,128)(2,1)S(1)}, bf16[128,1536]{1,0:T(8,128)(2,1)}, u32[]{:S(2)}) copy-start(bf16[128,1536]{1,0:T(8,128)(2,1)} %param.12) | copy-start | bytes 1179652
  26.3 2.9 %copy-start.6 = (bf16[1536,128]{1,0:T(8,128)(2,1)S(1)}, bf16[1536,128]{1,0:T(8,128)(2,1)}, u32[]{:S(2)}) copy-start(bf16[1536,128]{1,0:T(8,128)(2,1)} %param.14) | copy-start | bytes 1179652
  28.7 1.3 copy-start.4
  29.5 28.2 %copy-start.7 = (bf16[1536,128]{1,0:T(8,128)(2,1)S(1)}, bf16[1536,128]{1,0:T(8,128)(2,1)}, u32[]{:S(2)}) copy-start(bf16[1536,128]{1,0:T(8,128)(2,1)} %param.15) | copy-start | bytes 1179652
  55.5 5.5 %copy-start.2 = (bf16[64,32,256]{2,1,0:T(8,128)(2,1)}, bf16[64,32,256]{2,1,0:T(8,128)(2,1)S(1)}, u32[]{:S(2)}) copy-start(bf16[64,32,256]{2,1,0:T(8,128)(2,1)S(1)} %all-to-all-done) | copy-start | bytes 3145732
  55.5 8.6 %collective-permute-start = (bf16[2048,256]{1,0:T(8,128)(2,1)S(1)}, bf16[2048,256]{1,0:T(8,128)(2,1)}, u32[]{:S(2)}, u32[]{:S(2)}) collective-permute-start(bf16[2048,256]{1,0:T(8,128)(2,1)S(1)} %bitcast.65), channel_id=1, source_target_pairs={{0,4},{4,0},{1,5},{5,1},{2,6},{6,2},{3,7},{7,3},{8,12},{12,8},{9,1... | collective-permute-start | bytes 3145736 | tf_op jit(solution)/shard_map/ppermute | solution.py:152
  74.6 6.1 %copy-start.8 = (s32[32,8]{0,1:T(8,128)S(1)}, s32[32,8]{0,1:T(8,128)}, u32[]{:S(2)}) copy-start(s32[32,8]{0,1:T(8,128)} %param.20) | copy-start | bytes 3076
  75.9 15.7 %all-to-all-start.1 = ((f32[4,32,1536]{2,1,0:T(8,128)}), f32[4,32,1536]{2,1,0:T(8,128)S(1)}, u32[]{:S(2)}, u32[]{:S(2)}) async-start(f32[4,32,1536]{2,1,0:T(8,128)} %fusion.7), calls=%async_computation.1 | async-start | bytes 1572864 | tf_op jit(solution)/shard_map/all_to_all | solution.py:174
  93.7 59.1 %all-to-all-start.2 = ((bf16[32,16,1536]{2,1,0:T(8,128)(2,1)}), bf16[32,16,1536]{2,1,0:T(8,128)(2,1)}, u32[]{:S(2)}, u32[]{:S(2)}) async-start(bf16[32,16,1536]{2,1,0:T(8,128)(2,1)} %bitcast.22), calls=%async_computation.2 | async-start | bytes 3145728 | tf_op jit(solution)/shard_map/all_to_all | solution.py:199
  99.7 1.4 slice-start
  152.7 4.3 %copy-start.3 = (bf16[4,128,1536]{2,1,0:T(8,128)(2,1)S(1)}, bf16[4,128,1536]{2,1,0:T(8,128)(2,1)}, u32[]{:S(2)}) copy-start(bf16[4,128,1536]{2,1,0:T(8,128)(2,1)} %reshape.201) | copy-start | bytes 4718596
  160.2 4.7 %copy-start.9 = (f32[32,8]{0,1:T(8,128)S(1)}, f32[32,8]{0,1:T(8,128)}, u32[]{:S(2)}) copy-start(f32[32,8]{0,1:T(8,128)} %param.21) | copy-start | bytes 3076
  160.2 49.1 %all-to-all-start.3 = ((bf16[32,16,1536]{2,1,0:T(8,128)(2,1)}), bf16[32,16,1536]{2,1,0:T(8,128)(2,1)S(1)}, u32[]{:S(2)}, u32[]{:S(2)}) async-start(bf16[32,16,1536]{2,1,0:T(8,128)(2,1)} %bitcast.67), calls=%async_computation.3 | async-start | bytes 3145728 | tf_op jit(solution)/shard_map/all_to_all | solution.py:207
Sparse Core Ops, SparseCore 0:
  28.8 58.7 all-gather.1

commit v11 on v7

--- a/solution.py
+++ b/solution.py
@@ -161,9 +161,9 @@
     attn_part = jnp.dot(attended, w_out, preferred_element_type=jnp.float32)
     tp_count = lax.axis_size("tp")
     exchanged = lax.all_to_all(
-        attn_part.reshape(tp_count, moe_rows, column_list), "tp", 0, 0, tiled=True
-    )
-    attn_sum = jnp.sum(exchanged, axis=0)
+        attn_part.astype(jnp.bfloat16).reshape(tp_count, moe_rows, column_list), "tp", 0, 0, tiled=True
+    )
+    attn_sum = jnp.sum(exchanged.astype(jnp.float32), axis=0)
     residual = (
         lax.dynamic_slice_in_dim(hidden_in, row_start, moe_rows, 0).astype(jnp.float32)
         + RESIDUAL * attn_sum

time: 217 us -> 214 us (0.986)
  the two profiles are of different devices: /device:TPU:80 before, /device:TPU:6 now
where the time goes in v11:
time: 214 us; the launch traced here: 210 us
  waiting for transfers between devices  118 us (55%)
  starting transfers between devices  34 us (16%)
  matrix products  15.2 us (7%)
  between operations  14.3 us (7%)
  local copies, waits for them, and re-layouts  12.2 us (6%)
  other arithmetic  8.65 us (4%)
  Pallas kernels  7.83 us (4%)
    all_to_all x1, waiting for transfers between devices, body(): lax.all_to_all(outgoing, EXPERT_AXES, split_axis=0, concat_axis=0, tiled=...  48.9 us
    all_to_all x1, waiting for transfers between devices, body(): lax.all_to_all(part_total.reshape(experts, capacity, column_list), EXPERT...  38.3 us
    all_to_all x1, waiting for transfers between devices, body(): lax.all_to_all(jnp.broadcast_to(prefix_both[None], (chip_total,) + prefix...  24.6 us
    all_to_all x1, starting transfers between devices, body(): lax.all_to_all(jnp.broadcast_to(prefix_both[None], (chip_total,) + prefix...  16.6 us
    pallas_call x1, Pallas kernels, prefix_attention(): pl.pallas_call(kernel, out_shape=jax.ShapeDtypeStruct(queries.shape, jnp....  7.83 us
    all_to_all x1, waiting for transfers between devices, body(): lax.all_to_all(attn_part.astype(jnp.bfloat16).reshape(tp_count, moe_rows,...  6.39 us
    all_to_all x1, starting transfers between devices, body(): lax.all_to_all(outgoing, EXPERT_AXES, split_axis=0, concat_axis=0, tiled=...  5.97 us
    all_to_all x1, starting transfers between devices, body(): lax.all_to_all(attn_part.astype(jnp.bfloat16).reshape(tp_count, moe_rows,...  4.76 us
  transfers between devices with their start and end apart: 6, of which 4 were waited for; matrix products, arithmetic and copies ran while one was open for 11% of the time, Pallas kernels for 4%

profile of v11, /device:TPU:6, one launch (start us, length us, event | category | flops | bytes accessed | tf_op | source)
XLA Modules:
  0.0 210.4 jit_solution(30305449458433198)
XLA Ops:
  7.2 0.8 pad_maximum_fusion.4
  8.0 1.1 broadcast_in_dim.42
  9.1 16.6 %all-to-all-start = ((bf16[64,32,256]{2,1,0:T(8,128)(2,1)}), bf16[64,32,256]{2,1,0:T(8,128)(2,1)S(1)}, u32[]{:S(2)}, u32[]{:S(2)}) async-start(bf16[64,32,256]{2,1,0:T(8,128)(2,1)} %broadcast_in_dim.42), calls=%async_computation | async-start | bytes 2097152 | tf_op jit(solution)/shard_map/all_to_all | solution.py:137
  26.3 2.3 %pad_maximum_fusion.1 = bf16[1,1536,384]{2,1,0:T(8,128)(2,1)} fusion(bf16[1,1536,128]{2,1,0:T(8,128)(2,1)S(1)} %reshape.202, bf16[1,1536,256]{2,1,0:T(8,128)(2,1)} %param.22), kind=kLoop, calls=%fused_computation.10 | loop fusion | flops 2359296 | bytes 2359296 | tf_op jit(solution)/shard_map/concatenate | solution.py:83
  29.6 0.6 subtract_convert_fusion.1
  30.2 0.6 fusion.30
  30.9 24.6 %all-to-all-done = bf16[64,32,256]{2,1,0:T(8,128)(2,1)S(1)} async-done(((bf16[64,32,256]{2,1,0:T(8,128)(2,1)}), bf16[64,32,256]{2,1,0:T(8,128)(2,1)S(1)}, u32[]{:S(2)}, u32[]{:S(2)}) %all-to-all-start) | async-done | bytes 1048608 | tf_op jit(solution)/shard_map/all_to_all | solution.py:137
  55.5 1.9 collective-permute-start
  57.4 1.0 fusion.32
  58.8 0.9 fusion.15
  59.6 1.2 copy.85
  60.9 0.8 copy.89.num_ref
  61.9 0.9 reshape.212.den_ref
  62.9 0.9 reshape.211.top_ref
  64.0 0.7 copy.86.q_ref
  65.0 0.7 select_reduce_fusion.1
  65.7 2.8 %pad_maximum_fusion.kv_ref = bf16[4096,256]{1,0:T(8,128)(2,1)} fusion(bf16[2048,256]{1,0:T(8,128)(2,1)} %collective-permute-done, bf16[2048,256]{1,0:T(8,128)(2,1)S(1)} %bitcast.66), kind=kLoop, calls=%fused_computation.5 | loop fusion | flops 4194304 | bytes 4194304 | tf_op jit(solution)/shard_map/concatenate | solution.py:141
  68.5 7.8 %shard_map.139 = bf16[2,384,64]{2,1,0:T(8,128)(2,1)} custom-call(bf16[2,384,64]{2,1,0:T(8,128)(2,1)} %copy.86.q_ref, bf16[4096,256]{1,0:T(8,128)(2,1)} %pad_maximum_fusion.kv_ref, f32[2,384,1]{2,1,0:T(8,128)} %reshape.211.top_ref, f32[2,384,1]{2,1,0:T(8,128)} %reshape.212.den_ref, f32[2,384,64]{2,1,0:T(8,128)} %copy.89.num_ref), custom_call_target="tpu_custom_call" | custom-call | tf_op jit(solution)/shard_map/pallas_call | solution.py:63
  76.3 1.1 copy.90
  77.6 1.2 convolution_convert_fusion.1
  78.8 4.8 %all-to-all-start.1 = ((bf16[4,32,1536]{2,1,0:T(8,128)(2,1)}), bf16[4,32,1536]{2,1,0:T(8,128)(2,1)S(1)}, u32[]{:S(2)}, u32[]{:S(2)}) async-start(bf16[4,32,1536]{2,1,0:T(8,128)(2,1)} %bitcast.22), calls=%async_computation.1 | async-start | bytes 786432 | tf_op jit(solution)/shard_map/all_to_all | solution.py:163
  83.9 6.4 %all-to-all-done.1 = bf16[4,32,1536]{2,1,0:T(8,128)(2,1)S(1)} async-done(((bf16[4,32,1536]{2,1,0:T(8,128)(2,1)}), bf16[4,32,1536]{2,1,0:T(8,128)(2,1)S(1)}, u32[]{:S(2)}, u32[]{:S(2)}) %all-to-all-start.1) | async-done | bytes 393248 | tf_op jit(solution)/shard_map/all_to_all | solution.py:163
  90.5 1.9 convolution_convert_fusion
  92.3 6.0 %all-to-all-start.2 = ((bf16[32,16,1536]{2,1,0:T(8,128)(2,1)}), bf16[32,16,1536]{2,1,0:T(8,128)(2,1)}, u32[]{:S(2)}, u32[]{:S(2)}) async-start(bf16[32,16,1536]{2,1,0:T(8,128)(2,1)} %bitcast.23), calls=%async_computation.2 | async-start | bytes 3145728 | tf_op jit(solution)/shard_map/all_to_all | solution.py:188
  98.4 1.4 slice-done
  99.8 2.6 %reshape.205 = bf16[4,128,1536]{2,1,0:T(8,128)(2,1)} reshape(bf16[4,1536,128]{2,1,0:T(8,128)(2,1)S(1)} %slice-done) | data formatting | bytes 3145728 | tf_op jit(solution)/shard_map/reshape | solution.py:88
  102.4 48.9 %all-to-all-done.2 = bf16[32,16,1536]{2,1,0:T(8,128)(2,1)} async-done(((bf16[32,16,1536]{2,1,0:T(8,128)(2,1)}), bf16[32,16,1536]{2,1,0:T(8,128)(2,1)}, u32[]{:S(2)}, u32[]{:S(2)}) %all-to-all-start.2) | async-done | bytes 1572896 | tf_op jit(solution)/shard_map/all_to_all | solution.py:188
  151.3 4.3 %fusion.2 = f32[4,512,256]{1,2,0:T(8,128)S(1)} fusion(bf16[512,1536,1]{1,0,2:T(8,128)(2,1)} %bitcast.25, bf16[4,1536,384]{2,1,0:T(8,128)(2,1)} %all-gather.2.cloned.1.call-done), kind=kOutput, calls=%fused_computation.6 | convolution fusion | flops 1610612736 | bytes 6815744 | tf_op jit(solution)/shard_map/rd,pdf->prf/dot_general | solution.py:190
  155.6 3.1 %convert_reduce_fusion = bf16[512,1536]{1,0:T(8,128)(2,1)} fusion(bf16[4,128,1536]{2,1,0:T(8,128)(2,1)S(1)} %copy-done.2, f32[4,512,256]{1,2,0:T(8,128)S(1)} %fusion.2), kind=kOutput, calls=%fused_computation | convolution fusion | flops 812384256 | bytes 5242880 | tf_op jit(solution)/shard_map/prf,pfd->prd/dot_general | solution.py:192
  158.7 4.7 %all-to-all-start.3 = ((bf16[32,16,1536]{2,1,0:T(8,128)(2,1)}), bf16[32,16,1536]{2,1,0:T(8,128)(2,1)S(1)}, u32[]{:S(2)}, u32[]{:S(2)}) async-start(bf16[32,16,1536]{2,1,0:T(8,128)(2,1)} %bitcast.67), calls=%async_computation.3 | async-start | bytes 3145728 | tf_op jit(solution)/shard_map/all_to_all | solution.py:196
  163.7 38.3 %all-to-all-done.3 = bf16[32,16,1536]{2,1,0:T(8,128)(2,1)S(1)} async-done(((bf16[32,16,1536]{2,1,0:T(8,128)(2,1)}), bf16[32,16,1536]{2,1,0:T(8,128)(2,1)S(1)}, u32[]{:S(2)}, u32[]{:S(2)}) %all-to-all-start.3) | async-done | bytes 1572896 | tf_op jit(solution)/shard_map/all_to_all | solution.py:196
  202.0 1.5 add_convert_fusion
  (55 shorter events, 3.6 us)
Async XLA Ops:
  7.2 70.4 %copy-start = (bf16[384,1536]{1,0:T(8,128)(2,1)S(1)}, bf16[384,1536]{1,0:T(8,128)(2,1)}, u32[]{:S(2)}) copy-start(bf16[384,1536]{1,0:T(8,128)(2,1)} %param.16) | copy-start | bytes 3538948
  8.0 17.8 %copy-start.4 = (bf16[1,128,1536]{2,1,0:T(8,128)(2,1)S(1)}, bf16[1,128,1536]{2,1,0:T(8,128)(2,1)}, u32[]{:S(2)}) copy-start(bf16[1,128,1536]{2,1,0:T(8,128)(2,1)} %param.23) | copy-start | bytes 1179652
  9.1 46.3 %all-to-all-start = ((bf16[64,32,256]{2,1,0:T(8,128)(2,1)}), bf16[64,32,256]{2,1,0:T(8,128)(2,1)S(1)}, u32[]{:S(2)}, u32[]{:S(2)}) async-start(bf16[64,32,256]{2,1,0:T(8,128)(2,1)} %broadcast_in_dim.42), calls=%async_computation | async-start | bytes 2097152 | tf_op jit(solution)/shard_map/all_to_all | solution.py:137
  25.7 72.6 %all-gather.2.cloned.1.call-start = ((), (), s32[]{:S(2)}) async-start(), calls=%async_computation.4 | async-start | bytes 5898240 | tf_op jit(solution)/shard_map/all_gather | solution.py:86
  26.3 2.4 %copy-start.9 = (s32[1,128]{1,0:T(1,128)S(1)}, s32[1,128]{1,0:T(1,128)}, u32[]{:S(2)}) copy-start(s32[1,128]{1,0:T(1,128)} %param.19) | copy-start | bytes 1540
  26.3 2.5 %copy-start.1 = (bf16[128,1536]{1,0:T(8,128)(2,1)S(1)}, bf16[128,1536]{1,0:T(8,128)(2,1)}, u32[]{:S(2)}) copy-start(bf16[128,1536]{1,0:T(8,128)(2,1)} %param.12) | copy-start | bytes 1179652
  26.3 2.9 %copy-start.5 = (bf16[1536,128]{1,0:T(8,128)(2,1)S(1)}, bf16[1536,128]{1,0:T(8,128)(2,1)}, u32[]{:S(2)}) copy-start(bf16[1536,128]{1,0:T(8,128)(2,1)} %param.14) | copy-start | bytes 1179652
  28.7 1.6 copy-start.3
  29.6 28.8 %copy-start.6 = (bf16[1536,128]{1,0:T(8,128)(2,1)S(1)}, bf16[1536,128]{1,0:T(8,128)(2,1)}, u32[]{:S(2)}) copy-start(bf16[1536,128]{1,0:T(8,128)(2,1)} %param.15) | copy-start | bytes 1179652
  55.5 10.3 %collective-permute-start = (bf16[2048,256]{1,0:T(8,128)(2,1)S(1)}, bf16[2048,256]{1,0:T(8,128)(2,1)}, u32[]{:S(2)}, u32[]{:S(2)}) collective-permute-start(bf16[2048,256]{1,0:T(8,128)(2,1)S(1)} %bitcast.65), channel_id=1, source_target_pairs={{0,4},{4,0},{1,5},{5,1},{2,6},{6,2},{3,7},{7,3},{8,12},{12,8},{9,1... | collective-permute-start | bytes 3145736 | tf_op jit(solution)/shard_map/ppermute | solution.py:140
  60.8 3.9 %copy-start.7 = (s32[32,8]{0,1:T(8,128)S(1)}, s32[32,8]{0,1:T(8,128)}, u32[]{:S(2)}) copy-start(s32[32,8]{0,1:T(8,128)} %param.20) | copy-start | bytes 3076
  78.8 11.5 %all-to-all-start.1 = ((bf16[4,32,1536]{2,1,0:T(8,128)(2,1)}), bf16[4,32,1536]{2,1,0:T(8,128)(2,1)S(1)}, u32[]{:S(2)}, u32[]{:S(2)}) async-start(bf16[4,32,1536]{2,1,0:T(8,128)(2,1)} %bitcast.22), calls=%async_computation.1 | async-start | bytes 786432 | tf_op jit(solution)/shard_map/all_to_all | solution.py:163
  92.3 58.9 %all-to-all-start.2 = ((bf16[32,16,1536]{2,1,0:T(8,128)(2,1)}), bf16[32,16,1536]{2,1,0:T(8,128)(2,1)}, u32[]{:S(2)}, u32[]{:S(2)}) async-start(bf16[32,16,1536]{2,1,0:T(8,128)(2,1)} %bitcast.23), calls=%async_computation.2 | async-start | bytes 3145728 | tf_op jit(solution)/shard_map/all_to_all | solution.py:188
  98.3 1.4 slice-start
  151.3 4.3 %copy-start.2 = (bf16[4,128,1536]{2,1,0:T(8,128)(2,1)S(1)}, bf16[4,128,1536]{2,1,0:T(8,128)(2,1)}, u32[]{:S(2)}) copy-start(bf16[4,128,1536]{2,1,0:T(8,128)(2,1)} %reshape.205) | copy-start | bytes 4718596
  158.7 4.7 %copy-start.8 = (f32[32,8]{0,1:T(8,128)S(1)}, f32[32,8]{0,1:T(8,128)}, u32[]{:S(2)}) copy-start(f32[32,8]{0,1:T(8,128)} %param.21) | copy-start | bytes 3076
  158.7 43.3 %all-to-all-start.3 = ((bf16[32,16,1536]{2,1,0:T(8,128)(2,1)}), bf16[32,16,1536]{2,1,0:T(8,128)(2,1)S(1)}, u32[]{:S(2)}, u32[]{:S(2)}) async-start(bf16[32,16,1536]{2,1,0:T(8,128)(2,1)} %bitcast.67), calls=%async_computation.3 | async-start | bytes 3145728 | tf_op jit(solution)/shard_map/all_to_all | solution.py:196
Sparse Core Ops, SparseCore 0:
  28.8 58.7 all-gather.1
